TPU v7x, 32 devices: a whole 2x2x4 slice. The times are simulated.
32 devices in a mesh: groups: 2 (over y), seq: 4 (over z), heads: 2 (over x), pair: 2 (over core).
Axes of the slice: x: 2, y: 2, z: 4, core: 2. Of those that a mesh axis runs over, the one named last changes fastest.
Arguments:
- queries: bfloat16 [6656, 2048], P(('groups', 'seq'), ('heads', 'pair')), parts along dimension 0, may hold values from -25 to 25
- key_rows: bfloat16 [6656, 2048], P(('groups', 'seq'), ('heads', 'pair')), parts along dimension 0, may hold values from -9 to 9
- value_rows: bfloat16 [6656, 2048], P(('groups', 'seq'), ('heads', 'pair')), parts along dimension 0, may hold values from -6 to 6
- out_grad: bfloat16 [6656, 2048], P(('groups', 'seq'), ('heads', 'pair')), parts along dimension 0, may hold values from -96 to 96
- random_device: int32 [104, 2], P('groups'), parts along dimension 0, may hold values from 0 to 3, all different within a row; in each aligned block of 13 rows (0 to 12, 13 to 25, ...) at most 9 rows name the same one
- random_block: int32 [104, 2], P('groups'), parts along dimension 0, may hold values from 0 to 12
Outputs:
- query_gradient: bfloat16 [6656, 2048], P(('groups', 'seq'), ('heads', 'pair')), parts along dimension 0
- key_grad: bfloat16 [6656, 2048], P(('groups', 'seq'), ('heads', 'pair')), parts along dimension 0
- value_grad: bfloat16 [6656, 2048], P(('groups', 'seq'), ('heads', 'pair')), parts along dimension 0
There are 2 independent parts, one for each index of `groups`. A program takes and returns all parts, laid end to end along the dimension named above; each array names one. Nothing has to cross between parts.
Inputs may be any that keep to these rules, and one draw needn't show every extreme that they name: `random_device`: in the 13 rows of one index of seq (aligned blocks of rows) no device number appears more than 9 times, and in every draw some number appears exactly 9 times in some device's rows; the 2 entries of a row differ.
All inputs are finite; a program needn't handle non-finite values.
Results may differ from a plain program's by a relative error of at most 0.02.
Values may be sent and summed in bfloat16 or wider, within the bound.
No kernel may reach another device: no remote copies, remote signals or barrier semaphores. Data moves between devices by JAX's collectives and lax.ppermute only.
A program may use at most 128 MiB of HBM per device.

v0:
```python
import math

import jax
import jax.numpy as jnp
from jax import lax
from jax.sharding import PartitionSpec as P

DH = 128
BLOCK = 64
RAND = 2


def extended(block, sides, width):
    for axis, dim in sides:
        count = lax.axis_size(axis)
        forward = [(i, i + 1) for i in range(count - 1)]
        backward = [(target, source) for source, target in forward]
        low = lax.ppermute(
            lax.slice_in_dim(block, block.shape[dim] - width, None, axis=dim), axis, forward
        )
        high = lax.ppermute(lax.slice_in_dim(block, 0, width, axis=dim), axis, backward)
        block = jnp.concatenate([low, block, high], axis=dim)
    return block


def routing(random_device, random_block, own_index, seq_size, blocks_dev, capacity):
    entries = blocks_dev * RAND
    wanted_from = random_device.reshape(seq_size, entries)
    wanted_block = random_block.reshape(seq_size, entries)
    from_me = (wanted_from == own_index).astype(jnp.int32)
    rank_out = jnp.cumsum(from_me, axis=1) - from_me
    slot_hits = from_me[:, None, :] * (
        rank_out[:, None, :] == jnp.arange(capacity, dtype=jnp.int32)[None, :, None]
    ).astype(jnp.int32)
    block_hits = (
        wanted_block[:, :, None] == jnp.arange(blocks_dev, dtype=jnp.int32)[None, None, :]
    ).astype(jnp.float32)
    selector = jnp.einsum("sce,sej->scj", slot_hits.astype(jnp.float32), block_hits)
    selector = selector.reshape(seq_size * capacity, blocks_dev).astype(jnp.bfloat16)
    own_sources = lax.dynamic_slice_in_dim(
        random_device, own_index * blocks_dev, blocks_dev, 0
    ).reshape(entries)
    peer_hits = (own_sources[:, None] == jnp.arange(seq_size, dtype=jnp.int32)[None, :]).astype(
        jnp.int32
    )
    earlier = jnp.cumsum(peer_hits, axis=0) - peer_hits
    rank_in = jnp.sum(earlier * peer_hits, axis=1)
    slot_index = own_sources * capacity + rank_in
    return (selector, slot_index)


def far_context(arrived, slot_index, blocks_dev):
    picked = jnp.take(arrived, slot_index, axis=0)
    return picked.reshape(blocks_dev, RAND, arrived.shape[1], arrived.shape[2])


def usable_mask(own_index, seq_size, blocks_dev):
    block_ids = jnp.arange(blocks_dev, dtype=jnp.int32)[:, None]
    slot_ids = jnp.arange(3 + RAND, dtype=jnp.int32)[None, :]
    global_block = own_index * blocks_dev + block_ids
    missing = (slot_ids == 0) & (global_block == 0) | (slot_ids == 2) & (
        global_block == seq_size * blocks_dev - 1
    )
    return jnp.repeat(jnp.logical_not(missing), BLOCK, axis=1)


def slot_pieces(haloed, far_blocks, blocks_dev, start_col):
    pieces = []
    for slot in range(3):
        pieces.append(haloed[slot : slot + blocks_dev, :, start_col : start_col + DH])
    far_part = far_blocks[:, :, :, start_col : start_col + DH]
    return (pieces, far_part)


def forward_head(query_tiles, key_pieces, key_far, value_pieces, value_far, usable):
    blocks_dev = query_tiles.shape[0]
    logit_parts = [
        jnp.einsum("bje,bxe->bjx", query_tiles, piece, preferred_element_type=jnp.float32)
        for piece in key_pieces
    ]
    far_logits = jnp.einsum(
        "bje,brxe->bjrx", query_tiles, key_far, preferred_element_type=jnp.float32
    )
    logit_parts.append(far_logits.reshape(blocks_dev, BLOCK, RAND * BLOCK))
    attention_logits = jnp.concatenate(logit_parts, axis=-1) * (1.0 / math.sqrt(DH))
    attention_logits = jnp.where(usable[:, None, :], attention_logits, -jnp.inf)
    row_max = jnp.max(attention_logits, axis=-1, keepdims=True)
    exponent = jnp.exp(attention_logits - row_max)
    row_total = jnp.sum(exponent, axis=-1, keepdims=True)
    probability = exponent / row_total
    softmax_weights = probability.astype(jnp.bfloat16)
    attended = jnp.einsum(
        "bjx,bxe->bje",
        softmax_weights[:, :, :BLOCK],
        value_pieces[0],
        preferred_element_type=jnp.float32,
    )
    for slot in range(1, 3):
        attended = attended + jnp.einsum(
            "bjx,bxe->bje",
            softmax_weights[:, :, slot * BLOCK : (slot + 1) * BLOCK],
            value_pieces[slot],
            preferred_element_type=jnp.float32,
        )
    far_weights = softmax_weights[:, :, 3 * BLOCK :].reshape(blocks_dev, BLOCK, RAND, BLOCK)
    attended = attended + jnp.einsum(
        "bjrx,brxe->bje", far_weights, value_far, preferred_element_type=jnp.float32
    )
    return (probability, attended.astype(jnp.bfloat16))


def backward_head(
    query_tiles, key_pieces, key_far, value_pieces, value_far, gradient_tiles, forward_state
):
    probability, attended_output = forward_state
    blocks_dev = query_tiles.shape[0]
    logit_scale = 1.0 / math.sqrt(DH)
    softmax_weights = probability.astype(jnp.bfloat16)
    row_delta = jnp.sum(
        gradient_tiles.astype(jnp.float32) * attended_output.astype(jnp.float32),
        axis=-1,
        keepdims=True,
    )
    grad_parts = [
        jnp.einsum("bje,bxe->bjx", gradient_tiles, piece, preferred_element_type=jnp.float32)
        for piece in value_pieces
    ]
    far_grad = jnp.einsum(
        "bje,brxe->bjrx", gradient_tiles, value_far, preferred_element_type=jnp.float32
    )
    grad_parts.append(far_grad.reshape(blocks_dev, BLOCK, RAND * BLOCK))
    probability_gradient = jnp.concatenate(grad_parts, axis=-1)
    score_gradient = (probability * (probability_gradient - row_delta)).astype(jnp.bfloat16)
    query_sum = jnp.einsum(
        "bjx,bxe->bje",
        score_gradient[:, :, :BLOCK],
        key_pieces[0],
        preferred_element_type=jnp.float32,
    )
    for slot in range(1, 3):
        query_sum = query_sum + jnp.einsum(
            "bjx,bxe->bje",
            score_gradient[:, :, slot * BLOCK : (slot + 1) * BLOCK],
            key_pieces[slot],
            preferred_element_type=jnp.float32,
        )
    far_scores = score_gradient[:, :, 3 * BLOCK :].reshape(blocks_dev, BLOCK, RAND, BLOCK)
    query_sum = query_sum + jnp.einsum(
        "bjrx,brxe->bje", far_scores, key_far, preferred_element_type=jnp.float32
    )
    query_gradient = (logit_scale * query_sum).astype(jnp.bfloat16)
    key_window, value_window = ([], [])
    for slot in range(3):
        columns = slice(slot * BLOCK, (slot + 1) * BLOCK)
        key_window.append(
            logit_scale
            * jnp.einsum(
                "bjx,bje->bxe",
                score_gradient[:, :, columns],
                query_tiles,
                preferred_element_type=jnp.float32,
            )
        )
        value_window.append(
            jnp.einsum(
                "bjx,bje->bxe",
                softmax_weights[:, :, columns],
                gradient_tiles,
                preferred_element_type=jnp.float32,
            )
        )
    far_weights = softmax_weights[:, :, 3 * BLOCK :].reshape(blocks_dev, BLOCK, RAND, BLOCK)
    key_far_terms = (
        logit_scale
        * jnp.einsum("bjrx,bje->brxe", far_scores, query_tiles, preferred_element_type=jnp.float32)
    ).astype(jnp.bfloat16)
    value_far_terms = jnp.einsum(
        "bjrx,bje->brxe", far_weights, gradient_tiles, preferred_element_type=jnp.float32
    ).astype(jnp.bfloat16)
    return (query_gradient, key_window, value_window, key_far_terms, value_far_terms)


def shards(queries, key_rows, value_rows, out_grad, random_device, random_block):
    seq_size = lax.axis_size("seq")
    own_index = lax.axis_index("seq")
    tokens, row_width = queries.shape
    blocks_dev = tokens // BLOCK
    heads_dev = row_width // DH
    capacity = max(2, 3 * blocks_dev // seq_size)
    selector, slot_index = routing(
        random_device, random_block, own_index, seq_size, blocks_dev, capacity
    )
    packed = jnp.concatenate([key_rows, value_rows], axis=1).reshape(
        blocks_dev, BLOCK, 2 * row_width
    )
    flattened = packed.reshape(blocks_dev, BLOCK * 2 * row_width)
    outgoing_blocks = jnp.dot(selector, flattened, preferred_element_type=jnp.float32).astype(
        jnp.bfloat16
    )
    outgoing_blocks = outgoing_blocks.reshape(seq_size * capacity, BLOCK, 2 * row_width)
    haloed = extended(packed, (("seq", 0),), 1)
    arrived = lax.all_to_all(outgoing_blocks, "seq", split_axis=0, concat_axis=0, tiled=True)
    far_blocks = far_context(arrived, slot_index, blocks_dev)
    usable = usable_mask(own_index, seq_size, blocks_dev)
    query_tiles = queries.reshape(blocks_dev, BLOCK, row_width)
    gradient_tiles = out_grad.reshape(blocks_dev, BLOCK, row_width)
    states = []
    for head_index in range(heads_dev):
        key_pieces, key_far = slot_pieces(haloed, far_blocks, blocks_dev, head_index * DH)
        value_pieces, value_far = slot_pieces(
            haloed, far_blocks, blocks_dev, row_width + head_index * DH
        )
        query_head = query_tiles[:, :, head_index * DH : (head_index + 1) * DH]
        states.append(
            forward_head(query_head, key_pieces, key_far, value_pieces, value_far, usable)
        )
    query_parts = []
    window_lists = [[], [], []]
    value_lists = [[], [], []]
    far_keys, far_values = ([], [])
    for head_index in range(heads_dev):
        key_pieces, key_far = slot_pieces(haloed, far_blocks, blocks_dev, head_index * DH)
        value_pieces, value_far = slot_pieces(
            haloed, far_blocks, blocks_dev, row_width + head_index * DH
        )
        query_head = query_tiles[:, :, head_index * DH : (head_index + 1) * DH]
        gradient_head = gradient_tiles[:, :, head_index * DH : (head_index + 1) * DH]
        query_gradient, key_window, value_window, key_far_terms, value_far_terms = backward_head(
            query_head,
            key_pieces,
            key_far,
            value_pieces,
            value_far,
            gradient_head,
            states[head_index],
        )
        query_parts.append(query_gradient)
        for slot in range(3):
            window_lists[slot].append(key_window[slot])
            value_lists[slot].append(value_window[slot])
        far_keys.append(key_far_terms)
        far_values.append(value_far_terms)
    slot_terms = [
        jnp.concatenate(window_lists[slot] + value_lists[slot], axis=-1) for slot in range(3)
    ]
    left_terms = slot_terms[0]
    right_terms = slot_terms[2]
    far_terms = jnp.concatenate(far_keys + far_values, axis=-1).reshape(
        blocks_dev * RAND, BLOCK, 2 * row_width
    )
    edge_terms = jnp.stack([left_terms[0], right_terms[-1]])
    edge_haloed = extended(edge_terms.astype(jnp.bfloat16), (("seq", 0),), 1).astype(
        edge_terms.dtype
    )
    summed = (
        slot_terms[1]
        + jnp.concatenate([left_terms[1:], edge_haloed[3:]], axis=0)
        + jnp.concatenate([edge_haloed[:1], right_terms[:-1]], axis=0)
    )
    returning = (
        jnp.zeros((seq_size * capacity, BLOCK, 2 * row_width), jnp.bfloat16)
        .at[slot_index]
        .set(far_terms)
    )
    returned = lax.all_to_all(returning, "seq", split_axis=0, concat_axis=0, tiled=True)
    gathered_terms = jnp.dot(
        selector.T,
        returned.reshape(seq_size * capacity, BLOCK * 2 * row_width),
        preferred_element_type=jnp.float32,
    )
    summed = summed + gathered_terms.reshape(blocks_dev, BLOCK, 2 * row_width)
    summed = summed.reshape(tokens, 2 * row_width)
    query_out = jnp.concatenate(query_parts, axis=-1).reshape(tokens, row_width)
    return (
        query_out,
        summed[:, :row_width].astype(jnp.bfloat16),
        summed[:, row_width:].astype(jnp.bfloat16),
    )


def solution(mesh):
    return jax.shard_map(
        shards,
        mesh=mesh,
        in_specs=(
            P(("groups", "seq"), ("heads", "pair")),
            P(("groups", "seq"), ("heads", "pair")),
            P(("groups", "seq"), ("heads", "pair")),
            P(("groups", "seq"), ("heads", "pair")),
            P("groups", None),
            P("groups", None),
        ),
        out_specs=(
            P(("groups", "seq"), ("heads", "pair")),
            P(("groups", "seq"), ("heads", "pair")),
            P(("groups", "seq"), ("heads", "pair")),
        ),
        check_vma=False,
    )
```

profile of v0, /device:TPU:22, one launch (start us, length us, event | category | flops | bytes accessed | tf_op | source)
XLA Modules:
  0.0 421.3 jit_solution(7583532140127653463)
XLA Ops:
  4.2 2.6 reshape_reshape.3
  6.8 3.1 convolution_convert_fusion
  9.9 3.0 copy.229
  12.9 2.8 slice.488
  15.7 5.4 %all-to-all-start = ((bf16[36,64,1024]{2,1,0:T(8,128)(2,1)}), bf16[36,64,1024]{2,1,0:T(8,128)(2,1)}, u32[]{:S(2)}, u32[]{:S(2)}) async-start(bf16[36,64,1024]{2,1,0:T(8,128)(2,1)} %slice.488), calls=%async_computation | async-start | bytes 9437184 | tf_op jit(solution)/shard_map/all_to_all | solution.py:202
  21.9 2.5 collective-permute-start.1
  24.3 4.2 collective-permute-start
  59.2 66.1 %collective-permute-done.1 = bf16[1,64,1024]{2,1,0:T(8,128)(2,1)} collective-permute-done((bf16[1,64,1024]{2,1,0:T(8,128)(2,1)}, bf16[1,64,1024]{2,1,0:T(8,128)(2,1)}, u32[]{:S(2)}, u32[]{:S(2)}) %collective-permute-start.1) | collective-permute-done | bytes 131104 | tf_op jit(solution)/shard_map/ppermute | solution.py:21
  144.0 5.1 %gather_fusion = bf16[26,64,1024]{2,1,0:T(8,128)(2,1)} fusion(bf16[36,64,1024]{2,1,0:T(8,128)(2,1)} %all-to-all-done, s32[1024]{0:T(1024)} %pad_clamp_fusion), kind=kCustom, calls=%fused_computation | custom fusion | bytes 6815848 | tf_op jit(solution)/shard_map/jit(_take)/gather | solution.py:53
  149.1 2.3 broadcast_select_fusion
  156.9 6.1 %fusion.311 = (f32[13,64]{1,0:T(8,128)S(1)}, f32[13,64,320]{2,1,0:T(8,128)S(1)}) fusion(f32[13,64,128]{2,1,0:T(8,128)} %copy.219, f32[13,64,64]{2,1,0:T(8,128)} %convolution_bitcast_fusion.5, f32[13,64,64]{2,1,0:T(8,128)} %convolution_bitcast_fusion.6, f32[13,64,64]{2,1,0:T(8,128)} %convolution_bitcast_fusion.7, pred[13,320]{1,0:T(8,128)(4,1)S(1)} %copy-done.89), kind=kOutput, calls=%fused_computation.441 | output fusion | flops 1863999 | bytes 2137408 | tf_op jit(solution)/shard_map/sub | solution.py:88
  172.7 6.1 %fusion.312 = (f32[13,64]{1,0:T(8,128)S(1)}, f32[13,64,320]{2,1,0:T(8,128)S(1)}) fusion(f32[13,64,128]{2,1,0:T(8,128)} %copy.217, f32[13,64,64]{2,1,0:T(8,128)} %convolution_bitcast_fusion.13, f32[13,64,64]{2,1,0:T(8,128)} %convolution_bitcast_fusion.14, f32[13,64,64]{2,1,0:T(8,128)} %convolution_bitcast_fusion.15, pred[13,320]{1,0:T(8,128)(4,1)S(1)} %copy-done.89), kind=kOutput, calls=%fused_computation.442 | output fusion | flops 1863999 | bytes 2137408 | tf_op jit(solution)/shard_map/sub | solution.py:88
  188.6 6.5 %fusion.313 = (f32[13,64]{1,0:T(8,128)S(1)}, f32[13,64,320]{2,1,0:T(8,128)S(1)}) fusion(f32[13,64,128]{2,1,0:T(8,128)} %copy.215, f32[13,64,64]{2,1,0:T(8,128)} %convolution_bitcast_fusion.21, f32[13,64,64]{2,1,0:T(8,128)} %convolution_bitcast_fusion.22, f32[13,64,64]{2,1,0:T(8,128)} %convolution_bitcast_fusion.23, pred[13,320]{1,0:T(8,128)(4,1)S(1)} %copy-done.89), kind=kOutput, calls=%fused_computation.443 | output fusion | flops 1863999 | bytes 2137408 | tf_op jit(solution)/shard_map/sub | solution.py:88
  205.0 6.1 %fusion.314 = (f32[13,64]{1,0:T(8,128)S(1)}, f32[13,64,320]{2,1,0:T(8,128)S(1)}) fusion(f32[13,64,128]{2,1,0:T(8,128)} %copy.124, f32[13,64,64]{2,1,0:T(8,128)} %convolution_bitcast_fusion.29, f32[13,64,64]{2,1,0:T(8,128)} %convolution_bitcast_fusion.30, f32[13,64,64]{2,1,0:T(8,128)} %convolution_bitcast_fusion.31, pred[13,320]{1,0:T(8,128)(4,1)S(1)} %copy-done.89), kind=kOutput, calls=%fused_computation.444 | output fusion | flops 1863999 | bytes 2137408 | tf_op jit(solution)/shard_map/sub | solution.py:88
  282.0 2.8 broadcast_in_dim.68
  284.7 10.9 %scatter_fusion = bf16[36,64,1024]{2,1,0:T(8,128)(2,1)} fusion(bf16[36,64,1024]{2,1,0:T(8,128)(2,1)} %broadcast_in_dim.68, s32[26]{0:T(128)S(1)} %copy-done.90, bf16[26,64,1024]{2,1,0:T(8,128)(2,1)} %bitcast.344), kind=kCustom, calls=%fused_computation.1 | custom fusion | bytes 10223720 | tf_op jit(solution)/shard_map/scatter | solution.py:263
  295.7 5.1 %all-to-all-start.1 = ((bf16[36,64,1024]{2,1,0:T(8,128)(2,1)}), bf16[36,64,1024]{2,1,0:T(8,128)(2,1)}, u32[]{:S(2)}, u32[]{:S(2)}) async-start(bf16[36,64,1024]{2,1,0:T(8,128)(2,1)} %scatter_fusion), calls=%async_computation.1 | async-start | bytes 9437184 | tf_op jit(solution)/shard_map/all_to_all | solution.py:265
  310.0 4.1 slice.485
  314.2 4.2 %collective-permute-start.3 = (bf16[1,64,1024]{2,1,0:T(8,128)(2,1)S(1)}, bf16[1,64,1024]{2,1,0:T(8,128)(2,1)S(1)}, u32[]{:S(2)}, u32[]{:S(2)}) collective-permute-start(bf16[1,64,1024]{2,1,0:T(8,128)(2,1)S(1)} %slice.819), channel_id=1, source_target_pairs={{4,0},{8,4},{12,8},{5,1},{9,5},{13,9},{6,2},{10,6},{14,10},{7,3},{... | collective-permute-start | bytes 393224 | tf_op jit(solution)/shard_map/ppermute | solution.py:21
  331.7 72.4 %collective-permute-done.3 = bf16[1,64,1024]{2,1,0:T(8,128)(2,1)S(1)} collective-permute-done((bf16[1,64,1024]{2,1,0:T(8,128)(2,1)S(1)}, bf16[1,64,1024]{2,1,0:T(8,128)(2,1)S(1)}, u32[]{:S(2)}, u32[]{:S(2)}) %collective-permute-start.3) | collective-permute-done | bytes 131104 | tf_op jit(solution)/shard_map/ppermute | solution.py:21
  404.1 2.8 collective-permute-done.2
  407.7 3.0 slice_bitcast_fusion
  410.7 5.7 %fusion.4 = f32[13,64,1024]{2,0,1:T(8,128)S(1)} fusion(bf16[64,1024,36]{1,0,2:T(8,128)(2,1)S(1)} %slice_bitcast_fusion, bf16[36,13]{1,0:T(8,128)(2,1)S(1)} %reshape.252), kind=kOutput, calls=%fused_computation.7 | convolution fusion | flops 61341696 | bytes 8127400 | tf_op jit(solution)/shard_map/dot_general | solution.py:266
  416.4 3.4 fusion.8
  (358 shorter events, 182.6 us)
Async XLA Ops:
  15.7 28.6 %copy-start = (bf16[832,512]{1,0:T(8,128)(2,1)S(1)}, bf16[832,512]{1,0:T(8,128)(2,1)}, u32[]{:S(2)}) copy-start(bf16[832,512]{1,0:T(8,128)(2,1)} %param.9) | copy-start | bytes 2555908
  15.7 128.2 %all-to-all-start = ((bf16[36,64,1024]{2,1,0:T(8,128)(2,1)}), bf16[36,64,1024]{2,1,0:T(8,128)(2,1)}, u32[]{:S(2)}, u32[]{:S(2)}) async-start(bf16[36,64,1024]{2,1,0:T(8,128)(2,1)} %slice.488), calls=%async_computation | async-start | bytes 9437184 | tf_op jit(solution)/shard_map/all_to_all | solution.py:202
  21.1 25.2 %copy-start.1 = (bf16[832,512]{1,0:T(8,128)(2,1)S(1)}, bf16[832,512]{1,0:T(8,128)(2,1)}, u32[]{:S(2)}) copy-start(bf16[832,512]{1,0:T(8,128)(2,1)} %param.6) | copy-start | bytes 2555908
  21.9 103.5 %collective-permute-start.1 = (bf16[1,64,1024]{2,1,0:T(8,128)(2,1)}, bf16[1,64,1024]{2,1,0:T(8,128)(2,1)}, u32[]{:S(2)}, u32[]{:S(2)}) collective-permute-start(bf16[1,64,1024]{2,1,0:T(8,128)(2,1)} %get-tuple-element.24), channel_id=1, source_target_pairs={{4,0},{8,4},{12,8},{5,1},{9,5},{13,9},{6,2},{10,6},{14,10},{7,3},{... | collective-permute-start | bytes 393224 | tf_op jit(solution)/shard_map/ppermute | solution.py:21
  24.3 102.4 %collective-permute-start = (bf16[1,64,1024]{2,1,0:T(8,128)(2,1)}, bf16[1,64,1024]{2,1,0:T(8,128)(2,1)S(1)}, u32[]{:S(2)}, u32[]{:S(2)}) collective-permute-start(bf16[1,64,1024]{2,1,0:T(8,128)(2,1)} %get-tuple-element.23), channel_id=1, source_target_pairs={{0,4},{4,8},{8,12},{1,5},{5,9},{9,13},{2,6},{6,10},{10,14},{3,7},{... | collective-permute-start | bytes 393224 | tf_op jit(solution)/shard_map/ppermute | solution.py:18
  126.7 9.1 %copy-start.46 = (bf16[13,64,128]{2,1,0:T(8,128)(2,1)}, bf16[13,64,128]{2,1,0:T(8,128)(2,1)S(1)}, u32[]{:S(2)}) copy-start(bf16[13,64,128]{2,1,0:T(8,128)(2,1)S(1)} %get-tuple-element.17) | copy-start | bytes 638980
  126.7 11.1 %copy-start.38 = (bf16[13,64,128]{2,1,0:T(8,128)(2,1)}, bf16[13,64,128]{2,1,0:T(8,128)(2,1)S(1)}, u32[]{:S(2)}) copy-start(bf16[13,64,128]{2,1,0:T(8,128)(2,1)S(1)} %get-tuple-element.18) | copy-start | bytes 638980
  126.7 13.2 %copy-start.44 = (bf16[13,64,128]{2,1,0:T(8,128)(2,1)}, bf16[13,64,128]{2,1,0:T(8,128)(2,1)S(1)}, u32[]{:S(2)}) copy-start(bf16[13,64,128]{2,1,0:T(8,128)(2,1)S(1)} %get-tuple-element.19) | copy-start | bytes 638980
  126.7 15.3 %copy-start.36 = (bf16[13,64,128]{2,1,0:T(8,128)(2,1)}, bf16[13,64,128]{2,1,0:T(8,128)(2,1)S(1)}, u32[]{:S(2)}) copy-start(bf16[13,64,128]{2,1,0:T(8,128)(2,1)S(1)} %get-tuple-element.13) | copy-start | bytes 638980
  127.2 7.5 %copy-start.56 = (bf16[13,64,128]{2,1,0:T(8,128)(2,1)}, bf16[13,64,128]{2,1,0:T(8,128)(2,1)S(1)}, u32[]{:S(2)}) copy-start(bf16[13,64,128]{2,1,0:T(8,128)(2,1)S(1)} %get-tuple-element.8) | copy-start | bytes 638980
  127.2 9.6 %copy-start.60 = (bf16[13,64,128]{2,1,0:T(8,128)(2,1)}, bf16[13,64,128]{2,1,0:T(8,128)(2,1)S(1)}, u32[]{:S(2)}) copy-start(bf16[13,64,128]{2,1,0:T(8,128)(2,1)S(1)} %get-tuple-element.9) | copy-start | bytes 638980
  127.2 11.6 %copy-start.54 = (bf16[13,64,128]{2,1,0:T(8,128)(2,1)}, bf16[13,64,128]{2,1,0:T(8,128)(2,1)S(1)}, u32[]{:S(2)}) copy-start(bf16[13,64,128]{2,1,0:T(8,128)(2,1)S(1)} %get-tuple-element.10) | copy-start | bytes 638980
  127.3 13.7 %copy-start.63 = (bf16[13,64,128]{2,1,0:T(8,128)(2,1)}, bf16[13,64,128]{2,1,0:T(8,128)(2,1)S(1)}, u32[]{:S(2)}) copy-start(bf16[13,64,128]{2,1,0:T(8,128)(2,1)S(1)} %get-tuple-element.11) | copy-start | bytes 638980
  127.3 15.7 %copy-start.52 = (bf16[13,64,128]{2,1,0:T(8,128)(2,1)}, bf16[13,64,128]{2,1,0:T(8,128)(2,1)S(1)}, u32[]{:S(2)}) copy-start(bf16[13,64,128]{2,1,0:T(8,128)(2,1)S(1)} %get-tuple-element.5) | copy-start | bytes 638980
  163.2 7.3 %copy-start.14 = (bf16[13,64,320]{2,1,0:T(8,128)(2,1)}, bf16[13,64,320]{2,1,0:T(8,128)(2,1)S(1)}, u32[]{:S(2)}) copy-start(bf16[13,64,320]{2,1,0:T(8,128)(2,1)S(1)} %fusion.96) | copy-start | bytes 1597444
  179.1 7.4 %copy-start.16 = (bf16[13,64,320]{2,1,0:T(8,128)(2,1)}, bf16[13,64,320]{2,1,0:T(8,128)(2,1)S(1)}, u32[]{:S(2)}) copy-start(bf16[13,64,320]{2,1,0:T(8,128)(2,1)S(1)} %fusion.95) | copy-start | bytes 1597444
  195.4 7.4 %copy-start.18 = (bf16[13,64,320]{2,1,0:T(8,128)(2,1)}, bf16[13,64,320]{2,1,0:T(8,128)(2,1)S(1)}, u32[]{:S(2)}) copy-start(bf16[13,64,320]{2,1,0:T(8,128)(2,1)S(1)} %fusion.94) | copy-start | bytes 1597444
  295.7 112.0 %all-to-all-start.1 = ((bf16[36,64,1024]{2,1,0:T(8,128)(2,1)}), bf16[36,64,1024]{2,1,0:T(8,128)(2,1)}, u32[]{:S(2)}, u32[]{:S(2)}) async-start(bf16[36,64,1024]{2,1,0:T(8,128)(2,1)} %scatter_fusion), calls=%async_computation.1 | async-start | bytes 9437184 | tf_op jit(solution)/shard_map/all_to_all | solution.py:265
  310.0 10.4 %copy-start.3 = (bf16[13,2,64,1024]{3,2,1,0:T(8,128)(2,1)S(1)}, bf16[13,2,64,1024]{3,2,1,0:T(8,128)(2,1)}, u32[]{:S(2)}) copy-start(bf16[13,2,64,1024]{3,2,1,0:T(8,128)(2,1)} %copy-done.2) | copy-start | bytes 10223620
  310.0 10.4 %copy-start.82 = (bf16[13,64,128]{1,2,0:T(8,128)(2,1)S(1)}, bf16[13,64,128]{1,2,0:T(8,128)(2,1)}, u32[]{:S(2)}) copy-start(bf16[13,64,128]{1,2,0:T(8,128)(2,1)} %copy.228) | copy-start | bytes 638980
  310.0 10.7 %copy-start.84 = (bf16[13,64,128]{1,2,0:T(8,128)(2,1)S(1)}, bf16[13,64,128]{1,2,0:T(8,128)(2,1)}, u32[]{:S(2)}) copy-start(bf16[13,64,128]{1,2,0:T(8,128)(2,1)} %copy.226) | copy-start | bytes 638980
  314.2 89.9 %collective-permute-start.3 = (bf16[1,64,1024]{2,1,0:T(8,128)(2,1)S(1)}, bf16[1,64,1024]{2,1,0:T(8,128)(2,1)S(1)}, u32[]{:S(2)}, u32[]{:S(2)}) collective-permute-start(bf16[1,64,1024]{2,1,0:T(8,128)(2,1)S(1)} %slice.819), channel_id=1, source_target_pairs={{4,0},{8,4},{12,8},{5,1},{9,5},{13,9},{6,2},{10,6},{14,10},{7,3},{... | collective-permute-start | bytes 393224 | tf_op jit(solution)/shard_map/ppermute | solution.py:21
  318.4 88.5 %collective-permute-start.2 = (bf16[1,64,1024]{2,1,0:T(8,128)(2,1)S(1)}, bf16[1,64,1024]{2,1,0:T(8,128)(2,1)S(1)}, u32[]{:S(2)}, u32[]{:S(2)}) collective-permute-start(bf16[1,64,1024]{2,1,0:T(8,128)(2,1)S(1)} %slice.820), channel_id=1, source_target_pairs={{0,4},{4,8},{8,12},{1,5},{5,9},{9,13},{2,6},{6,10},{10,14},{3,7},{... | collective-permute-start | bytes 393224 | tf_op jit(solution)/shard_map/ppermute | solution.py:18
  407.7 8.7 %copy-start.29 = (f32[13,64,1024]{2,1,0:T(8,128)S(1)}, f32[13,64,1024]{2,1,0:T(8,128)}, u32[]{:S(2)}) copy-start(f32[13,64,1024]{2,1,0:T(8,128)} %copy-done.28) | copy-start | bytes 10223620
  (75 other events, 247.3 us)
where the time goes:
time: 429 us; the launch traced here: 421 us
  waiting for transfers between devices  141 us (33%)
  matrix products  105 us (24%)
  local copies, waits for them, and re-layouts  100 us (23%)
  other arithmetic  49.4 us (12%)
  starting transfers between devices  23.3 us (5%)
    ppermute x2, waiting for transfers between devices, extended(): lax.ppermute(lax.slice_in_dim(block, 0, width, axis=dim), axis, backward)  139 us
    sub x4, other arithmetic, forward_head(): exponent = jnp.exp(attention_logits - row_max)  25 us
    dot_general x12, matrix products, backward_head(): jnp.einsum('bjx,bje->bxe', softmax_weights[:, :, columns], gradient_tiles...  14.3 us
    dot_general x12, matrix products, backward_head(): jnp.einsum('bje,bxe->bjx', gradient_tiles, piece, preferred_element_type=...  12.5 us
    dot_general x12, matrix products, backward_head(): jnp.einsum('bjx,bje->bxe', score_gradient[:, :, columns], query_tiles, pr...  12.5 us
    dot_general x12, matrix products, forward_head(): jnp.einsum('bje,bxe->bjx', query_tiles, piece, preferred_element_type=jnp...  12.3 us
    unnamed x189, local copies, waits for them, and re-layouts  11.9 us
    scatter x1, local copies, waits for them, and re-layouts, shards(): returning = jnp.zeros((seq_size * capacity, BLOCK, 2 * row_width), jnp.bf...  10.9 us
  transfers between devices with their start and end apart: 6, of which 3 were waited for; matrix products, arithmetic and copies ran while one was open for 17% of the time, Pallas kernels for 0%

commit v1 on v0

--- a/solution.py
+++ b/solution.py
@@ -3,6 +3,8 @@
 import jax
 import jax.numpy as jnp
 from jax import lax
+from jax.experimental import pallas as pl
+from jax.experimental.pallas import tpu as pltpu
 from jax.sharding import PartitionSpec as P
 
 DH = 128
@@ -180,7 +182,7 @@
     return (query_gradient, key_window, value_window, key_far_terms, value_far_terms)
 
 
-def shards(queries, key_rows, value_rows, out_grad, random_device, random_block):
+def exchanged_shards(queries, key_rows, value_rows, out_grad, random_device, random_block):
     seq_size = lax.axis_size("seq")
     own_index = lax.axis_index("seq")
     tokens, row_width = queries.shape
@@ -278,6 +280,149 @@
     )
 
 
+SLOTS = 3 + RAND
+
+
+def block_kernel(ids_ref, valid_ref, q_ref, g_ref, *rest):
+    kv_refs = rest[:SLOTS]
+    dq_ref, terms_ref = rest[SLOTS:]
+    step = pl.program_id(0)
+    width = q_ref.shape[1]
+    logit_scale = 1.0 / math.sqrt(DH)
+    context = jnp.concatenate([ref[0] for ref in kv_refs], axis=0)
+    slot_of = lax.broadcasted_iota(jnp.int32, (1, SLOTS * BLOCK), 1) // BLOCK
+    usable = slot_of < 0
+    for slot in range(SLOTS):
+        usable = usable | ((slot_of == slot) & (valid_ref[step * SLOTS + slot] > 0))
+    for head in range(width // DH):
+        cols = slice(head * DH, (head + 1) * DH)
+        vcols = slice(width + head * DH, width + (head + 1) * DH)
+        query = q_ref[:, cols]
+        grad = g_ref[:, cols]
+        keys = context[:, cols]
+        values = context[:, vcols]
+        logits = lax.dot_general(
+            query, keys, (((1,), (1,)), ((), ())), preferred_element_type=jnp.float32
+        ) * logit_scale
+        logits = jnp.where(usable, logits, -jnp.inf)
+        row_max = jnp.max(logits, axis=-1, keepdims=True)
+        exponent = jnp.exp(logits - row_max)
+        row_total = jnp.sum(exponent, axis=-1, keepdims=True)
+        probability = exponent / row_total
+        weights = probability.astype(jnp.bfloat16)
+        attended = jnp.dot(weights, values, preferred_element_type=jnp.float32).astype(
+            jnp.bfloat16
+        )
+        row_delta = jnp.sum(
+            grad.astype(jnp.float32) * attended.astype(jnp.float32), axis=-1, keepdims=True
+        )
+        prob_grad = lax.dot_general(
+            grad, values, (((1,), (1,)), ((), ())), preferred_element_type=jnp.float32
+        )
+        score_grad = (probability * (prob_grad - row_delta)).astype(jnp.bfloat16)
+        query_grad = logit_scale * jnp.dot(
+            score_grad, keys, preferred_element_type=jnp.float32
+        )
+        dq_ref[:, cols] = query_grad.astype(jnp.bfloat16)
+        key_terms = logit_scale * lax.dot_general(
+            score_grad, query, (((0,), (0,)), ((), ())), preferred_element_type=jnp.float32
+        )
+        value_terms = lax.dot_general(
+            weights, grad, (((0,), (0,)), ((), ())), preferred_element_type=jnp.float32
+        )
+        for slot in range(SLOTS):
+            rows = slice(slot * BLOCK, (slot + 1) * BLOCK)
+            terms_ref[0, slot, :, cols] = key_terms[rows]
+            terms_ref[0, slot, :, vcols] = value_terms[rows]
+
+
+def block_attention(ids, valid, queries, out_grad, source):
+    tokens, width = queries.shape
+    blocks_dev = tokens // BLOCK
+
+    def context_spec(slot):
+        return pl.BlockSpec(
+            (1, BLOCK, 2 * width), lambda i, ids, valid: (ids[i * SLOTS + slot], 0, 0)
+        )
+
+    row_spec = pl.BlockSpec((BLOCK, width), lambda i, ids, valid: (i, 0))
+    grid_spec = pltpu.PrefetchScalarGridSpec(
+        num_scalar_prefetch=2,
+        grid=(blocks_dev,),
+        in_specs=[row_spec, row_spec] + [context_spec(s) for s in range(SLOTS)],
+        out_specs=[
+            row_spec,
+            pl.BlockSpec(
+                (1, SLOTS, BLOCK, 2 * width), lambda i, ids, valid: (i, 0, 0, 0)
+            ),
+        ],
+    )
+    return pl.pallas_call(
+        block_kernel,
+        grid_spec=grid_spec,
+        out_shape=[
+            jax.ShapeDtypeStruct((tokens, width), jnp.bfloat16),
+            jax.ShapeDtypeStruct((blocks_dev, SLOTS, BLOCK, 2 * width), jnp.float32),
+        ],
+    )(ids, valid, queries, out_grad, *([source] * SLOTS))
+
+
+def gathered_shards(queries, key_rows, value_rows, out_grad, random_device, random_block):
+    seq_size = lax.axis_size("seq")
+    own_index = lax.axis_index("seq")
+    tokens, width = queries.shape
+    blocks_dev = tokens // BLOCK
+    total = seq_size * blocks_dev
+    first = own_index * blocks_dev
+    packed = jnp.concatenate([key_rows, value_rows], axis=1)
+    source = lax.all_gather(packed, "seq", axis=0, tiled=True).reshape(total, BLOCK, 2 * width)
+    block_ids = first + jnp.arange(blocks_dev, dtype=jnp.int32)
+    own_device = lax.dynamic_slice_in_dim(random_device, first, blocks_dev, 0)
+    own_block = lax.dynamic_slice_in_dim(random_block, first, blocks_dev, 0)
+    chosen = (own_device * blocks_dev + own_block).astype(jnp.int32)
+    window = jnp.stack(
+        [jnp.clip(block_ids - 1, 0, total - 1), block_ids, jnp.clip(block_ids + 1, 0, total - 1)],
+        axis=1,
+    )
+    ids = jnp.concatenate([window, chosen], axis=1)
+    always = jnp.ones_like(block_ids, dtype=jnp.bool_)
+    valid = jnp.stack([block_ids > 0, always, block_ids < total - 1] + [always] * RAND, axis=1)
+    query_out, terms = block_attention(
+        ids.reshape(-1), valid.astype(jnp.int32).reshape(-1), queries, out_grad, source
+    )
+    zero_block = jnp.zeros((1, BLOCK, 2 * width), jnp.float32)
+    own_sum = (
+        terms[:, 1]
+        + jnp.concatenate([terms[1:, 0], zero_block], axis=0)
+        + jnp.concatenate([zero_block, terms[:-1, 2]], axis=0)
+    )
+    far_terms = terms[:, 3:].astype(jnp.bfloat16).reshape(blocks_dev * RAND, BLOCK * 2 * width)
+    edge_terms = jnp.stack([terms[0, 0], terms[-1, 2]]).astype(jnp.bfloat16)
+    sent = jnp.concatenate([far_terms, edge_terms.reshape(2, BLOCK * 2 * width)], axis=0)
+    targets = jnp.concatenate([chosen.reshape(-1), jnp.stack([first - 1, first + blocks_dev])])
+    target_ok = jnp.concatenate(
+        [jnp.ones((blocks_dev * RAND,), jnp.bool_), jnp.stack([first > 0, first + blocks_dev < total])]
+    )
+    placement = (
+        (targets[None, :] == jnp.arange(total, dtype=jnp.int32)[:, None]) & target_ok[None, :]
+    ).astype(jnp.bfloat16)
+    spread = jnp.dot(placement, sent, preferred_element_type=jnp.float32).astype(jnp.bfloat16)
+    spread = spread.reshape(total * BLOCK, 2 * width)
+    returned = lax.psum_scatter(spread, "seq", scatter_dimension=0, tiled=True)
+    summed = own_sum.reshape(tokens, 2 * width) + returned.astype(jnp.float32)
+    return (
+        query_out,
+        summed[:, :width].astype(jnp.bfloat16),
+        summed[:, width:].astype(jnp.bfloat16),
+    )
+
+
+def shards(queries, key_rows, value_rows, out_grad, random_device, random_block):
+    if lax.axis_size("seq") <= 8:
+        return gathered_shards(queries, key_rows, value_rows, out_grad, random_device, random_block)
+    return exchanged_shards(queries, key_rows, value_rows, out_grad, random_device, random_block)
+
+
 def solution(mesh):
     return jax.shard_map(
         shards,

time: 429 us -> 328 us (0.76); the launches traced: 421 us -> 327 us
  matrix products: 105 us -> 4.03 us
  waiting for transfers between devices: 141 us -> 233 us
  local copies, waits for them, and re-layouts: 100 us -> 21.9 us
  Pallas kernels: 0 us -> 37.9 us
  other arithmetic: 49.4 us -> 15.5 us
  starting transfers between devices: 23.3 us -> 0.08 us
  between operations: 2.29 us -> 14.2 us
    ppermute x4 -> x0, waiting for transfers between devices: 141 us -> none  [the longest x2 139 us: extended(): lax.ppermute(lax.slice_in_dim(block, 0, width, axis=dim), axis, backward)]
    all_gather x0 -> x1, waiting for transfers between devices: none -> 121 us  [gathered_shards(): lax.all_gather(packed, 'seq', axis=0, tiled=True)]
    reduce_scatter x0 -> x1, waiting for transfers between devices: none -> 112 us  [gathered_shards(): returned = lax.psum_scatter(spread, 'seq', scatter_dimension=0, tiled=True)]
    dot_general x99 -> x1, matrix products: 105 us -> 4.03 us  [gathered_shards(): jnp.dot(placement, sent, preferred_element_type=jnp.float32)]
    pallas_call x0 -> x1, Pallas kernels: none -> 37.9 us  [block_attention(): pl.pallas_call(block_kernel, grid_spec=grid_spec, out_shape=[jax.ShapeDty...]
    reshape x18 -> x3, local copies, waits for them, and re-layouts: 37.1 us -> 10.9 us  [the longest x1 10.2 us: gathered_shards(): spread = spread.reshape(total * BLOCK, 2 * width)]
    sub x5 -> x0, other arithmetic: 25 us -> none  [the longest x4 25 us: forward_head(): exponent = jnp.exp(attention_logits - row_max)]
    slice x14 -> x2, local copies, waits for them, and re-layouts: 15.7 us -> 1.85 us  [the longest x1 1.32 us: gathered_shards(): summed[:, width:].astype(jnp.bfloat16)]
  transfers between devices with their start and end apart: 6 -> 2, of which waited for: 3 -> 2; matrix products, arithmetic and copies ran while one was open for 17% -> 3% of each run, Pallas kernels for 0% -> 0%
where the time goes in v1:
time: 328 us; the launch traced here: 327 us
  waiting for transfers between devices  233 us (71%)
  Pallas kernels  37.9 us (12%)
  local copies, waits for them, and re-layouts  21.9 us (7%)
  other arithmetic  15.5 us (5%)
  between operations  14.2 us (4%)
  matrix products  4.03 us (1%)
    all_gather x1, waiting for transfers between devices, gathered_shards(): lax.all_gather(packed, 'seq', axis=0, tiled=True)  121 us
    reduce_scatter x1, waiting for transfers between devices, gathered_shards(): returned = lax.psum_scatter(spread, 'seq', scatter_dimension=0, tiled=True)  112 us
    pallas_call x1, Pallas kernels, block_attention(): pl.pallas_call(block_kernel, grid_spec=grid_spec, out_shape=[jax.ShapeDty...  37.9 us
    reshape x1, local copies, waits for them, and re-layouts, gathered_shards(): spread = spread.reshape(total * BLOCK, 2 * width)  10.2 us
    another operation x2, other arithmetic  9.01 us
  transfers between devices with their start and end apart: 2, of which 2 were waited for; matrix products, arithmetic and copies ran while one was open for 3% of the time, Pallas kernels for 0%

profile of v1, /device:TPU:22, one launch (start us, length us, event | category | flops | bytes accessed | tf_op | source)
XLA Modules:
  0.0 326.7 jit_solution(9621906147143635889)
XLA Ops:
  7.2 2.8 pad_maximum_fusion
  10.3 0.1 copy.17
  10.4 0.1 copy.16
  10.6 0.6 reshape.72.valid_ref
  11.3 0.1 copy.20
  11.4 0.1 copy.15
  11.5 0.6 reshape.66.ids_ref
  12.2 0.1 pad_add_fusion.1
  12.4 121.0 %all-gather.2.cloned.1.call-done = bf16[3328,1024]{1,0:T(8,128)(2,1)} async-done(((bf16[832,1024]{1,0:T(8,128)(2,1)}), bf16[3328,1024]{1,0:T(8,128)(2,1)}) %all-gather.2.cloned.1.call-update) | async-done | bytes 6815760 | tf_op jit(solution)/shard_map/all_gather | solution.py:378
  133.4 37.9 %shard_map.85 = (bf16[832,512]{1,0:T(8,128)(2,1)}, f32[13,5,64,1024]{3,2,1,0:T(8,128)}) custom-call(s32[65]{0:T(128)} %reshape.66.ids_ref, s32[65]{0:T(128)} %reshape.72.valid_ref, bf16[832,512]{1,0:T(8,128)(2,1)} %q_ref.1, bf16[832,512]{1,0:T(8,128)(2,1)} %g_ref.1, bf16[52,64,1024]{2,1,0:T(8,128)(2,1)} %bitcast.32, bf16[52,64,1024]{2,1,0:T(8,128)(2,1)} %bitcast.33, ...), custom_call_target="tpu_custom_call" | custom-call | tf_op jit(solution)/shard_map/pallas_call | solution.py:360
  171.3 6.7 %convert.14 = bf16[13,5,64,1024]{3,2,1,0:T(8,128)(2,1)S(1)} convert(f32[13,5,64,1024]{3,2,1,0:T(8,128)} %get-tuple-element.6) | non-fusion elementwise | flops 4259840 | bytes 25559040 | tf_op jit(solution)/shard_map/convert.9
  178.1 0.5 slice.39
  178.6 0.2 copy.22
  178.8 0.2 copy.23
  179.0 0.6 pad.21
  179.6 2.3 copy.21
  182.0 4.0 %convolution_convert_fusion = bf16[52,65536]{1,0:T(8,128)(2,1)} fusion(bf16[1,65536]{1,0:T(2,128)(2,1)S(1)} %bitcast.41, bf16[1,65536]{1,0:T(2,128)(2,1)S(1)} %bitcast.40, bf16[26,65536]{1,0:T(8,128)(2,1)S(1)} %bitcast.37, s32[28]{0:T(128)S(1)} %pad_add_fusion.2, pred[28]{0:T(512)(128)(4,1)S(1)} %pad_add_fusion.1), kind=kOutput, calls=%fused_computation | convolution fusion | flops 205261664 | bytes 10485900 | tf_op jit(solution)/shard_map/dot_general | solution.py:409
  186.0 10.2 %reshape.71 = bf16[3328,1024]{1,0:T(8,128)(2,1)} reshape(bf16[52,65536]{1,0:T(8,128)(2,1)} %convolution_convert_fusion) | data formatting | bytes 13631488 | tf_op jit(solution)/shard_map/reshape | solution.py:410
  196.3 2.3 slice_bitcast_fusion.2
  198.6 2.3 slice_bitcast_fusion.1
  200.8 3.3 %fusion.6 = f32[13,64,1024]{2,1,0:T(8,128)S(1)} fusion(f32[12,64,1024]{2,1,0:T(8,128)S(1)} %slice_bitcast_fusion.2, f32[12,64,1024]{2,1,0:T(8,128)S(1)} %slice_bitcast_fusion.1, f32[13,5,64,1024]{3,2,1,0:T(8,128)} %get-tuple-element.6), kind=kLoop, calls=%fused_computation.8 | loop fusion | flops 1703936 | bytes 13107200 | tf_op jit(solution)/shard_map/add | solution.py:395
  204.1 112.1 %reduce-scatter.2.cloned.1.call-done = bf16[832,1024]{1,0:T(8,128)(2,1)} async-done(((bf16[3328,1024]{1,0:T(8,128)(2,1)}), bf16[832,1024]{1,0:T(8,128)(2,1)}) %reduce-scatter.2.cloned.1.call-update) | async-done | bytes 1703952 | tf_op jit(solution)/shard_map/reduce_scatter | solution.py:411
  316.2 2.3 fusion.7
  318.5 1.3 fusion.13
  (21 shorter events, 0.6 us)
Async XLA Ops:
  7.2 4.1 %copy-start = (s32[52,2]{0,1:T(2,128)S(1)}, s32[52,2]{0,1:T(2,128)}, u32[]{:S(2)}) copy-start(s32[52,2]{0,1:T(2,128)} %param.11) | copy-start | bytes 1252
  7.2 4.1 %copy-start.1 = (s32[52,2]{0,1:T(2,128)S(1)}, s32[52,2]{0,1:T(2,128)}, u32[]{:S(2)}) copy-start(s32[52,2]{0,1:T(2,128)} %param.10) | copy-start | bytes 1252
  7.2 126.2 %all-gather.2.cloned.1.call-start = ((), (), s32[]{:S(2)}) async-start(), calls=%async_computation.1 | async-start | bytes 8519680 | tf_op jit(solution)/shard_map/all_gather | solution.py:378
  10.1 306.1 %reduce-scatter.2.cloned.1.call-start = ((), (), s32[]{:S(2)}) async-start(), calls=%async_computation.2 | async-start | bytes 8519680 | tf_op jit(solution)/shard_map/reduce_scatter | solution.py:411
Sparse Core Ops, SparseCore 0:
  10.2 123.1 all-gather.1
  196.4 119.7 reduce-scatter.1

commit v2 on v1

--- a/solution.py
+++ b/solution.py
@@ -283,17 +283,25 @@
 SLOTS = 3 + RAND
 
 
-def block_kernel(ids_ref, valid_ref, q_ref, g_ref, *rest):
+def block_kernel(ids_ref, valid_ref, first_ref, q_ref, g_ref, *rest):
     kv_refs = rest[:SLOTS]
-    dq_ref, terms_ref = rest[SLOTS:]
+    own_ref, spread_ref, dq_ref, acc_ref = rest[SLOTS:]
     step = pl.program_id(0)
+    steps = pl.num_programs(0)
     width = q_ref.shape[1]
+    blocks_dev = own_ref.shape[0]
     logit_scale = 1.0 / math.sqrt(DH)
+
+    @pl.when(step == 0)
+    def _():
+        acc_ref[...] = jnp.zeros(acc_ref.shape, jnp.float32)
+
     context = jnp.concatenate([ref[0] for ref in kv_refs], axis=0)
-    slot_of = lax.broadcasted_iota(jnp.int32, (1, SLOTS * BLOCK), 1) // BLOCK
+    slot_of = lax.broadcasted_iota(jnp.int32, (SLOTS * BLOCK, 1), 0) // BLOCK
     usable = slot_of < 0
     for slot in range(SLOTS):
         usable = usable | ((slot_of == slot) & (valid_ref[step * SLOTS + slot] > 0))
+    key_parts, value_parts = [], []
     for head in range(width // DH):
         cols = slice(head * DH, (head + 1) * DH)
         vcols = slice(width + head * DH, width + (head + 1) * DH)
@@ -302,69 +310,82 @@
         keys = context[:, cols]
         values = context[:, vcols]
         logits = lax.dot_general(
-            query, keys, (((1,), (1,)), ((), ())), preferred_element_type=jnp.float32
+            keys, query, (((1,), (1,)), ((), ())), preferred_element_type=jnp.float32
         ) * logit_scale
         logits = jnp.where(usable, logits, -jnp.inf)
-        row_max = jnp.max(logits, axis=-1, keepdims=True)
+        row_max = jnp.max(logits, axis=0, keepdims=True)
         exponent = jnp.exp(logits - row_max)
-        row_total = jnp.sum(exponent, axis=-1, keepdims=True)
+        row_total = jnp.sum(exponent, axis=0, keepdims=True)
         probability = exponent / row_total
         weights = probability.astype(jnp.bfloat16)
-        attended = jnp.dot(weights, values, preferred_element_type=jnp.float32).astype(
-            jnp.bfloat16
-        )
-        row_delta = jnp.sum(
-            grad.astype(jnp.float32) * attended.astype(jnp.float32), axis=-1, keepdims=True
-        )
+        attended = lax.dot_general(
+            weights, values, (((0,), (0,)), ((), ())), preferred_element_type=jnp.float32
+        ).astype(jnp.bfloat16)
+        product = grad.astype(jnp.float32) * attended.astype(jnp.float32)
+        row_delta = jnp.sum(product.T, axis=0, keepdims=True)
         prob_grad = lax.dot_general(
-            grad, values, (((1,), (1,)), ((), ())), preferred_element_type=jnp.float32
+            values, grad, (((1,), (1,)), ((), ())), preferred_element_type=jnp.float32
         )
         score_grad = (probability * (prob_grad - row_delta)).astype(jnp.bfloat16)
-        query_grad = logit_scale * jnp.dot(
-            score_grad, keys, preferred_element_type=jnp.float32
+        query_grad = logit_scale * lax.dot_general(
+            score_grad, keys, (((0,), (0,)), ((), ())), preferred_element_type=jnp.float32
         )
         dq_ref[:, cols] = query_grad.astype(jnp.bfloat16)
-        key_terms = logit_scale * lax.dot_general(
-            score_grad, query, (((0,), (0,)), ((), ())), preferred_element_type=jnp.float32
-        )
-        value_terms = lax.dot_general(
-            weights, grad, (((0,), (0,)), ((), ())), preferred_element_type=jnp.float32
-        )
-        for slot in range(SLOTS):
-            rows = slice(slot * BLOCK, (slot + 1) * BLOCK)
-            terms_ref[0, slot, :, cols] = key_terms[rows]
-            terms_ref[0, slot, :, vcols] = value_terms[rows]
-
-
-def block_attention(ids, valid, queries, out_grad, source):
+        key_parts.append(
+            logit_scale * jnp.dot(score_grad, query, preferred_element_type=jnp.float32)
+        )
+        value_parts.append(jnp.dot(weights, grad, preferred_element_type=jnp.float32))
+    terms = jnp.concatenate(key_parts + value_parts, axis=1)
+    for slot in range(SLOTS):
+        piece = terms[slot * BLOCK : (slot + 1) * BLOCK]
+        if slot >= 3:
+            piece = piece.astype(jnp.bfloat16).astype(jnp.float32)
+        target = ids_ref[step * SLOTS + slot]
+        acc_ref[target] = acc_ref[target] + piece
+
+    @pl.when(step == steps - 1)
+    def _():
+        first = first_ref[0]
+        spread_ref[...] = acc_ref[...].astype(jnp.bfloat16)
+        for block in range(blocks_dev):
+            own_ref[block] = acc_ref[first + block]
+            spread_ref[first + block] = jnp.zeros(spread_ref.shape[1:], jnp.bfloat16)
+
+
+def block_attention(ids, valid, first, queries, out_grad, source):
     tokens, width = queries.shape
     blocks_dev = tokens // BLOCK
+    total = source.shape[0]
 
     def context_spec(slot):
         return pl.BlockSpec(
-            (1, BLOCK, 2 * width), lambda i, ids, valid: (ids[i * SLOTS + slot], 0, 0)
-        )
-
-    row_spec = pl.BlockSpec((BLOCK, width), lambda i, ids, valid: (i, 0))
+            (1, BLOCK, 2 * width), lambda i, ids, valid, first: (ids[i * SLOTS + slot], 0, 0)
+        )
+
+    row_spec = pl.BlockSpec((BLOCK, width), lambda i, ids, valid, first: (i, 0))
     grid_spec = pltpu.PrefetchScalarGridSpec(
-        num_scalar_prefetch=2,
+        num_scalar_prefetch=3,
         grid=(blocks_dev,),
         in_specs=[row_spec, row_spec] + [context_spec(s) for s in range(SLOTS)],
         out_specs=[
+            pl.BlockSpec(
+                (blocks_dev, BLOCK, 2 * width), lambda i, ids, valid, first: (0, 0, 0)
+            ),
+            pl.BlockSpec((total, BLOCK, 2 * width), lambda i, ids, valid, first: (0, 0, 0)),
             row_spec,
-            pl.BlockSpec(
-                (1, SLOTS, BLOCK, 2 * width), lambda i, ids, valid: (i, 0, 0, 0)
-            ),
         ],
+        scratch_shapes=[pltpu.VMEM((total, BLOCK, 2 * width), jnp.float32)],
     )
     return pl.pallas_call(
         block_kernel,
         grid_spec=grid_spec,
         out_shape=[
+            jax.ShapeDtypeStruct((blocks_dev, BLOCK, 2 * width), jnp.float32),
+            jax.ShapeDtypeStruct((total, BLOCK, 2 * width), jnp.bfloat16),
             jax.ShapeDtypeStruct((tokens, width), jnp.bfloat16),
-            jax.ShapeDtypeStruct((blocks_dev, SLOTS, BLOCK, 2 * width), jnp.float32),
         ],
-    )(ids, valid, queries, out_grad, *([source] * SLOTS))
+        compiler_params=pltpu.CompilerParams(vmem_limit_bytes=60 * 1024 * 1024),
+    )(ids, valid, first, queries, out_grad, *([source] * SLOTS))
 
 
 def gathered_shards(queries, key_rows, value_rows, out_grad, random_device, random_block):
@@ -387,28 +408,17 @@
     ids = jnp.concatenate([window, chosen], axis=1)
     always = jnp.ones_like(block_ids, dtype=jnp.bool_)
     valid = jnp.stack([block_ids > 0, always, block_ids < total - 1] + [always] * RAND, axis=1)
-    query_out, terms = block_attention(
-        ids.reshape(-1), valid.astype(jnp.int32).reshape(-1), queries, out_grad, source
-    )
-    zero_block = jnp.zeros((1, BLOCK, 2 * width), jnp.float32)
-    own_sum = (
-        terms[:, 1]
-        + jnp.concatenate([terms[1:, 0], zero_block], axis=0)
-        + jnp.concatenate([zero_block, terms[:-1, 2]], axis=0)
-    )
-    far_terms = terms[:, 3:].astype(jnp.bfloat16).reshape(blocks_dev * RAND, BLOCK * 2 * width)
-    edge_terms = jnp.stack([terms[0, 0], terms[-1, 2]]).astype(jnp.bfloat16)
-    sent = jnp.concatenate([far_terms, edge_terms.reshape(2, BLOCK * 2 * width)], axis=0)
-    targets = jnp.concatenate([chosen.reshape(-1), jnp.stack([first - 1, first + blocks_dev])])
-    target_ok = jnp.concatenate(
-        [jnp.ones((blocks_dev * RAND,), jnp.bool_), jnp.stack([first > 0, first + blocks_dev < total])]
-    )
-    placement = (
-        (targets[None, :] == jnp.arange(total, dtype=jnp.int32)[:, None]) & target_ok[None, :]
-    ).astype(jnp.bfloat16)
-    spread = jnp.dot(placement, sent, preferred_element_type=jnp.float32).astype(jnp.bfloat16)
-    spread = spread.reshape(total * BLOCK, 2 * width)
-    returned = lax.psum_scatter(spread, "seq", scatter_dimension=0, tiled=True)
+    own_sum, spread, query_out = block_attention(
+        ids.reshape(-1),
+        valid.astype(jnp.int32).reshape(-1),
+        first.reshape(1).astype(jnp.int32),
+        queries,
+        out_grad,
+        source,
+    )
+    returned = lax.psum_scatter(
+        spread.reshape(total * BLOCK, 2 * width), "seq", scatter_dimension=0, tiled=True
+    )
     summed = own_sum.reshape(tokens, 2 * width) + returned.astype(jnp.float32)
     return (
         query_out,

time: 328 us -> 313 us (0.954)
  local copies, waits for them, and re-layouts: 21.9 us -> 3.09 us
  other arithmetic: 15.5 us -> 5.38 us
  Pallas kernels: 37.9 us -> 47.6 us
  waiting for transfers between devices: 233 us -> 241 us
  matrix products: 4.03 us -> 0 us
    reshape x2 -> x0, local copies, waits for them, and re-layouts: 10.3 us -> none  [the longest x1 10.2 us: gathered_shards(): spread = spread.reshape(total * BLOCK, 2 * width)]
    pallas_call x1, Pallas kernels: 37.9 us -> 47.6 us  [block_attention(): pl.pallas_call(block_kernel, grid_spec=grid_spec, out_shape=[jax.ShapeDty...]
    reduce_scatter x1, waiting for transfers between devices: 112 us -> 120 us  [gathered_shards(): lax.psum_scatter(spread.reshape(total * BLOCK, 2 * width), 'seq', scatter...]
    another operation x2 -> x1, other arithmetic: 9.01 us -> 2.33 us
    squeeze x2 -> x0, local copies, waits for them, and re-layouts: 4.56 us -> none  [the longest x1 2.28 us: gathered_shards(): terms[:-1, 2]]
    dot_general x1 -> x0, matrix products: 4.03 us -> none  [gathered_shards(): jnp.dot(placement, sent, preferred_element_type=jnp.float32)]
    unnamed x9 -> x6, local copies, waits for them, and re-layouts: 3.38 us -> 0.01 us
  transfers between devices with their start and end apart: 2 -> 2, of which waited for: 2 -> 2; matrix products, arithmetic and copies ran while one was open for 3% -> 1% of each run, Pallas kernels for 0% -> 0%
where the time goes in v2:
time: 313 us; the launch traced here: 311 us
  waiting for transfers between devices  241 us (77%)
  Pallas kernels  47.6 us (15%)
  between operations  14.1 us (5%)
  other arithmetic  5.38 us (2%)
    all_gather x1, waiting for transfers between devices, gathered_shards(): lax.all_gather(packed, 'seq', axis=0, tiled=True)  121 us
    reduce_scatter x1, waiting for transfers between devices, gathered_shards(): lax.psum_scatter(spread.reshape(total * BLOCK, 2 * width), 'seq', scatter...  120 us
    pallas_call x1, Pallas kernels, block_attention(): pl.pallas_call(block_kernel, grid_spec=grid_spec, out_shape=[jax.ShapeDty...  47.6 us
  transfers between devices with their start and end apart: 2, of which 2 were waited for; matrix products, arithmetic and copies ran while one was open for 1% of the time, Pallas kernels for 0%

profile of v2, /device:TPU:22, one launch (start us, length us, event | category | flops | bytes accessed | tf_op | source)
XLA Modules:
  0.0 311.5 jit_solution(3215368644867622027)
XLA Ops:
  7.2 0.0 copy-start.1
  7.2 0.0 copy-start.2
  7.2 0.0 all-gather.2.cloned.1.call-start
  7.2 2.9 pad_maximum_fusion
  10.1 0.0 all-gather.2.cloned.1.call-update
  10.1 0.0 reduce-scatter.2.cloned.1.call-start
  10.2 0.1 pad.3.clone
  10.3 0.1 pad.5.clone
  10.3 0.1 copy.14
  10.5 0.1 copy.13
  10.6 0.1 add_convert_fusion
  10.6 0.7 reshape.59.valid_ref
  11.3 0.0 copy-done.1
  11.3 0.0 copy-done.2
  11.4 0.1 dynamic-slice_add_fusion
  11.5 0.1 copy.12
  11.6 0.6 reshape.54.ids_ref
  12.2 121.3 %all-gather.2.cloned.1.call-done = bf16[3328,1024]{1,0:T(8,128)(2,1)} async-done(((bf16[832,1024]{1,0:T(8,128)(2,1)}), bf16[3328,1024]{1,0:T(8,128)(2,1)}) %all-gather.2.cloned.1.call-update) | async-done | bytes 6815760 | tf_op jit(solution)/shard_map/all_gather | solution.py:399
  133.4 47.6 %shard_map.85 = (f32[13,64,1024]{2,1,0:T(8,128)}, bf16[52,64,1024]{2,1,0:T(8,128)(2,1)}, bf16[832,512]{1,0:T(8,128)(2,1)}) custom-call(s32[65]{0:T(128)} %reshape.54.ids_ref, s32[65]{0:T(128)} %reshape.59.valid_ref, s32[1]{0:T(128)} %bitcast.first_ref, bf16[832,512]{1,0:T(8,128)(2,1)} %q_ref.1, bf16[832,512]{1,0:T(8,128)(2,1)} %g_ref.1, ...), custom_call_target="tpu_custom_call" | custom-call | tf_op jit(solution)/shard_map/pallas_call | solution.py:379
  181.0 0.0 reduce-scatter.2.cloned.1.call-update
  181.0 119.9 %reduce-scatter.2.cloned.1.call-done = bf16[832,1024]{1,0:T(8,128)(2,1)} async-done(((bf16[3328,1024]{1,0:T(8,128)(2,1)}), bf16[832,1024]{1,0:T(8,128)(2,1)}) %reduce-scatter.2.cloned.1.call-update) | async-done | bytes 1703952 | tf_op jit(solution)/shard_map/reduce_scatter | solution.py:419
  301.0 0.0 copy-done
  301.0 2.3 fusion
  303.3 1.3 fusion.1
  (6 shorter events, 0.0 us)
Async XLA Ops:
  7.2 4.2 %copy-start.1 = (s32[52,2]{0,1:T(2,128)S(1)}, s32[52,2]{0,1:T(2,128)}, u32[]{:S(2)}) copy-start(s32[52,2]{0,1:T(2,128)} %param.11) | copy-start | bytes 1252
  7.2 4.2 %copy-start.2 = (s32[52,2]{0,1:T(2,128)S(1)}, s32[52,2]{0,1:T(2,128)}, u32[]{:S(2)}) copy-start(s32[52,2]{0,1:T(2,128)} %param.10) | copy-start | bytes 1252
  7.2 126.3 %all-gather.2.cloned.1.call-start = ((), (), s32[]{:S(2)}) async-start(), calls=%async_computation.1 | async-start | bytes 8519680 | tf_op jit(solution)/shard_map/all_gather | solution.py:399
  10.1 290.8 %reduce-scatter.2.cloned.1.call-start = ((), (), s32[]{:S(2)}) async-start(), calls=%async_computation.2 | async-start | bytes 8519680 | tf_op jit(solution)/shard_map/reduce_scatter | solution.py:419
  181.0 119.9 %copy-start = (f32[13,64,1024]{2,1,0:T(8,128)S(1)}, f32[13,64,1024]{2,1,0:T(8,128)}, u32[]{:S(2)}) copy-start(f32[13,64,1024]{2,1,0:T(8,128)} %get-tuple-element.7) | copy-start | bytes 10223620
Sparse Core Ops, SparseCore 0:
  10.2 123.1 all-gather.1
  181.2 119.7 reduce-scatter.1

commit v3 on v2

--- a/solution.py
+++ b/solution.py
@@ -352,8 +352,8 @@
             spread_ref[first + block] = jnp.zeros(spread_ref.shape[1:], jnp.bfloat16)
 
 
-def block_attention(ids, valid, first, queries, out_grad, source):
-    tokens, width = queries.shape
+def block_attention(ids, valid, first, queries, out_grad, source, chunk, width):
+    tokens = queries.shape[0]
     blocks_dev = tokens // BLOCK
     total = source.shape[0]
 
@@ -362,11 +362,12 @@
             (1, BLOCK, 2 * width), lambda i, ids, valid, first: (ids[i * SLOTS + slot], 0, 0)
         )
 
+    column_spec = pl.BlockSpec((BLOCK, width), lambda i, ids, valid, first: (i, chunk))
     row_spec = pl.BlockSpec((BLOCK, width), lambda i, ids, valid, first: (i, 0))
     grid_spec = pltpu.PrefetchScalarGridSpec(
         num_scalar_prefetch=3,
         grid=(blocks_dev,),
-        in_specs=[row_spec, row_spec] + [context_spec(s) for s in range(SLOTS)],
+        in_specs=[column_spec, column_spec] + [context_spec(s) for s in range(SLOTS)],
         out_specs=[
             pl.BlockSpec(
                 (blocks_dev, BLOCK, 2 * width), lambda i, ids, valid, first: (0, 0, 0)
@@ -395,8 +396,6 @@
     blocks_dev = tokens // BLOCK
     total = seq_size * blocks_dev
     first = own_index * blocks_dev
-    packed = jnp.concatenate([key_rows, value_rows], axis=1)
-    source = lax.all_gather(packed, "seq", axis=0, tiled=True).reshape(total, BLOCK, 2 * width)
     block_ids = first + jnp.arange(blocks_dev, dtype=jnp.int32)
     own_device = lax.dynamic_slice_in_dim(random_device, first, blocks_dev, 0)
     own_block = lax.dynamic_slice_in_dim(random_block, first, blocks_dev, 0)
@@ -405,25 +404,35 @@
         [jnp.clip(block_ids - 1, 0, total - 1), block_ids, jnp.clip(block_ids + 1, 0, total - 1)],
         axis=1,
     )
-    ids = jnp.concatenate([window, chosen], axis=1)
+    ids = jnp.concatenate([window, chosen], axis=1).reshape(-1)
     always = jnp.ones_like(block_ids, dtype=jnp.bool_)
     valid = jnp.stack([block_ids > 0, always, block_ids < total - 1] + [always] * RAND, axis=1)
-    own_sum, spread, query_out = block_attention(
-        ids.reshape(-1),
-        valid.astype(jnp.int32).reshape(-1),
-        first.reshape(1).astype(jnp.int32),
-        queries,
-        out_grad,
-        source,
-    )
-    returned = lax.psum_scatter(
-        spread.reshape(total * BLOCK, 2 * width), "seq", scatter_dimension=0, tiled=True
-    )
-    summed = own_sum.reshape(tokens, 2 * width) + returned.astype(jnp.float32)
+    valid = valid.astype(jnp.int32).reshape(-1)
+    first_table = first.reshape(1).astype(jnp.int32)
+    chunks = 2 if (width // DH) % 2 == 0 else 1
+    part = width // chunks
+    sources = []
+    for chunk in range(chunks):
+        cols = slice(chunk * part, (chunk + 1) * part)
+        packed = jnp.concatenate([key_rows[:, cols], value_rows[:, cols]], axis=1)
+        gathered = lax.all_gather(packed, "seq", axis=0, tiled=True)
+        sources.append(gathered.reshape(total, BLOCK, 2 * part))
+    query_parts, key_parts, value_parts = [], [], []
+    for chunk in range(chunks):
+        own_sum, spread, query_out = block_attention(
+            ids, valid, first_table, queries, out_grad, sources[chunk], chunk, part
+        )
+        returned = lax.psum_scatter(
+            spread.reshape(total * BLOCK, 2 * part), "seq", scatter_dimension=0, tiled=True
+        )
+        summed = own_sum.reshape(tokens, 2 * part) + returned.astype(jnp.float32)
+        query_parts.append(query_out)
+        key_parts.append(summed[:, :part].astype(jnp.bfloat16))
+        value_parts.append(summed[:, part:].astype(jnp.bfloat16))
     return (
-        query_out,
-        summed[:, :width].astype(jnp.bfloat16),
-        summed[:, width:].astype(jnp.bfloat16),
+        jnp.concatenate(query_parts, axis=1),
+        jnp.concatenate(key_parts, axis=1),
+        jnp.concatenate(value_parts, axis=1),
     )
 
 

time: 313 us -> 292 us (0.933)
  waiting for transfers between devices: 241 us -> 211 us
  Pallas kernels: 47.6 us -> 52.4 us
    reduce_scatter x1 -> x2, waiting for transfers between devices: 120 us -> 104 us  [gathered_shards(): lax.psum_scatter(spread.reshape(total * BLOCK, 2 * part), 'seq', scatter_...]
    all_gather x1 -> x2, waiting for transfers between devices: 121 us -> 107 us  [gathered_shards(): gathered = lax.all_gather(packed, 'seq', axis=0, tiled=True)]
    pallas_call x1 -> x2, Pallas kernels: 47.6 us -> 52.4 us  [block_attention(): pl.pallas_call(block_kernel, grid_spec=grid_spec, out_shape=[jax.ShapeDty...]
  transfers between devices with their start and end apart: 2 -> 4, of which waited for: 2 -> 4; matrix products, arithmetic and copies ran while one was open for 1% -> 2% of each run, Pallas kernels for 0% -> 18%
where the time goes in v3:
time: 292 us; the launch traced here: 290 us
  waiting for transfers between devices  211 us (72%)
  Pallas kernels  52.4 us (18%)
  between operations  13.9 us (5%)
  other arithmetic  8.1 us (3%)
  local copies, waits for them, and re-layouts  4.55 us (2%)
    all_gather x2, waiting for transfers between devices, gathered_shards(): gathered = lax.all_gather(packed, 'seq', axis=0, tiled=True)  107 us
    reduce_scatter x2, waiting for transfers between devices, gathered_shards(): lax.psum_scatter(spread.reshape(total * BLOCK, 2 * part), 'seq', scatter_...  104 us
    pallas_call x2, Pallas kernels, block_attention(): pl.pallas_call(block_kernel, grid_spec=grid_spec, out_shape=[jax.ShapeDty...  52.4 us
  transfers between devices with their start and end apart: 4, of which 4 were waited for; matrix products, arithmetic and copies ran while one was open for 2% of the time, Pallas kernels for 18%

profile of v3, /device:TPU:22, one launch (start us, length us, event | category | flops | bytes accessed | tf_op | source)
XLA Modules:
  0.0 290.0 jit_solution(5351073577882398843)
XLA Ops:
  7.2 1.5 fusion.4
  8.8 1.0 pad_maximum_fusion
  9.8 1.0 pad_maximum_fusion.1
  10.9 0.1 dynamic-slice_add_fusion
  11.0 0.1 copy.12
  11.1 0.6 reshape.63.ids_ref
  11.7 0.1 copy.13
  11.8 0.1 copy.14
  11.9 0.1 pad.13.clone
  12.1 0.1 add_convert_fusion
  12.2 0.7 reshape.71.valid_ref
  12.9 64.8 %all-gather.3.cloned.1.call-done = bf16[3328,512]{1,0:T(8,128)(2,1)} async-done(((bf16[832,512]{1,0:T(8,128)(2,1)}), bf16[3328,512]{1,0:T(8,128)(2,1)}) %all-gather.3.cloned.1.call-update) | async-done | bytes 3407888 | tf_op jit(solution)/shard_map/all_gather | solution.py:418
  77.6 26.2 %shard_map.85 = (f32[13,64,512]{2,1,0:T(8,128)}, bf16[52,64,512]{2,1,0:T(8,128)(2,1)}, bf16[832,256]{1,0:T(8,128)(2,1)}) custom-call(s32[65]{0:T(128)} %reshape.63.ids_ref, s32[65]{0:T(128)} %reshape.71.valid_ref, s32[1]{0:T(128)} %bitcast.first_ref, bf16[832,512]{1,0:T(8,128)(2,1)} %q_ref.3, bf16[832,512]{1,0:T(8,128)(2,1)} %g_ref.3, ...), custom_call_target="tpu_custom_call" | custom-call | tf_op jit(solution)/shard_map/pallas_call | solution.py:380
  103.9 42.5 %all-gather.5.cloned.1.call-done = bf16[3328,512]{1,0:T(8,128)(2,1)} async-done(((bf16[832,512]{1,0:T(8,128)(2,1)}), bf16[3328,512]{1,0:T(8,128)(2,1)}) %all-gather.5.cloned.1.call-update) | async-done | bytes 3407888 | tf_op jit(solution)/shard_map/all_gather | solution.py:418
  146.4 26.3 %shard_map.86 = (f32[13,64,512]{2,1,0:T(8,128)}, bf16[52,64,512]{2,1,0:T(8,128)(2,1)}, bf16[832,256]{1,0:T(8,128)(2,1)}) custom-call(s32[65]{0:T(128)} %reshape.63.ids_ref, s32[65]{0:T(128)} %reshape.71.valid_ref, s32[1]{0:T(128)} %bitcast.first_ref, bf16[832,512]{1,0:T(8,128)(2,1)} %q_ref.3, bf16[832,512]{1,0:T(8,128)(2,1)} %g_ref.3, ...), custom_call_target="tpu_custom_call" | custom-call | tf_op jit(solution)/shard_map/pallas_call | solution.py:380
  172.7 1.0 copy-done.2
  173.6 0.1 copy-done.3
  173.8 1.0 pad_maximum_fusion.2
  174.7 38.5 %reduce-scatter.3.cloned.1.call-done = bf16[832,512]{1,0:T(8,128)(2,1)} async-done(((bf16[3328,512]{1,0:T(8,128)(2,1)}), bf16[832,512]{1,0:T(8,128)(2,1)}) %reduce-scatter.3.cloned.1.call-update) | async-done | bytes 851984 | tf_op jit(solution)/shard_map/reduce_scatter | solution.py:425
  213.2 1.5 fusion.1
  214.8 65.1 %reduce-scatter.5.cloned.1.call-done = bf16[832,512]{1,0:T(8,128)(2,1)} async-done(((bf16[3328,512]{1,0:T(8,128)(2,1)}), bf16[832,512]{1,0:T(8,128)(2,1)}) %reduce-scatter.5.cloned.1.call-update) | async-done | bytes 851984 | tf_op jit(solution)/shard_map/reduce_scatter | solution.py:425
  279.9 1.5 fusion
  281.5 1.0 pad_maximum_fusion.4
  282.5 1.0 pad_maximum_fusion.3
  (26 shorter events, 0.5 us)
Async XLA Ops:
  7.2 70.5 %all-gather.3.cloned.1.call-start = ((), (), s32[]{:S(2)}) async-start(), calls=%async_computation.2 | async-start | bytes 4259840 | tf_op jit(solution)/shard_map/all_gather | solution.py:418
  9.7 1.2 copy-start.4
  9.7 1.2 copy-start.5
  9.7 136.6 %all-gather.5.cloned.1.call-start = ((), (), s32[]{:S(2)}) async-start(), calls=%async_computation.3 | async-start | bytes 4259840 | tf_op jit(solution)/shard_map/all_gather | solution.py:418
  10.8 202.4 %reduce-scatter.3.cloned.1.call-start = ((), (), s32[]{:S(2)}) async-start(), calls=%async_computation.4 | async-start | bytes 4259840 | tf_op jit(solution)/shard_map/reduce_scatter | solution.py:425
  103.8 176.1 %reduce-scatter.5.cloned.1.call-start = ((), (), s32[]{:S(2)}) async-start(), calls=%async_computation.5 | async-start | bytes 4259840 | tf_op jit(solution)/shard_map/reduce_scatter | solution.py:425
  172.6 1.0 copy-start.2
  172.6 1.1 copy-start.3
  172.7 40.6 %copy-start = (f32[13,64,512]{2,1,0:T(8,128)S(1)}, f32[13,64,512]{2,1,0:T(8,128)}, u32[]{:S(2)}) copy-start(f32[13,64,512]{2,1,0:T(8,128)} %get-tuple-element.11) | copy-start | bytes 5111812
  214.8 65.2 %copy-start.1 = (f32[13,64,512]{2,1,0:T(8,128)S(1)}, f32[13,64,512]{2,1,0:T(8,128)}, u32[]{:S(2)}) copy-start(f32[13,64,512]{2,1,0:T(8,128)} %get-tuple-element.13) | copy-start | bytes 5111812
Sparse Core Ops, SparseCore 0:
  10.1 67.4 all-gather.2
  79.8 66.5 all-gather.4
  148.7 64.5 reduce-scatter.2
  215.4 64.5 reduce-scatter.4

commit v4 on v3

--- a/solution.py
+++ b/solution.py
@@ -283,7 +283,7 @@
 SLOTS = 3 + RAND
 
 
-def block_kernel(ids_ref, valid_ref, first_ref, q_ref, g_ref, *rest):
+def block_kernel(ids_ref, write_ref, valid_ref, first_ref, q_ref, g_ref, *rest):
     kv_refs = rest[:SLOTS]
     own_ref, spread_ref, dq_ref, acc_ref = rest[SLOTS:]
     step = pl.program_id(0)
@@ -340,7 +340,7 @@
         piece = terms[slot * BLOCK : (slot + 1) * BLOCK]
         if slot >= 3:
             piece = piece.astype(jnp.bfloat16).astype(jnp.float32)
-        target = ids_ref[step * SLOTS + slot]
+        target = write_ref[step * SLOTS + slot]
         acc_ref[target] = acc_ref[target] + piece
 
     @pl.when(step == steps - 1)
@@ -352,27 +352,26 @@
             spread_ref[first + block] = jnp.zeros(spread_ref.shape[1:], jnp.bfloat16)
 
 
-def block_attention(ids, valid, first, queries, out_grad, source, chunk, width):
+def block_attention(ids, write_ids, valid, first, queries, out_grad, source, chunk, width, total):
     tokens = queries.shape[0]
     blocks_dev = tokens // BLOCK
-    total = source.shape[0]
 
     def context_spec(slot):
         return pl.BlockSpec(
-            (1, BLOCK, 2 * width), lambda i, ids, valid, first: (ids[i * SLOTS + slot], 0, 0)
-        )
-
-    column_spec = pl.BlockSpec((BLOCK, width), lambda i, ids, valid, first: (i, chunk))
-    row_spec = pl.BlockSpec((BLOCK, width), lambda i, ids, valid, first: (i, 0))
+            (1, BLOCK, 2 * width), lambda i, ids, write_ids, valid, first: (ids[i * SLOTS + slot], 0, 0)
+        )
+
+    column_spec = pl.BlockSpec((BLOCK, width), lambda i, ids, write_ids, valid, first: (i, chunk))
+    row_spec = pl.BlockSpec((BLOCK, width), lambda i, ids, write_ids, valid, first: (i, 0))
     grid_spec = pltpu.PrefetchScalarGridSpec(
-        num_scalar_prefetch=3,
+        num_scalar_prefetch=4,
         grid=(blocks_dev,),
         in_specs=[column_spec, column_spec] + [context_spec(s) for s in range(SLOTS)],
         out_specs=[
             pl.BlockSpec(
-                (blocks_dev, BLOCK, 2 * width), lambda i, ids, valid, first: (0, 0, 0)
+                (blocks_dev, BLOCK, 2 * width), lambda i, ids, write_ids, valid, first: (0, 0, 0)
             ),
-            pl.BlockSpec((total, BLOCK, 2 * width), lambda i, ids, valid, first: (0, 0, 0)),
+            pl.BlockSpec((total, BLOCK, 2 * width), lambda i, ids, write_ids, valid, first: (0, 0, 0)),
             row_spec,
         ],
         scratch_shapes=[pltpu.VMEM((total, BLOCK, 2 * width), jnp.float32)],
@@ -386,7 +385,7 @@
             jax.ShapeDtypeStruct((tokens, width), jnp.bfloat16),
         ],
         compiler_params=pltpu.CompilerParams(vmem_limit_bytes=60 * 1024 * 1024),
-    )(ids, valid, first, queries, out_grad, *([source] * SLOTS))
+    )(ids, write_ids, valid, first, queries, out_grad, *([source] * SLOTS))
 
 
 def gathered_shards(queries, key_rows, value_rows, out_grad, random_device, random_block):
@@ -396,7 +395,12 @@
     blocks_dev = tokens // BLOCK
     total = seq_size * blocks_dev
     first = own_index * blocks_dev
+    capacity = max(2, 3 * blocks_dev // seq_size)
+    selector, slot_index = routing(
+        random_device, random_block, own_index, seq_size, blocks_dev, capacity
+    )
     block_ids = first + jnp.arange(blocks_dev, dtype=jnp.int32)
+    local_ids = jnp.arange(blocks_dev, dtype=jnp.int32)
     own_device = lax.dynamic_slice_in_dim(random_device, first, blocks_dev, 0)
     own_block = lax.dynamic_slice_in_dim(random_block, first, blocks_dev, 0)
     chosen = (own_device * blocks_dev + own_block).astype(jnp.int32)
@@ -404,7 +408,10 @@
         [jnp.clip(block_ids - 1, 0, total - 1), block_ids, jnp.clip(block_ids + 1, 0, total - 1)],
         axis=1,
     )
-    ids = jnp.concatenate([window, chosen], axis=1).reshape(-1)
+    write_ids = jnp.concatenate([window, chosen], axis=1).reshape(-1)
+    read_window = jnp.stack([local_ids, local_ids + 1, local_ids + 2], axis=1)
+    read_far = (slot_index + blocks_dev + 2).reshape(blocks_dev, RAND).astype(jnp.int32)
+    read_ids = jnp.concatenate([read_window, read_far], axis=1).reshape(-1)
     always = jnp.ones_like(block_ids, dtype=jnp.bool_)
     valid = jnp.stack([block_ids > 0, always, block_ids < total - 1] + [always] * RAND, axis=1)
     valid = valid.astype(jnp.int32).reshape(-1)
@@ -412,15 +419,27 @@
     chunks = 2 if (width // DH) % 2 == 0 else 1
     part = width // chunks
     sources = []
+    previous = None
     for chunk in range(chunks):
         cols = slice(chunk * part, (chunk + 1) * part)
         packed = jnp.concatenate([key_rows[:, cols], value_rows[:, cols]], axis=1)
-        gathered = lax.all_gather(packed, "seq", axis=0, tiled=True)
-        sources.append(gathered.reshape(total, BLOCK, 2 * part))
+        packed = packed.reshape(blocks_dev, BLOCK, 2 * part)
+        if previous is not None:
+            packed, _ = lax.optimization_barrier((packed, previous))
+        outgoing = jnp.dot(
+            selector, packed.reshape(blocks_dev, BLOCK * 2 * part),
+            preferred_element_type=jnp.float32,
+        ).astype(jnp.bfloat16)
+        outgoing = outgoing.reshape(seq_size * capacity, BLOCK, 2 * part)
+        haloed = extended(packed, (("seq", 0),), 1)
+        arrived = lax.all_to_all(outgoing, "seq", split_axis=0, concat_axis=0, tiled=True)
+        previous = arrived
+        sources.append(jnp.concatenate([haloed, arrived], axis=0))
     query_parts, key_parts, value_parts = [], [], []
     for chunk in range(chunks):
         own_sum, spread, query_out = block_attention(
-            ids, valid, first_table, queries, out_grad, sources[chunk], chunk, part
+            read_ids, write_ids, valid, first_table, queries, out_grad, sources[chunk],
+            chunk, part, total,
         )
         returned = lax.psum_scatter(
             spread.reshape(total * BLOCK, 2 * part), "seq", scatter_dimension=0, tiled=True

time: 292 us -> 323 us (1.11)
  starting transfers between devices: 0.16 us -> 22.4 us
  local copies, waits for them, and re-layouts: 4.55 us -> 16.7 us
  waiting for transfers between devices: 211 us -> 199 us
  other arithmetic: 8.1 us -> 13.8 us
    ppermute x0 -> x4, waiting for transfers between devices: none -> 138 us  [the longest x2 138 us: extended(): lax.ppermute(lax.slice_in_dim(block, block.shape[dim] - width, None, axis...]
    all_gather x2 -> x0, waiting for transfers between devices: 107 us -> none  [gathered_shards(): gathered = lax.all_gather(packed, 'seq', axis=0, tiled=True)]
    reduce_scatter x2, waiting for transfers between devices: 104 us -> 60.9 us  [gathered_shards(): lax.psum_scatter(spread.reshape(total * BLOCK, 2 * part), 'seq', scatter_...]
    ppermute x0 -> x4, starting transfers between devices: none -> 11.9 us  [the longest x2 6.75 us: extended(): lax.ppermute(lax.slice_in_dim(block, block.shape[dim] - width, None, axis...]
    all_to_all x0 -> x2, starting transfers between devices: none -> 10.6 us  [gathered_shards(): lax.all_to_all(outgoing, 'seq', split_axis=0, concat_axis=0, tiled=True)]
    unnamed x12 -> x26, local copies, waits for them, and re-layouts: 1.11 us -> 7.14 us
    concatenate x1 -> x4, other arithmetic: 0.01 us -> 4.09 us  [the longest x2 3.94 us: gathered_shards(): sources.append(jnp.concatenate([haloed, arrived], axis=0))]
    reshape x1 -> x4, local copies, waits for them, and re-layouts: 0.63 us -> 4.48 us  [the longest x2 3.16 us: gathered_shards(): outgoing = outgoing.reshape(seq_size * capacity, BLOCK, 2 * part)]
  transfers between devices with their start and end apart: 4 -> 8, of which waited for: 4 -> 3; matrix products, arithmetic and copies ran while one was open for 2% -> 5% of each run, Pallas kernels for 18% -> 8%
where the time goes in v4:
time: 323 us; the launch traced here: 320 us
  waiting for transfers between devices  199 us (62%)
  Pallas kernels  52.4 us (16%)
  starting transfers between devices  22.4 us (7%)
  local copies, waits for them, and re-layouts  16.7 us (5%)
  between operations  14.2 us (4%)
  other arithmetic  13.8 us (4%)
    ppermute x2, waiting for transfers between devices, extended(): lax.ppermute(lax.slice_in_dim(block, block.shape[dim] - width, None, axis...  138 us
    reduce_scatter x2, waiting for transfers between devices, gathered_shards(): lax.psum_scatter(spread.reshape(total * BLOCK, 2 * part), 'seq', scatter_...  60.9 us
    pallas_call x2, Pallas kernels, block_attention(): pl.pallas_call(block_kernel, grid_spec=grid_spec, out_shape=[jax.ShapeDty...  52.4 us
    all_to_all x2, starting transfers between devices, gathered_shards(): lax.all_to_all(outgoing, 'seq', split_axis=0, concat_axis=0, tiled=True)  10.6 us
    unnamed x26, local copies, waits for them, and re-layouts  7.14 us
    ppermute x2, starting transfers between devices, extended(): lax.ppermute(lax.slice_in_dim(block, block.shape[dim] - width, None, axis...  6.75 us
  transfers between devices with their start and end apart: 8, of which 3 were waited for; matrix products, arithmetic and copies ran while one was open for 5% of the time, Pallas kernels for 8%

profile of v4, /device:TPU:22, one launch (start us, length us, event | category | flops | bytes accessed | tf_op | source)
XLA Modules:
  0.0 320.5 jit_solution(9295167622440904192)
XLA Ops:
  9.3 2.4 fusion.19
  14.1 1.0 copy.20
  15.1 1.6 slice.68
  16.7 5.3 %all-to-all-start = ((bf16[36,64,512]{2,1,0:T(8,128)(2,1)}), bf16[36,64,512]{2,1,0:T(8,128)(2,1)S(1)}, u32[]{:S(2)}, u32[]{:S(2)}) async-start(bf16[36,64,512]{2,1,0:T(8,128)(2,1)} %slice.68), calls=%async_computation | async-start | bytes 4718592 | tf_op jit(solution)/shard_map/all_to_all | solution.py:435
  22.8 3.4 %collective-permute-start = (bf16[1,64,512]{2,1,0:T(8,128)(2,1)S(1)}, bf16[1,64,512]{2,1,0:T(8,128)(2,1)S(1)}, u32[]{:S(2)}, u32[]{:S(2)}) collective-permute-start(bf16[1,64,512]{2,1,0:T(8,128)(2,1)S(1)} %get-tuple-element.21), channel_id=1, source_target_pairs={{0,4},{4,8},{8,12},{1,5},{5,9},{9,13},{2,6},{6,10},{10,14},{3,7},{... | collective-permute-start | bytes 196616 | tf_op jit(solution)/shard_map/ppermute | solution.py:20
  26.2 2.5 collective-permute-start.1
  34.2 40.6 %collective-permute-done = bf16[1,64,512]{2,1,0:T(8,128)(2,1)S(1)} collective-permute-done((bf16[1,64,512]{2,1,0:T(8,128)(2,1)S(1)}, bf16[1,64,512]{2,1,0:T(8,128)(2,1)S(1)}, u32[]{:S(2)}, u32[]{:S(2)}) %collective-permute-start) | collective-permute-done | bytes 65568 | tf_op jit(solution)/shard_map/ppermute | solution.py:20
  74.9 2.0 pad_maximum_fusion.rest_0_.rest_1_.rest_2_.rest_3_.rest_4_
  76.9 26.2 %shard_map.85 = (f32[13,64,512]{2,1,0:T(8,128)}, bf16[52,64,512]{2,1,0:T(8,128)(2,1)}, bf16[832,256]{1,0:T(8,128)(2,1)}) custom-call(s32[65]{0:T(128)} %reshape.125.ids_ref, s32[65]{0:T(128)} %reshape.126.write_ref, s32[65]{0:T(128)} %reshape.137.valid_ref, s32[1]{0:T(128)} %bitcast.first_ref, bf16[832,512]{1,0:T(8,128)(2,1)} %q_ref.3, ...), custom_call_target="tpu_custom_call" | custom-call | tf_op jit(solution)/shard_map/pallas_call | solution.py:379
  103.1 1.0 copy-done.4
  105.8 1.0 copy.22
  106.7 1.6 slice.69
  108.3 5.2 %all-to-all-start.1 = ((bf16[36,64,512]{2,1,0:T(8,128)(2,1)}), bf16[36,64,512]{2,1,0:T(8,128)(2,1)S(1)}, u32[]{:S(2)}, u32[]{:S(2)}) async-start(bf16[36,64,512]{2,1,0:T(8,128)(2,1)} %slice.69), calls=%async_computation.1 | async-start | bytes 4718592 | tf_op jit(solution)/shard_map/all_to_all | solution.py:435
  113.6 3.4 %collective-permute-start.2 = (bf16[1,64,512]{2,1,0:T(8,128)(2,1)S(1)}, bf16[1,64,512]{2,1,0:T(8,128)(2,1)S(1)}, u32[]{:S(2)}, u32[]{:S(2)}) collective-permute-start(bf16[1,64,512]{2,1,0:T(8,128)(2,1)S(1)} %get-tuple-element.23), channel_id=1, source_target_pairs={{0,4},{4,8},{8,12},{1,5},{5,9},{9,13},{2,6},{6,10},{10,14},{3,7},{... | collective-permute-start | bytes 196616 | tf_op jit(solution)/shard_map/ppermute | solution.py:20
  117.0 2.6 collective-permute-start.3
  119.6 97.5 %collective-permute-done.2 = bf16[1,64,512]{2,1,0:T(8,128)(2,1)S(1)} collective-permute-done((bf16[1,64,512]{2,1,0:T(8,128)(2,1)S(1)}, bf16[1,64,512]{2,1,0:T(8,128)(2,1)S(1)}, u32[]{:S(2)}, u32[]{:S(2)}) %collective-permute-start.2) | collective-permute-done | bytes 65568 | tf_op jit(solution)/shard_map/ppermute | solution.py:20
  217.2 2.0 pad_maximum_fusion.1.rest_0_.rest_1_.rest_2_.rest_3_.rest_4_
  219.1 26.2 %shard_map.86 = (f32[13,64,512]{2,1,0:T(8,128)}, bf16[52,64,512]{2,1,0:T(8,128)(2,1)}, bf16[832,256]{1,0:T(8,128)(2,1)}) custom-call(s32[65]{0:T(128)} %reshape.125.ids_ref, s32[65]{0:T(128)} %reshape.126.write_ref, s32[65]{0:T(128)} %reshape.137.valid_ref, s32[1]{0:T(128)} %bitcast.first_ref, bf16[832,512]{1,0:T(8,128)(2,1)} %q_ref.3, ...), custom_call_target="tpu_custom_call" | custom-call | tf_op jit(solution)/shard_map/pallas_call | solution.py:379
  246.5 1.0 pad_maximum_fusion.4
  247.5 1.6 fusion.1
  249.2 60.9 %reduce-scatter.5.cloned.1.call-done = bf16[832,512]{1,0:T(8,128)(2,1)} async-done(((bf16[3328,512]{1,0:T(8,128)(2,1)}), bf16[832,512]{1,0:T(8,128)(2,1)}) %reduce-scatter.5.cloned.1.call-update) | async-done | bytes 851984 | tf_op jit(solution)/shard_map/reduce_scatter | solution.py:444
  310.1 1.5 fusion
  311.7 1.0 pad_maximum_fusion.6
  312.7 1.0 pad_maximum_fusion.5
  (70 shorter events, 13.7 us)
Async XLA Ops:
  11.7 0.8 copy-start
  11.7 0.9 copy-start.1
  16.7 12.0 %copy-start.9 = (s32[52,2]{0,1:T(2,128)S(1)}, s32[52,2]{0,1:T(2,128)}, u32[]{:S(2)}) copy-start(s32[52,2]{0,1:T(2,128)} %param.10) | copy-start | bytes 1252
  16.7 58.2 %all-to-all-start = ((bf16[36,64,512]{2,1,0:T(8,128)(2,1)}), bf16[36,64,512]{2,1,0:T(8,128)(2,1)S(1)}, u32[]{:S(2)}, u32[]{:S(2)}) async-start(bf16[36,64,512]{2,1,0:T(8,128)(2,1)} %slice.68), calls=%async_computation | async-start | bytes 4718592 | tf_op jit(solution)/shard_map/all_to_all | solution.py:435
  22.0 225.4 %reduce-scatter.3.cloned.1.call-start = ((), (), s32[]{:S(2)}) async-start(), calls=%async_computation.4 | async-start | bytes 4259840 | tf_op jit(solution)/shard_map/reduce_scatter | solution.py:444
  22.8 52.0 %collective-permute-start = (bf16[1,64,512]{2,1,0:T(8,128)(2,1)S(1)}, bf16[1,64,512]{2,1,0:T(8,128)(2,1)S(1)}, u32[]{:S(2)}, u32[]{:S(2)}) collective-permute-start(bf16[1,64,512]{2,1,0:T(8,128)(2,1)S(1)} %get-tuple-element.21), channel_id=1, source_target_pairs={{0,4},{4,8},{8,12},{1,5},{5,9},{9,13},{2,6},{6,10},{10,14},{3,7},{... | collective-permute-start | bytes 196616 | tf_op jit(solution)/shard_map/ppermute | solution.py:20
  26.2 48.7 %collective-permute-start.1 = (bf16[1,64,512]{2,1,0:T(8,128)(2,1)S(1)}, bf16[1,64,512]{2,1,0:T(8,128)(2,1)S(1)}, u32[]{:S(2)}, u32[]{:S(2)}) collective-permute-start(bf16[1,64,512]{2,1,0:T(8,128)(2,1)S(1)} %get-tuple-element.22), channel_id=1, source_target_pairs={{4,0},{8,4},{12,8},{5,1},{9,5},{13,9},{6,2},{10,6},{14,10},{7,3},{... | collective-permute-start | bytes 196616 | tf_op jit(solution)/shard_map/ppermute | solution.py:23
  29.0 0.5 copy-start.8
  103.0 1.0 copy-start.4
  103.0 1.1 copy-start.5
  108.3 108.8 %all-to-all-start.1 = ((bf16[36,64,512]{2,1,0:T(8,128)(2,1)}), bf16[36,64,512]{2,1,0:T(8,128)(2,1)S(1)}, u32[]{:S(2)}, u32[]{:S(2)}) async-start(bf16[36,64,512]{2,1,0:T(8,128)(2,1)} %slice.69), calls=%async_computation.1 | async-start | bytes 4718592 | tf_op jit(solution)/shard_map/all_to_all | solution.py:435
  113.6 196.5 %reduce-scatter.5.cloned.1.call-start = ((), (), s32[]{:S(2)}) async-start(), calls=%async_computation.5 | async-start | bytes 4259840 | tf_op jit(solution)/shard_map/reduce_scatter | solution.py:444
  113.6 103.6 %collective-permute-start.2 = (bf16[1,64,512]{2,1,0:T(8,128)(2,1)S(1)}, bf16[1,64,512]{2,1,0:T(8,128)(2,1)S(1)}, u32[]{:S(2)}, u32[]{:S(2)}) collective-permute-start(bf16[1,64,512]{2,1,0:T(8,128)(2,1)S(1)} %get-tuple-element.23), channel_id=1, source_target_pairs={{0,4},{4,8},{8,12},{1,5},{5,9},{9,13},{2,6},{6,10},{10,14},{3,7},{... | collective-permute-start | bytes 196616 | tf_op jit(solution)/shard_map/ppermute | solution.py:20
  117.0 100.2 %collective-permute-start.3 = (bf16[1,64,512]{2,1,0:T(8,128)(2,1)S(1)}, bf16[1,64,512]{2,1,0:T(8,128)(2,1)S(1)}, u32[]{:S(2)}, u32[]{:S(2)}) collective-permute-start(bf16[1,64,512]{2,1,0:T(8,128)(2,1)S(1)} %get-tuple-element.24), channel_id=1, source_target_pairs={{4,0},{8,4},{12,8},{5,1},{9,5},{13,9},{6,2},{10,6},{14,10},{7,3},{... | collective-permute-start | bytes 196616 | tf_op jit(solution)/shard_map/ppermute | solution.py:23
  245.4 1.0 copy-start.6
  245.4 1.1 copy-start.7
  245.4 2.1 copy-start.2
  247.5 62.6 %copy-start.3 = (f32[13,64,512]{2,1,0:T(8,128)S(1)}, f32[13,64,512]{2,1,0:T(8,128)}, u32[]{:S(2)}) copy-start(f32[13,64,512]{2,1,0:T(8,128)} %get-tuple-element.15) | copy-start | bytes 5111812
Sparse Core Ops, SparseCore 0:
  103.2 114.3 reduce-scatter.2
  245.5 64.5 reduce-scatter.4

commit v5 on v3

--- a/solution.py
+++ b/solution.py
@@ -389,6 +389,24 @@
     )(ids, valid, first, queries, out_grad, *([source] * SLOTS))
 
 
+def ring_reduce(spread, own_index, seq_size):
+    parts = spread.reshape((seq_size, spread.shape[0] // seq_size) + spread.shape[1:])
+    from_left = jnp.zeros(parts.shape[1:], jnp.bfloat16)
+    from_right = jnp.zeros(parts.shape[1:], jnp.bfloat16)
+    for hop in range(1, seq_size):
+        owner = jnp.clip(seq_size + own_index - hop, 0, seq_size - 1)
+        piece = lax.dynamic_index_in_dim(parts, owner, 0, keepdims=False).astype(jnp.float32)
+        piece = (piece + from_left.astype(jnp.float32)).astype(jnp.bfloat16)
+        from_left = lax.ppermute(piece, "seq", [(i, i + 1) for i in range(hop)])
+        owner = jnp.clip(own_index + hop - seq_size, 0, seq_size - 1)
+        piece = lax.dynamic_index_in_dim(parts, owner, 0, keepdims=False).astype(jnp.float32)
+        piece = (piece + from_right.astype(jnp.float32)).astype(jnp.bfloat16)
+        from_right = lax.ppermute(
+            piece, "seq", [(i, i - 1) for i in range(seq_size - hop, seq_size)]
+        )
+    return from_left.astype(jnp.float32) + from_right.astype(jnp.float32)
+
+
 def gathered_shards(queries, key_rows, value_rows, out_grad, random_device, random_block):
     seq_size = lax.axis_size("seq")
     own_index = lax.axis_index("seq")
@@ -418,14 +436,21 @@
         gathered = lax.all_gather(packed, "seq", axis=0, tiled=True)
         sources.append(gathered.reshape(total, BLOCK, 2 * part))
     query_parts, key_parts, value_parts = [], [], []
+    returned = None
     for chunk in range(chunks):
+        table = first_table
+        if returned is not None:
+            table = table + (returned[0, :1] * 0.0).astype(jnp.int32)
         own_sum, spread, query_out = block_attention(
-            ids, valid, first_table, queries, out_grad, sources[chunk], chunk, part
-        )
-        returned = lax.psum_scatter(
-            spread.reshape(total * BLOCK, 2 * part), "seq", scatter_dimension=0, tiled=True
-        )
-        summed = own_sum.reshape(tokens, 2 * part) + returned.astype(jnp.float32)
+            ids, valid, table, queries, out_grad, sources[chunk], chunk, part
+        )
+        if chunk == 0 and chunks > 1:
+            returned = ring_reduce(spread, own_index, seq_size).reshape(tokens, 2 * part)
+        else:
+            returned = lax.psum_scatter(
+                spread.reshape(total * BLOCK, 2 * part), "seq", scatter_dimension=0, tiled=True
+            ).astype(jnp.float32)
+        summed = own_sum.reshape(tokens, 2 * part) + returned
         query_parts.append(query_out)
         key_parts.append(summed[:, :part].astype(jnp.bfloat16))
         value_parts.append(summed[:, part:].astype(jnp.bfloat16))

time: 292 us -> 333 us (1.14)
  starting transfers between devices: 0.16 us -> 18.3 us
  waiting for transfers between devices: 211 us -> 224 us
  other arithmetic: 8.1 us -> 14 us
  local copies, waits for them, and re-layouts: 4.55 us -> 7.96 us
    ppermute x0 -> x6, waiting for transfers between devices: none -> 95.9 us  [the longest x3 70.2 us: ring_reduce(): lax.ppermute(piece, 'seq', [(i, i - 1) for i in range(seq_size - hop, seq...]
    all_gather x2, waiting for transfers between devices: 107 us -> 64.8 us  [gathered_shards(): gathered = lax.all_gather(packed, 'seq', axis=0, tiled=True)]
    reduce_scatter x2 -> x1, waiting for transfers between devices: 104 us -> 63.3 us  [gathered_shards(): lax.psum_scatter(spread.reshape(total * BLOCK, 2 * part), 'seq', scatter_...]
    ppermute x0 -> x6, starting transfers between devices: none -> 18.2 us  [the longest x3 13.4 us: ring_reduce(): lax.ppermute(piece, 'seq', [(i, i - 1) for i in range(seq_size - hop, seq...]
    convert_element_type x0 -> x3, other arithmetic: none -> 6.87 us  [the longest x2 5.48 us: ring_reduce(): piece = (piece + from_left.astype(jnp.float32)).astype(jnp.bfloat16)]
  transfers between devices with their start and end apart: 4 -> 9, of which waited for: 4 -> 6; matrix products, arithmetic and copies ran while one was open for 2% -> 4% of each run, Pallas kernels for 18% -> 8%
where the time goes in v5:
time: 333 us; the launch traced here: 331 us
  waiting for transfers between devices  224 us (67%)
  Pallas kernels  52.5 us (16%)
  starting transfers between devices  18.3 us (5%)
  between operations  14.6 us (4%)
  other arithmetic  14 us (4%)
  local copies, waits for them, and re-layouts  7.96 us (2%)
    ppermute x3, waiting for transfers between devices, ring_reduce(): lax.ppermute(piece, 'seq', [(i, i - 1) for i in range(seq_size - hop, seq...  70.2 us
    all_gather x2, waiting for transfers between devices, gathered_shards(): gathered = lax.all_gather(packed, 'seq', axis=0, tiled=True)  64.8 us
    reduce_scatter x1, waiting for transfers between devices, gathered_shards(): lax.psum_scatter(spread.reshape(total * BLOCK, 2 * part), 'seq', scatter_...  63.3 us
    pallas_call x2, Pallas kernels, block_attention(): pl.pallas_call(block_kernel, grid_spec=grid_spec, out_shape=[jax.ShapeDty...  52.5 us
    ppermute x3, waiting for transfers between devices, ring_reduce(): from_left = lax.ppermute(piece, 'seq', [(i, i + 1) for i in range(hop)])  25.7 us
    ppermute x3, starting transfers between devices, ring_reduce(): lax.ppermute(piece, 'seq', [(i, i - 1) for i in range(seq_size - hop, seq...  13.4 us
  transfers between devices with their start and end apart: 9, of which 6 were waited for; matrix products, arithmetic and copies ran while one was open for 4% of the time, Pallas kernels for 8%

profile of v5, /device:TPU:22, one launch (start us, length us, event | category | flops | bytes accessed | tf_op | source)
XLA Modules:
  0.0 331.3 jit_solution(2741408916549941705)
XLA Ops:
  7.2 1.5 fusion.10
  8.7 1.0 pad_maximum_fusion
  9.8 1.0 pad_maximum_fusion.1
  12.8 64.8 %all-gather.3.cloned.1.call-done = bf16[3328,512]{1,0:T(8,128)(2,1)} async-done(((bf16[832,512]{1,0:T(8,128)(2,1)}), bf16[3328,512]{1,0:T(8,128)(2,1)}) %all-gather.3.cloned.1.call-update) | async-done | bytes 3407888 | tf_op jit(solution)/shard_map/all_gather | solution.py:436
  77.6 26.2 %shard_map.85 = (f32[13,64,512]{2,1,0:T(8,128)}, bf16[52,64,512]{2,1,0:T(8,128)(2,1)}, bf16[832,256]{1,0:T(8,128)(2,1)}) custom-call(s32[65]{0:T(128)} %reshape.77.ids_ref, s32[65]{0:T(128)} %reshape.86.valid_ref, s32[1]{0:T(128)} %bitcast.first_ref, bf16[832,512]{1,0:T(8,128)(2,1)} %q_ref.3, bf16[832,512]{1,0:T(8,128)(2,1)} %g_ref.3, ...), custom_call_target="tpu_custom_call" | custom-call | tf_op jit(solution)/shard_map/pallas_call | solution.py:380
  103.8 2.9 dynamic-slice_bitcast_fusion.1
  106.8 1.6 collective-permute-start
  108.3 1.3 collective-permute-start.3
  109.7 2.3 fusion.2
  112.0 1.3 collective-permute-start.1
  113.3 36.9 %collective-permute-done.3 = bf16[13,64,512]{2,1,0:T(8,128)(2,1)} collective-permute-done((bf16[13,64,512]{2,1,0:T(8,128)(2,1)}, bf16[13,64,512]{2,1,0:T(8,128)(2,1)}, u32[]{:S(2)}, u32[]{:S(2)}) %collective-permute-start.3) | collective-permute-done | bytes 852000 | tf_op jit(solution)/shard_map/ppermute | solution.py:404
  150.2 25.7 %collective-permute-done.1 = bf16[13,64,512]{2,1,0:T(8,128)(2,1)} collective-permute-done((bf16[13,64,512]{2,1,0:T(8,128)(2,1)}, bf16[13,64,512]{2,1,0:T(8,128)(2,1)}, u32[]{:S(2)}, u32[]{:S(2)}) %collective-permute-start.1) | collective-permute-done | bytes 852000 | tf_op jit(solution)/shard_map/ppermute | solution.py:400
  175.9 3.2 fusion.3
  179.1 7.7 %collective-permute-start.4 = (bf16[13,64,512]{2,1,0:T(8,128)(2,1)}, bf16[13,64,512]{2,1,0:T(8,128)(2,1)}, u32[]{:S(2)}, u32[]{:S(2)}) collective-permute-start(bf16[13,64,512]{2,1,0:T(8,128)(2,1)} %get-tuple-element.16), channel_id=1, source_target_pairs={{8,4},{12,8},{9,5},{13,9},{10,6},{14,10},{11,7},{15,11},{24,20},{2... | collective-permute-start | bytes 2555912 | tf_op jit(solution)/shard_map/ppermute | solution.py:404
  186.8 1.9 collective-permute-start.2
  188.8 16.3 %collective-permute-done.4 = bf16[13,64,512]{2,1,0:T(8,128)(2,1)} collective-permute-done((bf16[13,64,512]{2,1,0:T(8,128)(2,1)}, bf16[13,64,512]{2,1,0:T(8,128)(2,1)}, u32[]{:S(2)}, u32[]{:S(2)}) %collective-permute-start.4) | collective-permute-done | bytes 852000 | tf_op jit(solution)/shard_map/ppermute | solution.py:404
  205.0 1.4 fusion.1
  206.4 4.4 %collective-permute-start.5 = (bf16[13,64,512]{2,1,0:T(8,128)(2,1)S(1)}, bf16[13,64,512]{2,1,0:T(8,128)(2,1)S(1)}, u32[]{:S(2)}, u32[]{:S(2)}) collective-permute-start(bf16[13,64,512]{2,1,0:T(8,128)(2,1)S(1)} %fusion.1), channel_id=1, source_target_pairs={{4,0},{8,4},{12,8},{5,1},{9,5},{13,9},{6,2},{10,6},{14,10},{7,3},{... | collective-permute-start | bytes 2555912 | tf_op jit(solution)/shard_map/ppermute | solution.py:404
  210.8 17.0 %collective-permute-done.5 = bf16[13,64,512]{2,1,0:T(8,128)(2,1)S(1)} collective-permute-done((bf16[13,64,512]{2,1,0:T(8,128)(2,1)S(1)}, bf16[13,64,512]{2,1,0:T(8,128)(2,1)S(1)}, u32[]{:S(2)}, u32[]{:S(2)}) %collective-permute-start.5) | collective-permute-done | bytes 852000 | tf_op jit(solution)/shard_map/ppermute | solution.py:404
  229.3 26.2 %shard_map.86 = (f32[13,64,512]{2,1,0:T(8,128)}, bf16[52,64,512]{2,1,0:T(8,128)(2,1)}, bf16[832,256]{1,0:T(8,128)(2,1)}) custom-call(s32[65]{0:T(128)} %reshape.77.ids_ref, s32[65]{0:T(128)} %reshape.86.valid_ref, s32[1]{0:T(128)S(6)} %add.123.first_ref, bf16[832,512]{1,0:T(8,128)(2,1)} %q_ref.3, bf16[832,512]{1,0:T(8,128)(2,1)} %g_ref.3, ...), custom_call_target="tpu_custom_call" | custom-call | tf_op jit(solution)/shard_map/pallas_call | solution.py:380
  256.7 1.0 pad_maximum_fusion.2
  258.0 63.3 %reduce-scatter.2.cloned.1.call-done = bf16[832,512]{1,0:T(8,128)(2,1)} async-done(((bf16[3328,512]{1,0:T(8,128)(2,1)}), bf16[832,512]{1,0:T(8,128)(2,1)}) %reduce-scatter.2.cloned.1.call-update) | async-done | bytes 851984 | tf_op jit(solution)/shard_map/reduce_scatter | solution.py:450
  321.3 1.5 fusion.4
  322.9 1.0 pad_maximum_fusion.4
  (43 shorter events, 5.4 us)
Async XLA Ops:
  7.2 70.5 %all-gather.3.cloned.1.call-start = ((), (), s32[]{:S(2)}) async-start(), calls=%async_computation.1 | async-start | bytes 4259840 | tf_op jit(solution)/shard_map/all_gather | solution.py:436
  9.7 1.2 copy-start.5
  9.7 1.2 copy-start.6
  9.7 219.5 %all-gather.5.cloned.1.call-start = ((), (), s32[]{:S(2)}) async-start(), calls=%async_computation.2 | async-start | bytes 4259840 | tf_op jit(solution)/shard_map/all_gather | solution.py:436
  10.8 310.5 %reduce-scatter.2.cloned.1.call-start = ((), (), s32[]{:S(2)}) async-start(), calls=%async_computation.3 | async-start | bytes 4259840 | tf_op jit(solution)/shard_map/reduce_scatter | solution.py:450
  103.8 5.8 %copy-start = (bf16[52,64,512]{2,1,0:T(8,128)(2,1)S(1)}, bf16[52,64,512]{2,1,0:T(8,128)(2,1)}, u32[]{:S(2)}) copy-start(bf16[52,64,512]{2,1,0:T(8,128)(2,1)} %get-tuple-element.10) | copy-start | bytes 10223620
  106.8 2.9 collective-permute-start
  108.3 41.9 %collective-permute-start.3 = (bf16[13,64,512]{2,1,0:T(8,128)(2,1)}, bf16[13,64,512]{2,1,0:T(8,128)(2,1)}, u32[]{:S(2)}, u32[]{:S(2)}) collective-permute-start(bf16[13,64,512]{2,1,0:T(8,128)(2,1)} %get-tuple-element.18), channel_id=1, source_target_pairs={{12,8},{13,9},{14,10},{15,11},{28,24},{29,25},{30,26},{31,27}} | collective-permute-start | bytes 2555912 | tf_op jit(solution)/shard_map/ppermute | solution.py:404
  112.0 64.0 %collective-permute-start.1 = (bf16[13,64,512]{2,1,0:T(8,128)(2,1)}, bf16[13,64,512]{2,1,0:T(8,128)(2,1)}, u32[]{:S(2)}, u32[]{:S(2)}) collective-permute-start(bf16[13,64,512]{2,1,0:T(8,128)(2,1)} %fusion.2), channel_id=1, source_target_pairs={{0,4},{4,8},{1,5},{5,9},{2,6},{6,10},{3,7},{7,11},{16,20},{20,24},... | collective-permute-start | bytes 2555912 | tf_op jit(solution)/shard_map/ppermute | solution.py:400
  179.1 25.9 %collective-permute-start.4 = (bf16[13,64,512]{2,1,0:T(8,128)(2,1)}, bf16[13,64,512]{2,1,0:T(8,128)(2,1)}, u32[]{:S(2)}, u32[]{:S(2)}) collective-permute-start(bf16[13,64,512]{2,1,0:T(8,128)(2,1)} %get-tuple-element.16), channel_id=1, source_target_pairs={{8,4},{12,8},{9,5},{13,9},{10,6},{14,10},{11,7},{15,11},{24,20},{2... | collective-permute-start | bytes 2555912 | tf_op jit(solution)/shard_map/ppermute | solution.py:404
  186.8 24.0 %collective-permute-start.2 = (bf16[13,64,512]{2,1,0:T(8,128)(2,1)}, bf16[13,64,512]{2,1,0:T(8,128)(2,1)S(1)}, u32[]{:S(2)}, u32[]{:S(2)}) collective-permute-start(bf16[13,64,512]{2,1,0:T(8,128)(2,1)} %get-tuple-element.15), channel_id=1, source_target_pairs={{0,4},{4,8},{8,12},{1,5},{5,9},{9,13},{2,6},{6,10},{10,14},{3,7},{... | collective-permute-start | bytes 2555912 | tf_op jit(solution)/shard_map/ppermute | solution.py:400
  206.4 21.4 %collective-permute-start.5 = (bf16[13,64,512]{2,1,0:T(8,128)(2,1)S(1)}, bf16[13,64,512]{2,1,0:T(8,128)(2,1)S(1)}, u32[]{:S(2)}, u32[]{:S(2)}) collective-permute-start(bf16[13,64,512]{2,1,0:T(8,128)(2,1)S(1)} %fusion.1), channel_id=1, source_target_pairs={{4,0},{8,4},{12,8},{5,1},{9,5},{13,9},{6,2},{10,6},{14,10},{7,3},{... | collective-permute-start | bytes 2555912 | tf_op jit(solution)/shard_map/ppermute | solution.py:404
  255.5 1.0 copy-start.3
  255.5 1.1 copy-start.4
  255.6 2.1 copy-start.1
  257.9 63.4 %copy-start.2 = (f32[13,64,512]{2,1,0:T(8,128)S(1)}, f32[13,64,512]{2,1,0:T(8,128)}, u32[]{:S(2)}) copy-start(f32[13,64,512]{2,1,0:T(8,128)} %get-tuple-element.13) | copy-start | bytes 5111812
Sparse Core Ops, SparseCore 0:
  10.1 67.4 all-gather.2
  79.8 87.4 all-gather.4
  255.7 65.5 reduce-scatter.1

commit v6 on v4

--- a/solution.py
+++ b/solution.py
@@ -418,29 +418,41 @@
     first_table = first.reshape(1).astype(jnp.int32)
     chunks = 2 if (width // DH) % 2 == 0 else 1
     part = width // chunks
-    sources = []
-    previous = None
+    global_ids = write_ids
+    results = []
+    link = None
     for chunk in range(chunks):
         cols = slice(chunk * part, (chunk + 1) * part)
         packed = jnp.concatenate([key_rows[:, cols], value_rows[:, cols]], axis=1)
-        packed = packed.reshape(blocks_dev, BLOCK, 2 * part)
-        if previous is not None:
-            packed, _ = lax.optimization_barrier((packed, previous))
-        outgoing = jnp.dot(
-            selector, packed.reshape(blocks_dev, BLOCK * 2 * part),
-            preferred_element_type=jnp.float32,
-        ).astype(jnp.bfloat16)
-        outgoing = outgoing.reshape(seq_size * capacity, BLOCK, 2 * part)
-        haloed = extended(packed, (("seq", 0),), 1)
-        arrived = lax.all_to_all(outgoing, "seq", split_axis=0, concat_axis=0, tiled=True)
-        previous = arrived
-        sources.append(jnp.concatenate([haloed, arrived], axis=0))
+        if chunk == 0:
+            source = lax.all_gather(packed, "seq", axis=0, tiled=True)
+            source = source.reshape(total, BLOCK, 2 * part)
+            table_ids = global_ids
+            link = source[0, 0, :1]
+        else:
+            packed = packed.reshape(blocks_dev, BLOCK, 2 * part)
+            route = selector + (link * 0).astype(selector.dtype)
+            outgoing = jnp.dot(
+                route, packed.reshape(blocks_dev, BLOCK * 2 * part),
+                preferred_element_type=jnp.float32,
+            ).astype(jnp.bfloat16)
+            outgoing = outgoing.reshape(seq_size * capacity, BLOCK, 2 * part)
+            haloed = extended(packed, (("seq", 0),), 1)
+            arrived = lax.all_to_all(outgoing, "seq", split_axis=0, concat_axis=0, tiled=True)
+            source = jnp.concatenate([haloed, arrived], axis=0)
+            table_ids = read_ids
+        results.append((source, table_ids))
     query_parts, key_parts, value_parts = [], [], []
+    after = None
     for chunk in range(chunks):
+        source, table_ids = results[chunk]
+        table = first_table
+        if after is not None:
+            table = table + (after[0, 0, :1] * 0.0).astype(jnp.int32)
         own_sum, spread, query_out = block_attention(
-            read_ids, write_ids, valid, first_table, queries, out_grad, sources[chunk],
-            chunk, part, total,
-        )
+            table_ids, global_ids, valid, table, queries, out_grad, source, chunk, part, total,
+        )
+        after = own_sum
         returned = lax.psum_scatter(
             spread.reshape(total * BLOCK, 2 * part), "seq", scatter_dimension=0, tiled=True
         )

time: 323 us -> 323 us (level)
  waiting for transfers between devices: 199 us -> 219 us
  starting transfers between devices: 22.4 us -> 11.4 us
  local copies, waits for them, and re-layouts: 16.7 us -> 11.2 us
    all_gather x0 -> x1, waiting for transfers between devices: none -> 65.4 us  [gathered_shards(): source = lax.all_gather(packed, 'seq', axis=0, tiled=True)]
    ppermute x2 -> x1, waiting for transfers between devices: 138 us -> 92.5 us  [extended(): lax.ppermute(lax.slice_in_dim(block, block.shape[dim] - width, None, axis...]
    all_to_all x2 -> x1, starting transfers between devices: 10.6 us -> 5.5 us  [gathered_shards(): lax.all_to_all(outgoing, 'seq', split_axis=0, concat_axis=0, tiled=True)]
    unnamed x26 -> x19, local copies, waits for them, and re-layouts: 7.14 us -> 2.32 us
    ppermute x2 -> x1, starting transfers between devices: 6.75 us -> 3.37 us  [extended(): lax.ppermute(lax.slice_in_dim(block, block.shape[dim] - width, None, axis...]
  transfers between devices with their start and end apart: 8 -> 6, of which waited for: 3 -> 3; matrix products, arithmetic and copies ran while one was open for 5% -> 5% of each run, Pallas kernels for 8% -> 8%
where the time goes in v6:
time: 323 us; the launch traced here: 321 us
  waiting for transfers between devices  219 us (68%)
  Pallas kernels  52.4 us (16%)
  between operations  15.3 us (5%)
  starting transfers between devices  11.4 us (4%)
  local copies, waits for them, and re-layouts  11.2 us (3%)
  other arithmetic  10.6 us (3%)
    ppermute x1, waiting for transfers between devices, extended(): lax.ppermute(lax.slice_in_dim(block, block.shape[dim] - width, None, axis...  92.5 us
    all_gather x1, waiting for transfers between devices, gathered_shards(): source = lax.all_gather(packed, 'seq', axis=0, tiled=True)  65.4 us
    reduce_scatter x2, waiting for transfers between devices, gathered_shards(): lax.psum_scatter(spread.reshape(total * BLOCK, 2 * part), 'seq', scatter_...  61 us
    pallas_call x2, Pallas kernels, block_attention(): pl.pallas_call(block_kernel, grid_spec=grid_spec, out_shape=[jax.ShapeDty...  52.4 us
  transfers between devices with their start and end apart: 6, of which 3 were waited for; matrix products, arithmetic and copies ran while one was open for 5% of the time, Pallas kernels for 8%

profile of v6, /device:TPU:22, one launch (start us, length us, event | category | flops | bytes accessed | tf_op | source)
XLA Modules:
  0.0 320.7 jit_solution(9286994741668540030)
XLA Ops:
  7.2 1.5 fusion.19
  8.8 1.0 pad_maximum_fusion.2
  11.6 0.7 reshape.125.ids_ref.write_ref
  12.3 65.4 %all-gather.2.cloned.1.call-done = bf16[3328,512]{1,0:T(8,128)(2,1)} async-done(((bf16[832,512]{1,0:T(8,128)(2,1)}), bf16[3328,512]{1,0:T(8,128)(2,1)}) %all-gather.2.cloned.1.call-update) | async-done | bytes 3407888 | tf_op jit(solution)/shard_map/all_gather | solution.py:428
  77.6 26.2 %shard_map.85 = (f32[13,64,512]{2,1,0:T(8,128)}, bf16[52,64,512]{2,1,0:T(8,128)(2,1)}, bf16[832,256]{1,0:T(8,128)(2,1)}) custom-call(s32[65]{0:T(128)} %reshape.125.ids_ref.write_ref, s32[65]{0:T(128)} %reshape.125.ids_ref.write_ref, s32[65]{0:T(128)} %reshape.135.valid_ref, s32[1]{0:T(128)} %bitcast.first_ref, bf16[832,512]{1,0:T(8,128)(2,1)} %q_ref.3, ...), custom_call_target="tpu_custom_call" | custom-call | tf_op jit(solution)/shard_map/pallas_call | solution.py:379
  105.1 1.3 slice.64
  107.2 0.8 convolution_convert_fusion
  108.0 1.0 copy.20
  109.0 1.6 slice.69
  110.6 5.5 %all-to-all-start = ((bf16[36,64,512]{2,1,0:T(8,128)(2,1)}), bf16[36,64,512]{2,1,0:T(8,128)(2,1)S(1)}, u32[]{:S(2)}, u32[]{:S(2)}) async-start(bf16[36,64,512]{2,1,0:T(8,128)(2,1)} %slice.69), calls=%async_computation | async-start | bytes 4718592 | tf_op jit(solution)/shard_map/all_to_all | solution.py:441
  116.1 0.8 fusion.6
  116.9 3.4 %collective-permute-start = (bf16[1,64,512]{2,1,0:T(8,128)(2,1)S(1)}, bf16[1,64,512]{2,1,0:T(8,128)(2,1)S(1)}, u32[]{:S(2)}, u32[]{:S(2)}) collective-permute-start(bf16[1,64,512]{2,1,0:T(8,128)(2,1)S(1)} %get-tuple-element.19), channel_id=1, source_target_pairs={{0,4},{4,8},{8,12},{1,5},{5,9},{9,13},{2,6},{6,10},{10,14},{3,7},{... | collective-permute-start | bytes 196616 | tf_op jit(solution)/shard_map/ppermute | solution.py:20
  120.3 2.5 collective-permute-start.1
  123.5 1.2 slice.48
  125.3 92.5 %collective-permute-done = bf16[1,64,512]{2,1,0:T(8,128)(2,1)S(1)} collective-permute-done((bf16[1,64,512]{2,1,0:T(8,128)(2,1)S(1)}, bf16[1,64,512]{2,1,0:T(8,128)(2,1)S(1)}, u32[]{:S(2)}, u32[]{:S(2)}) %collective-permute-start) | collective-permute-done | bytes 65568 | tf_op jit(solution)/shard_map/ppermute | solution.py:20
  217.8 2.0 pad_maximum_fusion.rest_0_.rest_1_.rest_2_.rest_3_.rest_4_
  219.7 26.2 %shard_map.86 = (f32[13,64,512]{2,1,0:T(8,128)}, bf16[52,64,512]{2,1,0:T(8,128)(2,1)}, bf16[832,256]{1,0:T(8,128)(2,1)}) custom-call(s32[65]{0:T(128)} %reshape.128.ids_ref, s32[65]{0:T(128)} %reshape.125.ids_ref.write_ref, s32[65]{0:T(128)} %reshape.135.valid_ref, s32[1]{0:T(128)S(6)} %add.124.first_ref, bf16[832,512]{1,0:T(8,128)(2,1)} %q_ref.3, ...), custom_call_target="tpu_custom_call" | custom-call | tf_op jit(solution)/shard_map/pallas_call | solution.py:379
  246.0 1.0 copy-done.4
  247.1 1.0 pad_maximum_fusion.3
  248.1 1.5 fusion.1
  249.7 61.0 %reduce-scatter.5.cloned.1.call-done = bf16[832,512]{1,0:T(8,128)(2,1)} async-done(((bf16[3328,512]{1,0:T(8,128)(2,1)}), bf16[832,512]{1,0:T(8,128)(2,1)}) %reduce-scatter.5.cloned.1.call-update) | async-done | bytes 851984 | tf_op jit(solution)/shard_map/reduce_scatter | solution.py:456
  310.7 1.5 fusion
  312.3 1.0 pad_maximum_fusion.5
  313.3 1.0 pad_maximum_fusion.4
  (58 shorter events, 4.2 us)
Async XLA Ops:
  7.2 70.5 %all-gather.2.cloned.1.call-start = ((), (), s32[]{:S(2)}) async-start(), calls=%async_computation.3 | async-start | bytes 4259840 | tf_op jit(solution)/shard_map/all_gather | solution.py:428
  8.7 95.6 %copy-start = (bf16[832,256]{1,0:T(8,128)(2,1)}, bf16[832,256]{1,0:T(8,128)(2,1)S(1)}, u32[]{:S(2)}) copy-start(bf16[832,256]{1,0:T(8,128)(2,1)S(1)} %get-tuple-element.21) | copy-start | bytes 1277956
  8.8 95.6 %copy-start.1 = (bf16[832,256]{1,0:T(8,128)(2,1)}, bf16[832,256]{1,0:T(8,128)(2,1)S(1)}, u32[]{:S(2)}) copy-start(bf16[832,256]{1,0:T(8,128)(2,1)S(1)} %get-tuple-element.34) | copy-start | bytes 1277956
  8.8 1.9 copy-start.6
  8.8 2.6 copy-start.7
  9.8 238.3 %reduce-scatter.3.cloned.1.call-start = ((), (), s32[]{:S(2)}) async-start(), calls=%async_computation.4 | async-start | bytes 4259840 | tf_op jit(solution)/shard_map/reduce_scatter | solution.py:456
  110.6 107.2 %all-to-all-start = ((bf16[36,64,512]{2,1,0:T(8,128)(2,1)}), bf16[36,64,512]{2,1,0:T(8,128)(2,1)S(1)}, u32[]{:S(2)}, u32[]{:S(2)}) async-start(bf16[36,64,512]{2,1,0:T(8,128)(2,1)} %slice.69), calls=%async_computation | async-start | bytes 4718592 | tf_op jit(solution)/shard_map/all_to_all | solution.py:441
  116.1 194.6 %reduce-scatter.5.cloned.1.call-start = ((), (), s32[]{:S(2)}) async-start(), calls=%async_computation.5 | async-start | bytes 4259840 | tf_op jit(solution)/shard_map/reduce_scatter | solution.py:456
  116.9 100.9 %collective-permute-start = (bf16[1,64,512]{2,1,0:T(8,128)(2,1)S(1)}, bf16[1,64,512]{2,1,0:T(8,128)(2,1)S(1)}, u32[]{:S(2)}, u32[]{:S(2)}) collective-permute-start(bf16[1,64,512]{2,1,0:T(8,128)(2,1)S(1)} %get-tuple-element.19), channel_id=1, source_target_pairs={{0,4},{4,8},{8,12},{1,5},{5,9},{9,13},{2,6},{6,10},{10,14},{3,7},{... | collective-permute-start | bytes 196616 | tf_op jit(solution)/shard_map/ppermute | solution.py:20
  120.3 97.5 %collective-permute-start.1 = (bf16[1,64,512]{2,1,0:T(8,128)(2,1)S(1)}, bf16[1,64,512]{2,1,0:T(8,128)(2,1)S(1)}, u32[]{:S(2)}, u32[]{:S(2)}) collective-permute-start(bf16[1,64,512]{2,1,0:T(8,128)(2,1)S(1)} %get-tuple-element.20), channel_id=1, source_target_pairs={{4,0},{8,4},{12,8},{5,1},{9,5},{13,9},{6,2},{10,6},{14,10},{7,3},{... | collective-permute-start | bytes 196616 | tf_op jit(solution)/shard_map/ppermute | solution.py:23
  246.0 1.0 copy-start.4
  246.0 1.1 copy-start.5
  246.0 2.1 copy-start.2
  249.6 61.1 %copy-start.3 = (f32[13,64,512]{2,1,0:T(8,128)S(1)}, f32[13,64,512]{2,1,0:T(8,128)}, u32[]{:S(2)}) copy-start(f32[13,64,512]{2,1,0:T(8,128)} %get-tuple-element.13) | copy-start | bytes 5111812
Sparse Core Ops, SparseCore 0:
  10.1 67.4 all-gather.1
  104.0 112.3 reduce-scatter.2
  246.1 64.5 reduce-scatter.4

commit v7 on v6

--- a/solution.py
+++ b/solution.py
@@ -431,7 +431,7 @@
             link = source[0, 0, :1]
         else:
             packed = packed.reshape(blocks_dev, BLOCK, 2 * part)
-            route = selector + (link * 0).astype(selector.dtype)
+            route = selector
             outgoing = jnp.dot(
                 route, packed.reshape(blocks_dev, BLOCK * 2 * part),
                 preferred_element_type=jnp.float32,
@@ -443,7 +443,7 @@
             table_ids = read_ids
         results.append((source, table_ids))
     query_parts, key_parts, value_parts = [], [], []
-    after = None
+    after = results[-1][0][blocks_dev + 2 :] if chunks > 1 else None
     for chunk in range(chunks):
         source, table_ids = results[chunk]
         table = first_table

time: 323 us -> 298 us (0.923)
  waiting for transfers between devices: 219 us -> 194 us
    all_to_all x1, waiting for transfers between devices: 0.01 us -> 101 us  [gathered_shards(): lax.all_to_all(outgoing, 'seq', split_axis=0, concat_axis=0, tiled=True)]
    ppermute x1, waiting for transfers between devices: 92.5 us -> 0.01 us  [extended(): lax.ppermute(lax.slice_in_dim(block, block.shape[dim] - width, None, axis...]
    all_gather x1, waiting for transfers between devices: 65.4 us -> 0.82 us  [gathered_shards(): source = lax.all_gather(packed, 'seq', axis=0, tiled=True)]
    reduce_scatter x2, waiting for transfers between devices: 61 us -> 88.1 us  [gathered_shards(): lax.psum_scatter(spread.reshape(total * BLOCK, 2 * part), 'seq', scatter_...]
    ppermute x1, waiting for transfers between devices: 0.01 us -> 4.52 us  [extended(): lax.ppermute(lax.slice_in_dim(block, 0, width, axis=dim), axis, backward)]
  transfers between devices with their start and end apart: 6 -> 6, of which waited for: 3 -> 5; matrix products, arithmetic and copies ran while one was open for 5% -> 5% of each run, Pallas kernels for 8% -> 9%
where the time goes in v7:
time: 298 us; the launch traced here: 296 us
  waiting for transfers between devices  194 us (65%)
  Pallas kernels  52.5 us (18%)
  between operations  15.3 us (5%)
  starting transfers between devices  11.9 us (4%)
  other arithmetic  10.6 us (4%)
  local copies, waits for them, and re-layouts  10.5 us (4%)
    all_to_all x1, waiting for transfers between devices, gathered_shards(): lax.all_to_all(outgoing, 'seq', split_axis=0, concat_axis=0, tiled=True)  101 us
    reduce_scatter x2, waiting for transfers between devices, gathered_shards(): lax.psum_scatter(spread.reshape(total * BLOCK, 2 * part), 'seq', scatter_...  88.1 us
    pallas_call x2, Pallas kernels, block_attention(): pl.pallas_call(block_kernel, grid_spec=grid_spec, out_shape=[jax.ShapeDty...  52.5 us
  transfers between devices with their start and end apart: 6, of which 5 were waited for; matrix products, arithmetic and copies ran while one was open for 5% of the time, Pallas kernels for 9%

profile of v7, /device:TPU:22, one launch (start us, length us, event | category | flops | bytes accessed | tf_op | source)
XLA Modules:
  0.0 296.1 jit_solution(14877606553612691641)
XLA Ops:
  7.2 1.5 fusion.18
  8.8 1.0 pad_maximum_fusion.2
  11.3 0.8 convolution_convert_fusion
  12.1 1.0 copy.20
  13.1 1.6 slice.69
  14.7 5.2 %all-to-all-start = ((bf16[36,64,512]{2,1,0:T(8,128)(2,1)}), bf16[36,64,512]{2,1,0:T(8,128)(2,1)S(1)}, u32[]{:S(2)}, u32[]{:S(2)}) async-start(bf16[36,64,512]{2,1,0:T(8,128)(2,1)} %slice.69), calls=%async_computation | async-start | bytes 4718592 | tf_op jit(solution)/shard_map/all_to_all | solution.py:441
  22.2 100.9 %all-to-all-done = bf16[36,64,512]{2,1,0:T(8,128)(2,1)S(1)} async-done(((bf16[36,64,512]{2,1,0:T(8,128)(2,1)}), bf16[36,64,512]{2,1,0:T(8,128)(2,1)S(1)}, u32[]{:S(2)}, u32[]{:S(2)}) %all-to-all-start) | async-done | bytes 2359328 | tf_op jit(solution)/shard_map/all_to_all | solution.py:441
  124.4 0.8 all-gather.2.cloned.1.call-done
  125.2 26.2 %shard_map.85 = (f32[13,64,512]{2,1,0:T(8,128)}, bf16[52,64,512]{2,1,0:T(8,128)(2,1)}, bf16[832,256]{1,0:T(8,128)(2,1)}) custom-call(s32[65]{0:T(128)} %reshape.125.ids_ref.write_ref, s32[65]{0:T(128)} %reshape.125.ids_ref.write_ref, s32[65]{0:T(128)} %reshape.135.valid_ref, s32[1]{0:T(128)S(6)} %add.109.first_ref, bf16[832,512]{1,0:T(8,128)(2,1)} %q_ref.3, ...), custom_call_target="tpu_custom_call" | custom-call | tf_op jit(solution)/shard_map/pallas_call | solution.py:379
  151.5 0.8 fusion.5
  152.3 4.6 %collective-permute-start = (bf16[1,64,512]{2,1,0:T(8,128)(2,1)S(1)}, bf16[1,64,512]{2,1,0:T(8,128)(2,1)S(1)}, u32[]{:S(2)}, u32[]{:S(2)}) collective-permute-start(bf16[1,64,512]{2,1,0:T(8,128)(2,1)S(1)} %get-tuple-element.19), channel_id=1, source_target_pairs={{0,4},{4,8},{8,12},{1,5},{5,9},{9,13},{2,6},{6,10},{10,14},{3,7},{... | collective-permute-start | bytes 196616 | tf_op jit(solution)/shard_map/ppermute | solution.py:20
  157.0 1.9 collective-permute-start.1
  159.6 4.5 %collective-permute-done.1 = bf16[1,64,512]{2,1,0:T(8,128)(2,1)S(1)} collective-permute-done((bf16[1,64,512]{2,1,0:T(8,128)(2,1)S(1)}, bf16[1,64,512]{2,1,0:T(8,128)(2,1)S(1)}, u32[]{:S(2)}, u32[]{:S(2)}) %collective-permute-start.1) | collective-permute-done | bytes 65568 | tf_op jit(solution)/shard_map/ppermute | solution.py:23
  164.1 1.9 pad_maximum_fusion.rest_0_.rest_1_.rest_2_.rest_3_.rest_4_
  166.0 1.2 slice.51
  167.9 26.3 %shard_map.86 = (f32[13,64,512]{2,1,0:T(8,128)}, bf16[52,64,512]{2,1,0:T(8,128)(2,1)}, bf16[832,256]{1,0:T(8,128)(2,1)}) custom-call(s32[65]{0:T(128)} %reshape.129.ids_ref, s32[65]{0:T(128)} %reshape.125.ids_ref.write_ref, s32[65]{0:T(128)} %reshape.135.valid_ref, s32[1]{0:T(128)S(6)} %add.115.first_ref, bf16[832,512]{1,0:T(8,128)(2,1)} %q_ref.3, ...), custom_call_target="tpu_custom_call" | custom-call | tf_op jit(solution)/shard_map/pallas_call | solution.py:379
  194.2 1.0 copy-done.4
  195.3 1.0 pad_maximum_fusion.3
  196.3 22.9 %reduce-scatter.3.cloned.1.call-done = bf16[832,512]{1,0:T(8,128)(2,1)} async-done(((bf16[3328,512]{1,0:T(8,128)(2,1)}), bf16[832,512]{1,0:T(8,128)(2,1)}) %reduce-scatter.3.cloned.1.call-update) | async-done | bytes 851984 | tf_op jit(solution)/shard_map/reduce_scatter | solution.py:456
  219.2 1.5 fusion.1
  220.8 65.2 %reduce-scatter.5.cloned.1.call-done = bf16[832,512]{1,0:T(8,128)(2,1)} async-done(((bf16[3328,512]{1,0:T(8,128)(2,1)}), bf16[832,512]{1,0:T(8,128)(2,1)}) %reduce-scatter.5.cloned.1.call-update) | async-done | bytes 851984 | tf_op jit(solution)/shard_map/reduce_scatter | solution.py:456
  286.0 1.5 fusion
  287.6 1.0 pad_maximum_fusion.5
  288.6 1.0 pad_maximum_fusion.4
  (58 shorter events, 5.4 us)
Async XLA Ops:
  7.2 118.0 %all-gather.2.cloned.1.call-start = ((), (), s32[]{:S(2)}) async-start(), calls=%async_computation.3 | async-start | bytes 4259840 | tf_op jit(solution)/shard_map/all_gather | solution.py:428
  8.7 1.8 copy-start
  8.8 1.8 copy-start.1
  8.8 1.0 copy-start.6
  8.8 1.4 copy-start.7
  14.7 108.4 %all-to-all-start = ((bf16[36,64,512]{2,1,0:T(8,128)(2,1)}), bf16[36,64,512]{2,1,0:T(8,128)(2,1)S(1)}, u32[]{:S(2)}, u32[]{:S(2)}) async-start(bf16[36,64,512]{2,1,0:T(8,128)(2,1)} %slice.69), calls=%async_computation | async-start | bytes 4718592 | tf_op jit(solution)/shard_map/all_to_all | solution.py:441
  19.9 199.3 %reduce-scatter.3.cloned.1.call-start = ((), (), s32[]{:S(2)}) async-start(), calls=%async_computation.4 | async-start | bytes 4259840 | tf_op jit(solution)/shard_map/reduce_scatter | solution.py:456
  151.4 134.6 %reduce-scatter.5.cloned.1.call-start = ((), (), s32[]{:S(2)}) async-start(), calls=%async_computation.5 | async-start | bytes 4259840 | tf_op jit(solution)/shard_map/reduce_scatter | solution.py:456
  152.3 7.3 %collective-permute-start = (bf16[1,64,512]{2,1,0:T(8,128)(2,1)S(1)}, bf16[1,64,512]{2,1,0:T(8,128)(2,1)S(1)}, u32[]{:S(2)}, u32[]{:S(2)}) collective-permute-start(bf16[1,64,512]{2,1,0:T(8,128)(2,1)S(1)} %get-tuple-element.19), channel_id=1, source_target_pairs={{0,4},{4,8},{8,12},{1,5},{5,9},{9,13},{2,6},{6,10},{10,14},{3,7},{... | collective-permute-start | bytes 196616 | tf_op jit(solution)/shard_map/ppermute | solution.py:20
  157.0 7.2 %collective-permute-start.1 = (bf16[1,64,512]{2,1,0:T(8,128)(2,1)S(1)}, bf16[1,64,512]{2,1,0:T(8,128)(2,1)S(1)}, u32[]{:S(2)}, u32[]{:S(2)}) collective-permute-start(bf16[1,64,512]{2,1,0:T(8,128)(2,1)S(1)} %get-tuple-element.20), channel_id=1, source_target_pairs={{4,0},{8,4},{12,8},{5,1},{9,5},{13,9},{6,2},{10,6},{14,10},{7,3},{... | collective-permute-start | bytes 196616 | tf_op jit(solution)/shard_map/ppermute | solution.py:23
  194.2 1.0 copy-start.4
  194.2 1.1 copy-start.5
  194.2 24.9 %copy-start.2 = (f32[13,64,512]{2,1,0:T(8,128)S(1)}, f32[13,64,512]{2,1,0:T(8,128)}, u32[]{:S(2)}) copy-start(f32[13,64,512]{2,1,0:T(8,128)} %get-tuple-element.10) | copy-start | bytes 5111812
  220.7 65.3 %copy-start.3 = (f32[13,64,512]{2,1,0:T(8,128)S(1)}, f32[13,64,512]{2,1,0:T(8,128)}, u32[]{:S(2)}) copy-start(f32[13,64,512]{2,1,0:T(8,128)} %get-tuple-element.13) | copy-start | bytes 5111812
Sparse Core Ops, SparseCore 0:
  10.1 115.0 all-gather.1
  151.5 67.5 reduce-scatter.2
  221.5 64.5 reduce-scatter.4

commit v8 on v7

--- a/solution.py
+++ b/solution.py
@@ -449,14 +449,48 @@
         table = first_table
         if after is not None:
             table = table + (after[0, 0, :1] * 0.0).astype(jnp.int32)
-        own_sum, spread, query_out = block_attention(
-            table_ids, global_ids, valid, table, queries, out_grad, source, chunk, part, total,
-        )
+        if chunk == 0:
+            own_sum, spread, query_out = block_attention(
+                table_ids, global_ids, valid, table, queries, out_grad, source, chunk, part, total,
+            )
+            returned = lax.psum_scatter(
+                spread.reshape(total * BLOCK, 2 * part), "seq", scatter_dimension=0, tiled=True
+            )
+            summed = own_sum.reshape(tokens, 2 * part) + returned.astype(jnp.float32)
+        else:
+            extra = blocks_dev * RAND
+            far_rows = (total + jnp.arange(extra, dtype=jnp.int32)).reshape(blocks_dev, RAND)
+            far_write = jnp.concatenate([window, far_rows], axis=1).reshape(-1)
+            own_sum, spread, query_out = block_attention(
+                table_ids, far_write, valid, table, queries, out_grad, source, chunk, part,
+                total + extra,
+            )
+            returning = (
+                jnp.zeros((seq_size * capacity, BLOCK, 2 * part), jnp.bfloat16)
+                .at[slot_index]
+                .set(spread[total:])
+            )
+            returned = lax.all_to_all(returning, "seq", split_axis=0, concat_axis=0, tiled=True)
+            gathered = jnp.dot(
+                selector.T,
+                returned.reshape(seq_size * capacity, BLOCK * 2 * part),
+                preferred_element_type=jnp.float32,
+            ).reshape(blocks_dev, BLOCK, 2 * part)
+            left_edge = lax.dynamic_index_in_dim(
+                spread, jnp.clip(first - 1, 0, total - 1), 0, keepdims=False
+            )
+            right_edge = lax.dynamic_index_in_dim(
+                spread, jnp.clip(first + blocks_dev, 0, total - 1), 0, keepdims=False
+            )
+            from_right = lax.ppermute(left_edge, "seq", [(i, i - 1) for i in range(1, seq_size)])
+            from_left = lax.ppermute(right_edge, "seq", [(i, i + 1) for i in range(seq_size - 1)])
+            combined = (
+                (own_sum + gathered)
+                .at[0].add(from_left.astype(jnp.float32))
+                .at[blocks_dev - 1].add(from_right.astype(jnp.float32))
+            )
+            summed = combined.reshape(tokens, 2 * part)
         after = own_sum
-        returned = lax.psum_scatter(
-            spread.reshape(total * BLOCK, 2 * part), "seq", scatter_dimension=0, tiled=True
-        )
-        summed = own_sum.reshape(tokens, 2 * part) + returned.astype(jnp.float32)
         query_parts.append(query_out)
         key_parts.append(summed[:, :part].astype(jnp.bfloat16))
         value_parts.append(summed[:, part:].astype(jnp.bfloat16))

time: 298 us -> 287 us (0.963); the launches traced: 296 us -> 282 us
  waiting for transfers between devices: 194 us -> 155 us
  starting transfers between devices: 11.9 us -> 23.3 us
  local copies, waits for them, and re-layouts: 10.5 us -> 21.2 us
    reduce_scatter x2 -> x1, waiting for transfers between devices: 88.1 us -> 0.02 us  [gathered_shards(): lax.psum_scatter(spread.reshape(total * BLOCK, 2 * part), 'seq', scatter_...]
    all_to_all x0 -> x1, waiting for transfers between devices: none -> 49.2 us  [gathered_shards(): lax.all_to_all(returning, 'seq', split_axis=0, concat_axis=0, tiled=True)]
    ppermute x0 -> x2, starting transfers between devices: none -> 6.02 us  [the longest x1 3.21 us: gathered_shards(): lax.ppermute(right_edge, 'seq', [(i, i + 1) for i in range(seq_size - 1)])]
    all_to_all x0 -> x1, starting transfers between devices: none -> 5.45 us  [gathered_shards(): lax.all_to_all(returning, 'seq', split_axis=0, concat_axis=0, tiled=True)]
    scatter x0 -> x1, local copies, waits for them, and re-layouts: none -> 5.38 us  [gathered_shards(): returning = jnp.zeros((seq_size * capacity, BLOCK, 2 * part), jnp.bfloat1...]
  transfers between devices with their start and end apart: 6 -> 8, of which waited for: 5 -> 4; matrix products, arithmetic and copies ran while one was open for 5% -> 10% of each run, Pallas kernels for 9% -> 10%
where the time goes in v8:
time: 287 us; the launch traced here: 282 us
  waiting for transfers between devices  155 us (54%)
  Pallas kernels  53.4 us (19%)
  starting transfers between devices  23.3 us (8%)
  local copies, waits for them, and re-layouts  21.2 us (7%)
  between operations  15.7 us (5%)
  other arithmetic  10.3 us (4%)
    all_to_all x1, waiting for transfers between devices, gathered_shards(): lax.all_to_all(outgoing, 'seq', split_axis=0, concat_axis=0, tiled=True)  101 us
    pallas_call x2, Pallas kernels, block_attention(): pl.pallas_call(block_kernel, grid_spec=grid_spec, out_shape=[jax.ShapeDty...  53.4 us
    all_to_all x1, waiting for transfers between devices, gathered_shards(): lax.all_to_all(returning, 'seq', split_axis=0, concat_axis=0, tiled=True)  49.2 us
  transfers between devices with their start and end apart: 8, of which 4 were waited for; matrix products, arithmetic and copies ran while one was open for 10% of the time, Pallas kernels for 10%

profile of v8, /device:TPU:22, one launch (start us, length us, event | category | flops | bytes accessed | tf_op | source)
XLA Modules:
  0.0 281.6 jit_solution(16093682589590391556)
XLA Ops:
  7.2 1.5 fusion.23
  12.1 1.0 copy.24
  13.1 1.6 slice.121
  14.7 5.2 %all-to-all-start = ((bf16[36,64,512]{2,1,0:T(8,128)(2,1)}), bf16[36,64,512]{2,1,0:T(8,128)(2,1)S(1)}, u32[]{:S(2)}, u32[]{:S(2)}) async-start(bf16[36,64,512]{2,1,0:T(8,128)(2,1)} %slice.121), calls=%async_computation | async-start | bytes 4718592 | tf_op jit(solution)/shard_map/all_to_all | solution.py:441
  22.1 100.9 %all-to-all-done = bf16[36,64,512]{2,1,0:T(8,128)(2,1)S(1)} async-done(((bf16[36,64,512]{2,1,0:T(8,128)(2,1)}), bf16[36,64,512]{2,1,0:T(8,128)(2,1)S(1)}, u32[]{:S(2)}, u32[]{:S(2)}) %all-to-all-start) | async-done | bytes 2359328 | tf_op jit(solution)/shard_map/all_to_all | solution.py:441
  125.2 26.2 %shard_map.85 = (f32[13,64,512]{2,1,0:T(8,128)}, bf16[52,64,512]{2,1,0:T(8,128)(2,1)}, bf16[832,256]{1,0:T(8,128)(2,1)}) custom-call(s32[65]{0:T(128)} %reshape.225.ids_ref.write_ref, s32[65]{0:T(128)} %reshape.225.ids_ref.write_ref, s32[65]{0:T(128)} %reshape.238.valid_ref, s32[1]{0:T(128)S(6)} %add.152.first_ref, bf16[832,512]{1,0:T(8,128)(2,1)} %q_ref.3, ...), custom_call_target="tpu_custom_call" | custom-call | tf_op jit(solution)/shard_map/pallas_call | solution.py:379
  152.3 4.6 %collective-permute-start = (bf16[1,64,512]{2,1,0:T(8,128)(2,1)S(1)}, bf16[1,64,512]{2,1,0:T(8,128)(2,1)S(1)}, u32[]{:S(2)}, u32[]{:S(2)}) collective-permute-start(bf16[1,64,512]{2,1,0:T(8,128)(2,1)S(1)} %get-tuple-element.45), channel_id=1, source_target_pairs={{0,4},{4,8},{8,12},{1,5},{5,9},{9,13},{2,6},{6,10},{10,14},{3,7},{... | collective-permute-start | bytes 196616 | tf_op jit(solution)/shard_map/ppermute | solution.py:20
  156.9 1.9 collective-permute-start.1
  160.3 3.7 %collective-permute-done.1 = bf16[1,64,512]{2,1,0:T(8,128)(2,1)S(1)} collective-permute-done((bf16[1,64,512]{2,1,0:T(8,128)(2,1)S(1)}, bf16[1,64,512]{2,1,0:T(8,128)(2,1)S(1)}, u32[]{:S(2)}, u32[]{:S(2)}) %collective-permute-start.1) | collective-permute-done | bytes 65568 | tf_op jit(solution)/shard_map/ppermute | solution.py:23
  164.1 1.9 pad_maximum_fusion.rest_0_.rest_1_.rest_2_.rest_3_.rest_4_
  166.0 1.2 slice.98
  167.9 27.2 %shard_map.86 = (f32[13,64,512]{2,1,0:T(8,128)}, bf16[78,64,512]{2,1,0:T(8,128)(2,1)}, bf16[832,256]{1,0:T(8,128)(2,1)}) custom-call(s32[65]{0:T(128)} %reshape.229.ids_ref, s32[65]{0:T(128)} %reshape.230.write_ref, s32[65]{0:T(128)} %reshape.238.valid_ref, s32[1]{0:T(128)S(6)} %add.159.first_ref, bf16[832,512]{1,0:T(8,128)(2,1)} %q_ref.3, ...), custom_call_target="tpu_custom_call" | custom-call | tf_op jit(solution)/shard_map/pallas_call | solution.py:379
  195.0 1.6 slice.104
  196.6 1.8 broadcast_in_dim.2
  198.4 5.4 %scatter_fusion = bf16[36,64,512]{2,1,0:T(8,128)(2,1)} fusion(bf16[36,64,512]{2,1,0:T(8,128)(2,1)} %broadcast_in_dim.2, s32[26]{0:T(128)S(1)} %fusion.20, bf16[26,64,512]{2,1,0:T(8,128)(2,1)S(1)} %slice.104), kind=kCustom, calls=%fused_computation | custom fusion | bytes 5111912 | tf_op jit(solution)/shard_map/scatter | solution.py:471
  203.8 5.5 %all-to-all-start.1 = ((bf16[36,64,512]{2,1,0:T(8,128)(2,1)}), bf16[36,64,512]{2,1,0:T(8,128)(2,1)S(1)}, u32[]{:S(2)}, u32[]{:S(2)}) async-start(bf16[36,64,512]{2,1,0:T(8,128)(2,1)} %scatter_fusion), calls=%async_computation.2 | async-start | bytes 4718592 | tf_op jit(solution)/shard_map/all_to_all | solution.py:473
  210.1 2.8 collective-permute-start.3
  212.9 3.2 %collective-permute-start.2 = (bf16[64,512]{1,0:T(8,128)(2,1)S(1)}, bf16[64,512]{1,0:T(8,128)(2,1)S(1)}, u32[]{:S(2)}, u32[]{:S(2)}) collective-permute-start(bf16[64,512]{1,0:T(8,128)(2,1)S(1)} %get-tuple-element.40), channel_id=1, source_target_pairs={{0,4},{4,8},{8,12},{1,5},{5,9},{9,13},{2,6},{6,10},{10,14},{3,7},{... | collective-permute-start | bytes 196616 | tf_op jit(solution)/shard_map/ppermute | solution.py:486
  217.2 49.2 %all-to-all-done.1 = bf16[36,64,512]{2,1,0:T(8,128)(2,1)S(1)} async-done(((bf16[36,64,512]{2,1,0:T(8,128)(2,1)}), bf16[36,64,512]{2,1,0:T(8,128)(2,1)S(1)}, u32[]{:S(2)}, u32[]{:S(2)}) %all-to-all-start.1) | async-done | bytes 2359328 | tf_op jit(solution)/shard_map/all_to_all | solution.py:473
  266.6 1.9 fusion
  268.6 1.1 copy_add_fusion
  270.0 1.2 copy-done.2
  271.2 1.5 fusion.2
  272.8 1.0 pad_maximum_fusion.5
  (73 shorter events, 12.7 us)
Async XLA Ops:
  7.2 118.0 %all-gather.2.cloned.1.call-start = ((), (), s32[]{:S(2)}) async-start(), calls=%async_computation.3 | async-start | bytes 4259840 | tf_op jit(solution)/shard_map/all_gather | solution.py:428
  8.7 1.8 copy-start
  8.7 1.8 copy-start.1
  8.7 1.0 copy-start.6
  8.8 1.4 copy-start.7
  14.7 108.4 %all-to-all-start = ((bf16[36,64,512]{2,1,0:T(8,128)(2,1)}), bf16[36,64,512]{2,1,0:T(8,128)(2,1)S(1)}, u32[]{:S(2)}, u32[]{:S(2)}) async-start(bf16[36,64,512]{2,1,0:T(8,128)(2,1)} %slice.121), calls=%async_computation | async-start | bytes 4718592 | tf_op jit(solution)/shard_map/all_to_all | solution.py:441
  19.9 250.1 %reduce-scatter.2.cloned.1.call-start = ((), (), s32[]{:S(2)}) async-start(), calls=%async_computation.4 | async-start | bytes 4259840 | tf_op jit(solution)/shard_map/reduce_scatter | solution.py:456
  152.3 8.1 %collective-permute-start = (bf16[1,64,512]{2,1,0:T(8,128)(2,1)S(1)}, bf16[1,64,512]{2,1,0:T(8,128)(2,1)S(1)}, u32[]{:S(2)}, u32[]{:S(2)}) collective-permute-start(bf16[1,64,512]{2,1,0:T(8,128)(2,1)S(1)} %get-tuple-element.45), channel_id=1, source_target_pairs={{0,4},{4,8},{8,12},{1,5},{5,9},{9,13},{2,6},{6,10},{10,14},{3,7},{... | collective-permute-start | bytes 196616 | tf_op jit(solution)/shard_map/ppermute | solution.py:20
  156.9 7.1 %collective-permute-start.1 = (bf16[1,64,512]{2,1,0:T(8,128)(2,1)S(1)}, bf16[1,64,512]{2,1,0:T(8,128)(2,1)S(1)}, u32[]{:S(2)}, u32[]{:S(2)}) collective-permute-start(bf16[1,64,512]{2,1,0:T(8,128)(2,1)S(1)} %get-tuple-element.46), channel_id=1, source_target_pairs={{4,0},{8,4},{12,8},{5,1},{9,5},{13,9},{6,2},{10,6},{14,10},{7,3},{... | collective-permute-start | bytes 196616 | tf_op jit(solution)/shard_map/ppermute | solution.py:23
  203.8 12.4 %copy-start.4 = (bf16[832,256]{1,0:T(8,128)(2,1)S(1)}, bf16[832,256]{1,0:T(8,128)(2,1)}, u32[]{:S(2)}) copy-start(bf16[832,256]{1,0:T(8,128)(2,1)} %get-tuple-element.33) | copy-start | bytes 1277956
  203.8 12.4 %copy-start.5 = (bf16[832,256]{1,0:T(8,128)(2,1)S(1)}, bf16[832,256]{1,0:T(8,128)(2,1)}, u32[]{:S(2)}) copy-start(bf16[832,256]{1,0:T(8,128)(2,1)} %get-tuple-element.35) | copy-start | bytes 1277956
  203.8 62.6 %all-to-all-start.1 = ((bf16[36,64,512]{2,1,0:T(8,128)(2,1)}), bf16[36,64,512]{2,1,0:T(8,128)(2,1)S(1)}, u32[]{:S(2)}, u32[]{:S(2)}) async-start(bf16[36,64,512]{2,1,0:T(8,128)(2,1)} %scatter_fusion), calls=%async_computation.2 | async-start | bytes 4718592 | tf_op jit(solution)/shard_map/all_to_all | solution.py:473
  210.1 59.6 %collective-permute-start.3 = (bf16[64,512]{1,0:T(8,128)(2,1)S(1)}, bf16[64,512]{1,0:T(8,128)(2,1)S(1)}, u32[]{:S(2)}, u32[]{:S(2)}) collective-permute-start(bf16[64,512]{1,0:T(8,128)(2,1)S(1)} %get-tuple-element.39), channel_id=1, source_target_pairs={{4,0},{8,4},{12,8},{5,1},{9,5},{13,9},{6,2},{10,6},{14,10},{7,3},{... | collective-permute-start | bytes 196616 | tf_op jit(solution)/shard_map/ppermute | solution.py:485
  212.9 56.7 %collective-permute-start.2 = (bf16[64,512]{1,0:T(8,128)(2,1)S(1)}, bf16[64,512]{1,0:T(8,128)(2,1)S(1)}, u32[]{:S(2)}, u32[]{:S(2)}) collective-permute-start(bf16[64,512]{1,0:T(8,128)(2,1)S(1)} %get-tuple-element.40), channel_id=1, source_target_pairs={{0,4},{4,8},{8,12},{1,5},{5,9},{9,13},{2,6},{6,10},{10,14},{3,7},{... | collective-permute-start | bytes 196616 | tf_op jit(solution)/shard_map/ppermute | solution.py:486
  266.6 1.9 copy-start.3
  269.8 1.5 copy-start.2
Sparse Core Ops, SparseCore 0:
  10.1 114.9 all-gather.1
  151.6 81.3 reduce-scatter.1

commit v9 on v8

--- a/solution.py
+++ b/solution.py
@@ -458,19 +458,17 @@
             )
             summed = own_sum.reshape(tokens, 2 * part) + returned.astype(jnp.float32)
         else:
-            extra = blocks_dev * RAND
-            far_rows = (total + jnp.arange(extra, dtype=jnp.int32)).reshape(blocks_dev, RAND)
-            far_write = jnp.concatenate([window, far_rows], axis=1).reshape(-1)
+            slots = seq_size * capacity
+            far_rows = slot_index.reshape(blocks_dev, RAND).astype(jnp.int32)
+            far_write = jnp.concatenate([window + slots, far_rows], axis=1).reshape(-1)
             own_sum, spread, query_out = block_attention(
-                table_ids, far_write, valid, table, queries, out_grad, source, chunk, part,
-                total + extra,
-            )
-            returning = (
-                jnp.zeros((seq_size * capacity, BLOCK, 2 * part), jnp.bfloat16)
-                .at[slot_index]
-                .set(spread[total:])
-            )
-            returned = lax.all_to_all(returning, "seq", split_axis=0, concat_axis=0, tiled=True)
+                table_ids, far_write, valid, table + slots, queries, out_grad, source, chunk,
+                part, slots + total,
+            )
+            returned = lax.all_to_all(
+                spread[:slots], "seq", split_axis=0, concat_axis=0, tiled=True
+            )
+            spread = spread[slots:]
             gathered = jnp.dot(
                 selector.T,
                 returned.reshape(seq_size * capacity, BLOCK * 2 * part),

time: 287 us -> 287 us (level)
  local copies, waits for them, and re-layouts: 21.2 us -> 17.9 us
  waiting for transfers between devices: 155 us -> 158 us
    scatter x1 -> x0, local copies, waits for them, and re-layouts: 5.38 us -> none  [gathered_shards(): returning = jnp.zeros((seq_size * capacity, BLOCK, 2 * part), jnp.bfloat1...]
    slice x1 -> x2, local copies, waits for them, and re-layouts: 1.59 us -> 5.6 us  [the longest x1 3.31 us: gathered_shards(): spread[:slots]]
    all_to_all x1, waiting for transfers between devices: 49.2 us -> 53.2 us  [gathered_shards(): lax.all_to_all(spread[:slots], 'seq', split_axis=0, concat_axis=0, tiled=...]
  transfers between devices with their start and end apart: 8 -> 8, of which waited for: 4 -> 4; matrix products, arithmetic and copies ran while one was open for 10% -> 8% of each run, Pallas kernels for 10% -> 10%
where the time goes in v9:
time: 287 us; the launch traced here: 282 us
  waiting for transfers between devices  158 us (55%)
  Pallas kernels  53.8 us (19%)
  starting transfers between devices  23.1 us (8%)
  local copies, waits for them, and re-layouts  17.9 us (6%)
  between operations  15.6 us (5%)
  other arithmetic  10.3 us (4%)
    all_to_all x1, waiting for transfers between devices, gathered_shards(): lax.all_to_all(outgoing, 'seq', split_axis=0, concat_axis=0, tiled=True)  100 us
    pallas_call x2, Pallas kernels, block_attention(): pl.pallas_call(block_kernel, grid_spec=grid_spec, out_shape=[jax.ShapeDty...  53.8 us
    all_to_all x1, waiting for transfers between devices, gathered_shards(): lax.all_to_all(spread[:slots], 'seq', split_axis=0, concat_axis=0, tiled=...  53.2 us
  transfers between devices with their start and end apart: 8, of which 4 were waited for; matrix products, arithmetic and copies ran while one was open for 8% of the time, Pallas kernels for 10%

profile of v9, /device:TPU:22, one launch (start us, length us, event | category | flops | bytes accessed | tf_op | source)
XLA Modules:
  0.0 281.8 jit_solution(12452803081415378978)
XLA Ops:
  7.2 1.5 fusion.20
  12.1 1.0 copy.51
  13.1 1.6 slice.125
  14.7 5.2 %all-to-all-start = ((bf16[36,64,512]{2,1,0:T(8,128)(2,1)}), bf16[36,64,512]{2,1,0:T(8,128)(2,1)S(1)}, u32[]{:S(2)}, u32[]{:S(2)}) async-start(bf16[36,64,512]{2,1,0:T(8,128)(2,1)} %slice.125), calls=%async_computation | async-start | bytes 4718592 | tf_op jit(solution)/shard_map/all_to_all | solution.py:441
  22.7 100.3 %all-to-all-done = bf16[36,64,512]{2,1,0:T(8,128)(2,1)S(1)} async-done(((bf16[36,64,512]{2,1,0:T(8,128)(2,1)}), bf16[36,64,512]{2,1,0:T(8,128)(2,1)S(1)}, u32[]{:S(2)}, u32[]{:S(2)}) %all-to-all-start) | async-done | bytes 2359328 | tf_op jit(solution)/shard_map/all_to_all | solution.py:441
  125.2 26.2 %shard_map.85 = (f32[13,64,512]{2,1,0:T(8,128)}, bf16[52,64,512]{2,1,0:T(8,128)(2,1)}, bf16[832,256]{1,0:T(8,128)(2,1)}) custom-call(s32[65]{0:T(128)} %reshape.197.ids_ref.write_ref, s32[65]{0:T(128)} %reshape.197.ids_ref.write_ref, s32[65]{0:T(128)} %reshape.210.valid_ref, s32[1]{0:T(128)S(6)} %add.138.first_ref, bf16[832,512]{1,0:T(8,128)(2,1)} %q_ref.3, ...), custom_call_target="tpu_custom_call" | custom-call | tf_op jit(solution)/shard_map/pallas_call | solution.py:379
  152.2 4.7 %collective-permute-start = (bf16[1,64,512]{2,1,0:T(8,128)(2,1)S(1)}, bf16[1,64,512]{2,1,0:T(8,128)(2,1)S(1)}, u32[]{:S(2)}, u32[]{:S(2)}) collective-permute-start(bf16[1,64,512]{2,1,0:T(8,128)(2,1)S(1)} %get-tuple-element.47), channel_id=1, source_target_pairs={{0,4},{4,8},{8,12},{1,5},{5,9},{9,13},{2,6},{6,10},{10,14},{3,7},{... | collective-permute-start | bytes 196616 | tf_op jit(solution)/shard_map/ppermute | solution.py:20
  156.9 1.9 collective-permute-start.1
  160.4 3.6 %collective-permute-done.1 = bf16[1,64,512]{2,1,0:T(8,128)(2,1)S(1)} collective-permute-done((bf16[1,64,512]{2,1,0:T(8,128)(2,1)S(1)}, bf16[1,64,512]{2,1,0:T(8,128)(2,1)S(1)}, u32[]{:S(2)}, u32[]{:S(2)}) %collective-permute-start.1) | collective-permute-done | bytes 65568 | tf_op jit(solution)/shard_map/ppermute | solution.py:23
  164.0 2.0 pad_maximum_fusion.rest_0_.rest_1_.rest_2_.rest_3_.rest_4_
  166.0 1.2 slice.101
  167.8 27.6 %shard_map.86 = (f32[13,64,512]{2,1,0:T(8,128)}, bf16[88,64,512]{2,1,0:T(8,128)(2,1)}, bf16[832,256]{1,0:T(8,128)(2,1)}) custom-call(s32[65]{0:T(128)} %reshape.201.ids_ref, s32[65]{0:T(128)} %reshape.202.write_ref, s32[65]{0:T(128)} %reshape.210.valid_ref, s32[1]{0:T(128)S(6)} %add.147.first_ref, bf16[832,512]{1,0:T(8,128)(2,1)} %q_ref.3, ...), custom_call_target="tpu_custom_call" | custom-call | tf_op jit(solution)/shard_map/pallas_call | solution.py:379
  195.4 3.3 %slice.107 = bf16[36,64,512]{2,1,0:T(8,128)(2,1)} slice(bf16[88,64,512]{2,1,0:T(8,128)(2,1)} %get-tuple-element.38), slice={[0:36], [0:64], [0:512]} | slice | bytes 4718592 | tf_op jit(solution)/shard_map/slice | solution.py:469
  198.7 5.3 %all-to-all-start.1 = ((bf16[36,64,512]{2,1,0:T(8,128)(2,1)}), bf16[36,64,512]{2,1,0:T(8,128)(2,1)S(1)}, u32[]{:S(2)}, u32[]{:S(2)}) async-start(bf16[36,64,512]{2,1,0:T(8,128)(2,1)} %slice.107), calls=%async_computation.2 | async-start | bytes 4718592 | tf_op jit(solution)/shard_map/all_to_all | solution.py:468
  204.0 2.3 slice.109
  206.3 2.8 %collective-permute-start.3 = (bf16[64,512]{1,0:T(8,128)(2,1)S(1)}, bf16[64,512]{1,0:T(8,128)(2,1)S(1)}, u32[]{:S(2)}, u32[]{:S(2)}) collective-permute-start(bf16[64,512]{1,0:T(8,128)(2,1)S(1)} %get-tuple-element.41), channel_id=1, source_target_pairs={{4,0},{8,4},{12,8},{5,1},{9,5},{13,9},{6,2},{10,6},{14,10},{7,3},{... | collective-permute-start | bytes 196616 | tf_op jit(solution)/shard_map/ppermute | solution.py:483
  209.2 3.2 %collective-permute-start.2 = (bf16[64,512]{1,0:T(8,128)(2,1)S(1)}, bf16[64,512]{1,0:T(8,128)(2,1)S(1)}, u32[]{:S(2)}, u32[]{:S(2)}) collective-permute-start(bf16[64,512]{1,0:T(8,128)(2,1)S(1)} %get-tuple-element.42), channel_id=1, source_target_pairs={{0,4},{4,8},{8,12},{1,5},{5,9},{9,13},{2,6},{6,10},{10,14},{3,7},{... | collective-permute-start | bytes 196616 | tf_op jit(solution)/shard_map/ppermute | solution.py:484
  212.4 1.0 pad_maximum_fusion.3
  213.3 53.2 %all-to-all-done.1 = bf16[36,64,512]{2,1,0:T(8,128)(2,1)S(1)} async-done(((bf16[36,64,512]{2,1,0:T(8,128)(2,1)}), bf16[36,64,512]{2,1,0:T(8,128)(2,1)S(1)}, u32[]{:S(2)}, u32[]{:S(2)}) %all-to-all-start.1) | async-done | bytes 2359328 | tf_op jit(solution)/shard_map/all_to_all | solution.py:468
  266.8 1.9 fusion
  268.7 1.1 copy_add_fusion
  270.2 1.2 copy-done.2
  271.4 1.5 fusion.2
  273.0 1.0 pad_maximum_fusion.5
  (81 shorter events, 11.6 us)
Async XLA Ops:
  7.2 118.0 %all-gather.2.cloned.1.call-start = ((), (), s32[]{:S(2)}) async-start(), calls=%async_computation.3 | async-start | bytes 4259840 | tf_op jit(solution)/shard_map/all_gather | solution.py:428
  8.7 1.8 copy-start
  8.7 1.8 copy-start.1
  8.7 1.0 copy-start.6
  8.8 1.4 copy-start.7
  14.7 108.4 %all-to-all-start = ((bf16[36,64,512]{2,1,0:T(8,128)(2,1)}), bf16[36,64,512]{2,1,0:T(8,128)(2,1)S(1)}, u32[]{:S(2)}, u32[]{:S(2)}) async-start(bf16[36,64,512]{2,1,0:T(8,128)(2,1)} %slice.125), calls=%async_computation | async-start | bytes 4718592 | tf_op jit(solution)/shard_map/all_to_all | solution.py:441
  19.9 250.3 %reduce-scatter.2.cloned.1.call-start = ((), (), s32[]{:S(2)}) async-start(), calls=%async_computation.4 | async-start | bytes 4259840 | tf_op jit(solution)/shard_map/reduce_scatter | solution.py:456
  152.2 8.2 %collective-permute-start = (bf16[1,64,512]{2,1,0:T(8,128)(2,1)S(1)}, bf16[1,64,512]{2,1,0:T(8,128)(2,1)S(1)}, u32[]{:S(2)}, u32[]{:S(2)}) collective-permute-start(bf16[1,64,512]{2,1,0:T(8,128)(2,1)S(1)} %get-tuple-element.47), channel_id=1, source_target_pairs={{0,4},{4,8},{8,12},{1,5},{5,9},{9,13},{2,6},{6,10},{10,14},{3,7},{... | collective-permute-start | bytes 196616 | tf_op jit(solution)/shard_map/ppermute | solution.py:20
  156.9 7.1 %collective-permute-start.1 = (bf16[1,64,512]{2,1,0:T(8,128)(2,1)S(1)}, bf16[1,64,512]{2,1,0:T(8,128)(2,1)S(1)}, u32[]{:S(2)}, u32[]{:S(2)}) collective-permute-start(bf16[1,64,512]{2,1,0:T(8,128)(2,1)S(1)} %get-tuple-element.48), channel_id=1, source_target_pairs={{4,0},{8,4},{12,8},{5,1},{9,5},{13,9},{6,2},{10,6},{14,10},{7,3},{... | collective-permute-start | bytes 196616 | tf_op jit(solution)/shard_map/ppermute | solution.py:23
  198.7 67.8 %all-to-all-start.1 = ((bf16[36,64,512]{2,1,0:T(8,128)(2,1)}), bf16[36,64,512]{2,1,0:T(8,128)(2,1)S(1)}, u32[]{:S(2)}, u32[]{:S(2)}) async-start(bf16[36,64,512]{2,1,0:T(8,128)(2,1)} %slice.107), calls=%async_computation.2 | async-start | bytes 4718592 | tf_op jit(solution)/shard_map/all_to_all | solution.py:468
  204.0 8.4 %copy-start.4 = (bf16[832,256]{1,0:T(8,128)(2,1)S(1)}, bf16[832,256]{1,0:T(8,128)(2,1)}, u32[]{:S(2)}) copy-start(bf16[832,256]{1,0:T(8,128)(2,1)} %get-tuple-element.33) | copy-start | bytes 1277956
  204.0 8.4 %copy-start.5 = (bf16[832,256]{1,0:T(8,128)(2,1)S(1)}, bf16[832,256]{1,0:T(8,128)(2,1)}, u32[]{:S(2)}) copy-start(bf16[832,256]{1,0:T(8,128)(2,1)} %get-tuple-element.35) | copy-start | bytes 1277956
  206.3 63.6 %collective-permute-start.3 = (bf16[64,512]{1,0:T(8,128)(2,1)S(1)}, bf16[64,512]{1,0:T(8,128)(2,1)S(1)}, u32[]{:S(2)}, u32[]{:S(2)}) collective-permute-start(bf16[64,512]{1,0:T(8,128)(2,1)S(1)} %get-tuple-element.41), channel_id=1, source_target_pairs={{4,0},{8,4},{12,8},{5,1},{9,5},{13,9},{6,2},{10,6},{14,10},{7,3},{... | collective-permute-start | bytes 196616 | tf_op jit(solution)/shard_map/ppermute | solution.py:483
  209.2 60.7 %collective-permute-start.2 = (bf16[64,512]{1,0:T(8,128)(2,1)S(1)}, bf16[64,512]{1,0:T(8,128)(2,1)S(1)}, u32[]{:S(2)}, u32[]{:S(2)}) collective-permute-start(bf16[64,512]{1,0:T(8,128)(2,1)S(1)} %get-tuple-element.42), channel_id=1, source_target_pairs={{0,4},{4,8},{8,12},{1,5},{5,9},{9,13},{2,6},{6,10},{10,14},{3,7},{... | collective-permute-start | bytes 196616 | tf_op jit(solution)/shard_map/ppermute | solution.py:484
  266.8 1.9 copy-start.3
  269.9 1.5 copy-start.2
Sparse Core Ops, SparseCore 0:
  10.1 114.9 all-gather.1
  151.5 84.1 reduce-scatter.1

commit v10 on v9

--- a/solution.py
+++ b/solution.py
@@ -460,10 +460,11 @@
         else:
             slots = seq_size * capacity
             far_rows = slot_index.reshape(blocks_dev, RAND).astype(jnp.int32)
-            far_write = jnp.concatenate([window + slots, far_rows], axis=1).reshape(-1)
+            near = window - first + 1 + slots
+            far_write = jnp.concatenate([near, far_rows], axis=1).reshape(-1)
             own_sum, spread, query_out = block_attention(
-                table_ids, far_write, valid, table + slots, queries, out_grad, source, chunk,
-                part, slots + total,
+                table_ids, far_write, valid, table - first + 1 + slots, queries, out_grad, source,
+                chunk, part, slots + blocks_dev + 2,
             )
             returned = lax.all_to_all(
                 spread[:slots], "seq", split_axis=0, concat_axis=0, tiled=True
@@ -474,12 +475,8 @@
                 returned.reshape(seq_size * capacity, BLOCK * 2 * part),
                 preferred_element_type=jnp.float32,
             ).reshape(blocks_dev, BLOCK, 2 * part)
-            left_edge = lax.dynamic_index_in_dim(
-                spread, jnp.clip(first - 1, 0, total - 1), 0, keepdims=False
-            )
-            right_edge = lax.dynamic_index_in_dim(
-                spread, jnp.clip(first + blocks_dev, 0, total - 1), 0, keepdims=False
-            )
+            left_edge = spread[0]
+            right_edge = spread[blocks_dev + 1]
             from_right = lax.ppermute(left_edge, "seq", [(i, i - 1) for i in range(1, seq_size)])
             from_left = lax.ppermute(right_edge, "seq", [(i, i + 1) for i in range(seq_size - 1)])
             combined = (

time: 287 us -> 287 us (level)
  waiting for transfers between devices: 158 us -> 161 us
  transfers between devices with their start and end apart: 8 -> 8, of which waited for: 4 -> 4; matrix products, arithmetic and copies ran while one was open for 8% -> 8% of each run, Pallas kernels for 10% -> 9%
where the time goes in v10:
time: 287 us; the launch traced here: 282 us
  waiting for transfers between devices  161 us (56%)
  Pallas kernels  52.4 us (18%)
  starting transfers between devices  23.2 us (8%)
  local copies, waits for them, and re-layouts  16.6 us (6%)
  between operations  15.7 us (5%)
  other arithmetic  10.3 us (4%)
    all_to_all x1, waiting for transfers between devices, gathered_shards(): lax.all_to_all(outgoing, 'seq', split_axis=0, concat_axis=0, tiled=True)  100 us
    all_to_all x1, waiting for transfers between devices, gathered_shards(): lax.all_to_all(spread[:slots], 'seq', split_axis=0, concat_axis=0, tiled=...  55.9 us
    pallas_call x2, Pallas kernels, block_attention(): pl.pallas_call(block_kernel, grid_spec=grid_spec, out_shape=[jax.ShapeDty...  52.4 us
  transfers between devices with their start and end apart: 8, of which 4 were waited for; matrix products, arithmetic and copies ran while one was open for 8% of the time, Pallas kernels for 9%

profile of v10, /device:TPU:22, one launch (start us, length us, event | category | flops | bytes accessed | tf_op | source)
XLA Modules:
  0.0 281.9 jit_solution(10732259214365623205)
XLA Ops:
  7.2 1.5 fusion.21
  8.8 1.0 pad_maximum_fusion.2
  12.1 1.0 copy.51
  13.1 1.6 slice.132
  14.7 5.2 %all-to-all-start = ((bf16[36,64,512]{2,1,0:T(8,128)(2,1)}), bf16[36,64,512]{2,1,0:T(8,128)(2,1)S(1)}, u32[]{:S(2)}, u32[]{:S(2)}) async-start(bf16[36,64,512]{2,1,0:T(8,128)(2,1)} %slice.132), calls=%async_computation | async-start | bytes 4718592 | tf_op jit(solution)/shard_map/all_to_all | solution.py:441
  22.8 100.3 %all-to-all-done = bf16[36,64,512]{2,1,0:T(8,128)(2,1)S(1)} async-done(((bf16[36,64,512]{2,1,0:T(8,128)(2,1)}), bf16[36,64,512]{2,1,0:T(8,128)(2,1)S(1)}, u32[]{:S(2)}, u32[]{:S(2)}) %all-to-all-start) | async-done | bytes 2359328 | tf_op jit(solution)/shard_map/all_to_all | solution.py:441
  125.2 26.2 %shard_map.85 = (f32[13,64,512]{2,1,0:T(8,128)}, bf16[52,64,512]{2,1,0:T(8,128)(2,1)}, bf16[832,256]{1,0:T(8,128)(2,1)}) custom-call(s32[65]{0:T(128)} %reshape.199.ids_ref.write_ref, s32[65]{0:T(128)} %reshape.199.ids_ref.write_ref, s32[65]{0:T(128)} %reshape.212.valid_ref, s32[1]{0:T(128)S(6)} %add.138.first_ref, bf16[832,512]{1,0:T(8,128)(2,1)} %q_ref.3, ...), custom_call_target="tpu_custom_call" | custom-call | tf_op jit(solution)/shard_map/pallas_call | solution.py:379
  152.3 4.6 %collective-permute-start = (bf16[1,64,512]{2,1,0:T(8,128)(2,1)S(1)}, bf16[1,64,512]{2,1,0:T(8,128)(2,1)S(1)}, u32[]{:S(2)}, u32[]{:S(2)}) collective-permute-start(bf16[1,64,512]{2,1,0:T(8,128)(2,1)S(1)} %get-tuple-element.47), channel_id=1, source_target_pairs={{0,4},{4,8},{8,12},{1,5},{5,9},{9,13},{2,6},{6,10},{10,14},{3,7},{... | collective-permute-start | bytes 196616 | tf_op jit(solution)/shard_map/ppermute | solution.py:20
  156.9 1.9 collective-permute-start.1
  160.5 3.6 %collective-permute-done.1 = bf16[1,64,512]{2,1,0:T(8,128)(2,1)S(1)} collective-permute-done((bf16[1,64,512]{2,1,0:T(8,128)(2,1)S(1)}, bf16[1,64,512]{2,1,0:T(8,128)(2,1)S(1)}, u32[]{:S(2)}, u32[]{:S(2)}) %collective-permute-start.1) | collective-permute-done | bytes 65568 | tf_op jit(solution)/shard_map/ppermute | solution.py:23
  164.1 1.9 pad_maximum_fusion.rest_0_.rest_1_.rest_2_.rest_3_.rest_4_
  166.0 1.2 slice.107
  167.8 26.2 %shard_map.86 = (f32[13,64,512]{2,1,0:T(8,128)}, bf16[51,64,512]{2,1,0:T(8,128)(2,1)}, bf16[832,256]{1,0:T(8,128)(2,1)}) custom-call(s32[65]{0:T(128)} %reshape.203.ids_ref, s32[65]{0:T(128)} %reshape.204.write_ref, s32[65]{0:T(128)} %reshape.212.valid_ref, s32[1]{0:T(128)} %bitcast.3.first_ref, bf16[832,512]{1,0:T(8,128)(2,1)} %q_ref.3, ...), custom_call_target="tpu_custom_call" | custom-call | tf_op jit(solution)/shard_map/pallas_call | solution.py:379
  194.1 3.4 %slice.113 = bf16[36,64,512]{2,1,0:T(8,128)(2,1)} slice(bf16[51,64,512]{2,1,0:T(8,128)(2,1)} %get-tuple-element.38), slice={[0:36], [0:64], [0:512]} | slice | bytes 4718592 | tf_op jit(solution)/shard_map/slice | solution.py:470
  197.4 5.4 %all-to-all-start.1 = ((bf16[36,64,512]{2,1,0:T(8,128)(2,1)}), bf16[36,64,512]{2,1,0:T(8,128)(2,1)S(1)}, u32[]{:S(2)}, u32[]{:S(2)}) async-start(bf16[36,64,512]{2,1,0:T(8,128)(2,1)} %slice.113), calls=%async_computation.2 | async-start | bytes 4718592 | tf_op jit(solution)/shard_map/all_to_all | solution.py:469
  203.7 2.8 collective-permute-start.3
  206.6 3.2 %collective-permute-start.2 = (bf16[64,512]{1,0:T(8,128)(2,1)S(1)}, bf16[64,512]{1,0:T(8,128)(2,1)S(1)}, u32[]{:S(2)}, u32[]{:S(2)}) collective-permute-start(bf16[64,512]{1,0:T(8,128)(2,1)S(1)} %get-tuple-element.42), channel_id=1, source_target_pairs={{0,4},{4,8},{8,12},{1,5},{5,9},{9,13},{2,6},{6,10},{10,14},{3,7},{... | collective-permute-start | bytes 196616 | tf_op jit(solution)/shard_map/ppermute | solution.py:481
  209.8 1.0 pad_maximum_fusion.3
  210.8 55.9 %all-to-all-done.1 = bf16[36,64,512]{2,1,0:T(8,128)(2,1)S(1)} async-done(((bf16[36,64,512]{2,1,0:T(8,128)(2,1)}), bf16[36,64,512]{2,1,0:T(8,128)(2,1)S(1)}, u32[]{:S(2)}, u32[]{:S(2)}) %all-to-all-start.1) | async-done | bytes 2359328 | tf_op jit(solution)/shard_map/all_to_all | solution.py:469
  266.9 1.9 fusion
  268.8 1.1 copy_add_fusion
  270.2 1.2 copy-done.2
  271.5 1.5 fusion.2
  273.1 1.0 pad_maximum_fusion.5
  (80 shorter events, 11.5 us)
Async XLA Ops:
  7.2 118.0 %all-gather.2.cloned.1.call-start = ((), (), s32[]{:S(2)}) async-start(), calls=%async_computation.3 | async-start | bytes 4259840 | tf_op jit(solution)/shard_map/all_gather | solution.py:428
  8.7 1.8 copy-start
  8.8 1.8 copy-start.1
  8.8 1.0 copy-start.6
  8.8 1.4 copy-start.7
  14.7 108.4 %all-to-all-start = ((bf16[36,64,512]{2,1,0:T(8,128)(2,1)}), bf16[36,64,512]{2,1,0:T(8,128)(2,1)S(1)}, u32[]{:S(2)}, u32[]{:S(2)}) async-start(bf16[36,64,512]{2,1,0:T(8,128)(2,1)} %slice.132), calls=%async_computation | async-start | bytes 4718592 | tf_op jit(solution)/shard_map/all_to_all | solution.py:441
  19.9 250.4 %reduce-scatter.2.cloned.1.call-start = ((), (), s32[]{:S(2)}) async-start(), calls=%async_computation.4 | async-start | bytes 4259840 | tf_op jit(solution)/shard_map/reduce_scatter | solution.py:456
  152.3 8.2 %collective-permute-start = (bf16[1,64,512]{2,1,0:T(8,128)(2,1)S(1)}, bf16[1,64,512]{2,1,0:T(8,128)(2,1)S(1)}, u32[]{:S(2)}, u32[]{:S(2)}) collective-permute-start(bf16[1,64,512]{2,1,0:T(8,128)(2,1)S(1)} %get-tuple-element.47), channel_id=1, source_target_pairs={{0,4},{4,8},{8,12},{1,5},{5,9},{9,13},{2,6},{6,10},{10,14},{3,7},{... | collective-permute-start | bytes 196616 | tf_op jit(solution)/shard_map/ppermute | solution.py:20
  156.9 7.1 %collective-permute-start.1 = (bf16[1,64,512]{2,1,0:T(8,128)(2,1)S(1)}, bf16[1,64,512]{2,1,0:T(8,128)(2,1)S(1)}, u32[]{:S(2)}, u32[]{:S(2)}) collective-permute-start(bf16[1,64,512]{2,1,0:T(8,128)(2,1)S(1)} %get-tuple-element.48), channel_id=1, source_target_pairs={{4,0},{8,4},{12,8},{5,1},{9,5},{13,9},{6,2},{10,6},{14,10},{7,3},{... | collective-permute-start | bytes 196616 | tf_op jit(solution)/shard_map/ppermute | solution.py:23
  197.4 12.3 %copy-start.4 = (bf16[832,256]{1,0:T(8,128)(2,1)S(1)}, bf16[832,256]{1,0:T(8,128)(2,1)}, u32[]{:S(2)}) copy-start(bf16[832,256]{1,0:T(8,128)(2,1)} %get-tuple-element.33) | copy-start | bytes 1277956
  197.4 12.3 %copy-start.5 = (bf16[832,256]{1,0:T(8,128)(2,1)S(1)}, bf16[832,256]{1,0:T(8,128)(2,1)}, u32[]{:S(2)}) copy-start(bf16[832,256]{1,0:T(8,128)(2,1)} %get-tuple-element.35) | copy-start | bytes 1277956
  197.4 69.2 %all-to-all-start.1 = ((bf16[36,64,512]{2,1,0:T(8,128)(2,1)}), bf16[36,64,512]{2,1,0:T(8,128)(2,1)S(1)}, u32[]{:S(2)}, u32[]{:S(2)}) async-start(bf16[36,64,512]{2,1,0:T(8,128)(2,1)} %slice.113), calls=%async_computation.2 | async-start | bytes 4718592 | tf_op jit(solution)/shard_map/all_to_all | solution.py:469
  203.7 66.2 %collective-permute-start.3 = (bf16[64,512]{1,0:T(8,128)(2,1)S(1)}, bf16[64,512]{1,0:T(8,128)(2,1)S(1)}, u32[]{:S(2)}, u32[]{:S(2)}) collective-permute-start(bf16[64,512]{1,0:T(8,128)(2,1)S(1)} %get-tuple-element.41), channel_id=1, source_target_pairs={{4,0},{8,4},{12,8},{5,1},{9,5},{13,9},{6,2},{10,6},{14,10},{7,3},{... | collective-permute-start | bytes 196616 | tf_op jit(solution)/shard_map/ppermute | solution.py:480
  206.6 63.4 %collective-permute-start.2 = (bf16[64,512]{1,0:T(8,128)(2,1)S(1)}, bf16[64,512]{1,0:T(8,128)(2,1)S(1)}, u32[]{:S(2)}, u32[]{:S(2)}) collective-permute-start(bf16[64,512]{1,0:T(8,128)(2,1)S(1)} %get-tuple-element.42), channel_id=1, source_target_pairs={{0,4},{4,8},{8,12},{1,5},{5,9},{9,13},{2,6},{6,10},{10,14},{3,7},{... | collective-permute-start | bytes 196616 | tf_op jit(solution)/shard_map/ppermute | solution.py:481
  266.9 1.9 copy-start.3
  270.0 1.5 copy-start.2
Sparse Core Ops, SparseCore 0:
  10.1 115.0 all-gather.1
  151.5 84.4 reduce-scatter.1

commit v11 on v10

--- a/solution.py
+++ b/solution.py
@@ -297,7 +297,7 @@
         acc_ref[...] = jnp.zeros(acc_ref.shape, jnp.float32)
 
     context = jnp.concatenate([ref[0] for ref in kv_refs], axis=0)
-    slot_of = lax.broadcasted_iota(jnp.int32, (SLOTS * BLOCK, 1), 0) // BLOCK
+    slot_of = lax.broadcasted_iota(jnp.int32, (1, SLOTS * BLOCK), 1) // BLOCK
     usable = slot_of < 0
     for slot in range(SLOTS):
         usable = usable | ((slot_of == slot) & (valid_ref[step * SLOTS + slot] > 0))
@@ -310,31 +310,37 @@
         keys = context[:, cols]
         values = context[:, vcols]
         logits = lax.dot_general(
-            keys, query, (((1,), (1,)), ((), ())), preferred_element_type=jnp.float32
+            query, keys, (((1,), (1,)), ((), ())), preferred_element_type=jnp.float32
         ) * logit_scale
         logits = jnp.where(usable, logits, -jnp.inf)
-        row_max = jnp.max(logits, axis=0, keepdims=True)
+        row_max = jnp.max(logits, axis=-1, keepdims=True)
         exponent = jnp.exp(logits - row_max)
-        row_total = jnp.sum(exponent, axis=0, keepdims=True)
+        row_total = jnp.sum(exponent, axis=-1, keepdims=True)
         probability = exponent / row_total
         weights = probability.astype(jnp.bfloat16)
-        attended = lax.dot_general(
-            weights, values, (((0,), (0,)), ((), ())), preferred_element_type=jnp.float32
-        ).astype(jnp.bfloat16)
-        product = grad.astype(jnp.float32) * attended.astype(jnp.float32)
-        row_delta = jnp.sum(product.T, axis=0, keepdims=True)
+        attended = jnp.dot(weights, values, preferred_element_type=jnp.float32).astype(
+            jnp.bfloat16
+        )
+        row_delta = jnp.sum(
+            grad.astype(jnp.float32) * attended.astype(jnp.float32), axis=-1, keepdims=True
+        )
         prob_grad = lax.dot_general(
-            values, grad, (((1,), (1,)), ((), ())), preferred_element_type=jnp.float32
+            grad, values, (((1,), (1,)), ((), ())), preferred_element_type=jnp.float32
         )
         score_grad = (probability * (prob_grad - row_delta)).astype(jnp.bfloat16)
-        query_grad = logit_scale * lax.dot_general(
-            score_grad, keys, (((0,), (0,)), ((), ())), preferred_element_type=jnp.float32
-        )
+        query_grad = logit_scale * jnp.dot(score_grad, keys, preferred_element_type=jnp.float32)
         dq_ref[:, cols] = query_grad.astype(jnp.bfloat16)
         key_parts.append(
-            logit_scale * jnp.dot(score_grad, query, preferred_element_type=jnp.float32)
-        )
-        value_parts.append(jnp.dot(weights, grad, preferred_element_type=jnp.float32))
+            logit_scale
+            * lax.dot_general(
+                score_grad, query, (((0,), (0,)), ((), ())), preferred_element_type=jnp.float32
+            )
+        )
+        value_parts.append(
+            lax.dot_general(
+                weights, grad, (((0,), (0,)), ((), ())), preferred_element_type=jnp.float32
+            )
+        )
     terms = jnp.concatenate(key_parts + value_parts, axis=1)
     for slot in range(SLOTS):
         piece = terms[slot * BLOCK : (slot + 1) * BLOCK]

time: 287 us -> 285 us (level)
  Pallas kernels: 52.4 us -> 48.8 us
    pallas_call x2, Pallas kernels: 52.4 us -> 48.8 us  [block_attention(): pl.pallas_call(block_kernel, grid_spec=grid_spec, out_shape=[jax.ShapeDty...]
where the time goes in v11:
time: 285 us; the launch traced here: 280 us
  waiting for transfers between devices  162 us (57%)
  Pallas kernels  48.8 us (17%)
  starting transfers between devices  23.2 us (8%)
  local copies, waits for them, and re-layouts  16.7 us (6%)
  between operations  15.7 us (6%)
  other arithmetic  10.3 us (4%)
  matrix products  2.86 us (1%)
    all_to_all x1, waiting for transfers between devices, gathered_shards(): lax.all_to_all(outgoing, 'seq', split_axis=0, concat_axis=0, tiled=True)  100 us
    all_to_all x1, waiting for transfers between devices, gathered_shards(): lax.all_to_all(spread[:slots], 'seq', split_axis=0, concat_axis=0, tiled=...  57.2 us
    pallas_call x2, Pallas kernels, block_attention(): pl.pallas_call(block_kernel, grid_spec=grid_spec, out_shape=[jax.ShapeDty...  48.8 us
  transfers between devices with their start and end apart: 8, of which 4 were waited for; matrix products, arithmetic and copies ran while one was open for 8% of the time, Pallas kernels for 9%

profile of v11, /device:TPU:22, one launch (start us, length us, event | category | flops | bytes accessed | tf_op | source)
XLA Modules:
  0.0 279.6 jit_solution(1225782067542608788)
XLA Ops:
  7.2 1.5 fusion.21
  8.8 1.0 pad_maximum_fusion.2
  12.1 1.0 copy.51
  13.1 1.6 slice.132
  14.7 5.2 %all-to-all-start = ((bf16[36,64,512]{2,1,0:T(8,128)(2,1)}), bf16[36,64,512]{2,1,0:T(8,128)(2,1)S(1)}, u32[]{:S(2)}, u32[]{:S(2)}) async-start(bf16[36,64,512]{2,1,0:T(8,128)(2,1)} %slice.132), calls=%async_computation | async-start | bytes 4718592 | tf_op jit(solution)/shard_map/all_to_all | solution.py:447
  22.8 100.3 %all-to-all-done = bf16[36,64,512]{2,1,0:T(8,128)(2,1)S(1)} async-done(((bf16[36,64,512]{2,1,0:T(8,128)(2,1)}), bf16[36,64,512]{2,1,0:T(8,128)(2,1)S(1)}, u32[]{:S(2)}, u32[]{:S(2)}) %all-to-all-start) | async-done | bytes 2359328 | tf_op jit(solution)/shard_map/all_to_all | solution.py:447
  125.2 24.4 %shard_map.85 = (f32[13,64,512]{2,1,0:T(8,128)}, bf16[52,64,512]{2,1,0:T(8,128)(2,1)}, bf16[832,256]{1,0:T(8,128)(2,1)}) custom-call(s32[65]{0:T(128)} %reshape.199.ids_ref.write_ref, s32[65]{0:T(128)} %reshape.199.ids_ref.write_ref, s32[65]{0:T(128)} %reshape.212.valid_ref, s32[1]{0:T(128)S(6)} %add.138.first_ref, bf16[832,512]{1,0:T(8,128)(2,1)} %q_ref.3, ...), custom_call_target="tpu_custom_call" | custom-call | tf_op jit(solution)/shard_map/pallas_call | solution.py:385
  150.4 4.6 %collective-permute-start = (bf16[1,64,512]{2,1,0:T(8,128)(2,1)S(1)}, bf16[1,64,512]{2,1,0:T(8,128)(2,1)S(1)}, u32[]{:S(2)}, u32[]{:S(2)}) collective-permute-start(bf16[1,64,512]{2,1,0:T(8,128)(2,1)S(1)} %get-tuple-element.47), channel_id=1, source_target_pairs={{0,4},{4,8},{8,12},{1,5},{5,9},{9,13},{2,6},{6,10},{10,14},{3,7},{... | collective-permute-start | bytes 196616 | tf_op jit(solution)/shard_map/ppermute | solution.py:20
  155.1 1.9 collective-permute-start.1
  158.6 3.6 %collective-permute-done.1 = bf16[1,64,512]{2,1,0:T(8,128)(2,1)S(1)} collective-permute-done((bf16[1,64,512]{2,1,0:T(8,128)(2,1)S(1)}, bf16[1,64,512]{2,1,0:T(8,128)(2,1)S(1)}, u32[]{:S(2)}, u32[]{:S(2)}) %collective-permute-start.1) | collective-permute-done | bytes 65568 | tf_op jit(solution)/shard_map/ppermute | solution.py:23
  162.2 1.9 pad_maximum_fusion.rest_0_.rest_1_.rest_2_.rest_3_.rest_4_
  164.2 1.2 slice.107
  166.0 24.4 %shard_map.86 = (f32[13,64,512]{2,1,0:T(8,128)}, bf16[51,64,512]{2,1,0:T(8,128)(2,1)}, bf16[832,256]{1,0:T(8,128)(2,1)}) custom-call(s32[65]{0:T(128)} %reshape.203.ids_ref, s32[65]{0:T(128)} %reshape.204.write_ref, s32[65]{0:T(128)} %reshape.212.valid_ref, s32[1]{0:T(128)} %bitcast.3.first_ref, bf16[832,512]{1,0:T(8,128)(2,1)} %q_ref.3, ...), custom_call_target="tpu_custom_call" | custom-call | tf_op jit(solution)/shard_map/pallas_call | solution.py:385
  190.4 3.4 %slice.113 = bf16[36,64,512]{2,1,0:T(8,128)(2,1)} slice(bf16[51,64,512]{2,1,0:T(8,128)(2,1)} %get-tuple-element.38), slice={[0:36], [0:64], [0:512]} | slice | bytes 4718592 | tf_op jit(solution)/shard_map/slice | solution.py:476
  193.8 5.4 %all-to-all-start.1 = ((bf16[36,64,512]{2,1,0:T(8,128)(2,1)}), bf16[36,64,512]{2,1,0:T(8,128)(2,1)S(1)}, u32[]{:S(2)}, u32[]{:S(2)}) async-start(bf16[36,64,512]{2,1,0:T(8,128)(2,1)} %slice.113), calls=%async_computation.2 | async-start | bytes 4718592 | tf_op jit(solution)/shard_map/all_to_all | solution.py:475
  200.1 2.8 %collective-permute-start.3 = (bf16[64,512]{1,0:T(8,128)(2,1)S(1)}, bf16[64,512]{1,0:T(8,128)(2,1)S(1)}, u32[]{:S(2)}, u32[]{:S(2)}) collective-permute-start(bf16[64,512]{1,0:T(8,128)(2,1)S(1)} %get-tuple-element.41), channel_id=1, source_target_pairs={{4,0},{8,4},{12,8},{5,1},{9,5},{13,9},{6,2},{10,6},{14,10},{7,3},{... | collective-permute-start | bytes 196616 | tf_op jit(solution)/shard_map/ppermute | solution.py:486
  202.9 3.2 %collective-permute-start.2 = (bf16[64,512]{1,0:T(8,128)(2,1)S(1)}, bf16[64,512]{1,0:T(8,128)(2,1)S(1)}, u32[]{:S(2)}, u32[]{:S(2)}) collective-permute-start(bf16[64,512]{1,0:T(8,128)(2,1)S(1)} %get-tuple-element.42), channel_id=1, source_target_pairs={{0,4},{4,8},{8,12},{1,5},{5,9},{9,13},{2,6},{6,10},{10,14},{3,7},{... | collective-permute-start | bytes 196616 | tf_op jit(solution)/shard_map/ppermute | solution.py:487
  206.1 1.0 pad_maximum_fusion.3
  207.1 57.2 %all-to-all-done.1 = bf16[36,64,512]{2,1,0:T(8,128)(2,1)S(1)} async-done(((bf16[36,64,512]{2,1,0:T(8,128)(2,1)}), bf16[36,64,512]{2,1,0:T(8,128)(2,1)S(1)}, u32[]{:S(2)}, u32[]{:S(2)}) %all-to-all-start.1) | async-done | bytes 2359328 | tf_op jit(solution)/shard_map/all_to_all | solution.py:475
  264.6 1.9 fusion
  266.5 1.1 copy_add_fusion
  267.9 1.2 copy-done.2
  269.2 1.5 fusion.2
  270.8 1.0 pad_maximum_fusion.5
  (80 shorter events, 11.5 us)
Async XLA Ops:
  7.2 118.0 %all-gather.2.cloned.1.call-start = ((), (), s32[]{:S(2)}) async-start(), calls=%async_computation.3 | async-start | bytes 4259840 | tf_op jit(solution)/shard_map/all_gather | solution.py:434
  8.7 1.8 copy-start
  8.8 1.8 copy-start.1
  8.8 1.0 copy-start.6
  8.8 1.4 copy-start.7
  14.7 108.4 %all-to-all-start = ((bf16[36,64,512]{2,1,0:T(8,128)(2,1)}), bf16[36,64,512]{2,1,0:T(8,128)(2,1)S(1)}, u32[]{:S(2)}, u32[]{:S(2)}) async-start(bf16[36,64,512]{2,1,0:T(8,128)(2,1)} %slice.132), calls=%async_computation | async-start | bytes 4718592 | tf_op jit(solution)/shard_map/all_to_all | solution.py:447
  19.9 248.1 %reduce-scatter.2.cloned.1.call-start = ((), (), s32[]{:S(2)}) async-start(), calls=%async_computation.4 | async-start | bytes 4259840 | tf_op jit(solution)/shard_map/reduce_scatter | solution.py:462
  150.4 8.2 %collective-permute-start = (bf16[1,64,512]{2,1,0:T(8,128)(2,1)S(1)}, bf16[1,64,512]{2,1,0:T(8,128)(2,1)S(1)}, u32[]{:S(2)}, u32[]{:S(2)}) collective-permute-start(bf16[1,64,512]{2,1,0:T(8,128)(2,1)S(1)} %get-tuple-element.47), channel_id=1, source_target_pairs={{0,4},{4,8},{8,12},{1,5},{5,9},{9,13},{2,6},{6,10},{10,14},{3,7},{... | collective-permute-start | bytes 196616 | tf_op jit(solution)/shard_map/ppermute | solution.py:20
  155.1 7.1 %collective-permute-start.1 = (bf16[1,64,512]{2,1,0:T(8,128)(2,1)S(1)}, bf16[1,64,512]{2,1,0:T(8,128)(2,1)S(1)}, u32[]{:S(2)}, u32[]{:S(2)}) collective-permute-start(bf16[1,64,512]{2,1,0:T(8,128)(2,1)S(1)} %get-tuple-element.48), channel_id=1, source_target_pairs={{4,0},{8,4},{12,8},{5,1},{9,5},{13,9},{6,2},{10,6},{14,10},{7,3},{... | collective-permute-start | bytes 196616 | tf_op jit(solution)/shard_map/ppermute | solution.py:23
  193.8 12.3 %copy-start.4 = (bf16[832,256]{1,0:T(8,128)(2,1)S(1)}, bf16[832,256]{1,0:T(8,128)(2,1)}, u32[]{:S(2)}) copy-start(bf16[832,256]{1,0:T(8,128)(2,1)} %get-tuple-element.33) | copy-start | bytes 1277956
  193.8 12.3 %copy-start.5 = (bf16[832,256]{1,0:T(8,128)(2,1)S(1)}, bf16[832,256]{1,0:T(8,128)(2,1)}, u32[]{:S(2)}) copy-start(bf16[832,256]{1,0:T(8,128)(2,1)} %get-tuple-element.35) | copy-start | bytes 1277956
  193.8 70.5 %all-to-all-start.1 = ((bf16[36,64,512]{2,1,0:T(8,128)(2,1)}), bf16[36,64,512]{2,1,0:T(8,128)(2,1)S(1)}, u32[]{:S(2)}, u32[]{:S(2)}) async-start(bf16[36,64,512]{2,1,0:T(8,128)(2,1)} %slice.113), calls=%async_computation.2 | async-start | bytes 4718592 | tf_op jit(solution)/shard_map/all_to_all | solution.py:475
  200.1 67.6 %collective-permute-start.3 = (bf16[64,512]{1,0:T(8,128)(2,1)S(1)}, bf16[64,512]{1,0:T(8,128)(2,1)S(1)}, u32[]{:S(2)}, u32[]{:S(2)}) collective-permute-start(bf16[64,512]{1,0:T(8,128)(2,1)S(1)} %get-tuple-element.41), channel_id=1, source_target_pairs={{4,0},{8,4},{12,8},{5,1},{9,5},{13,9},{6,2},{10,6},{14,10},{7,3},{... | collective-permute-start | bytes 196616 | tf_op jit(solution)/shard_map/ppermute | solution.py:486
  202.9 64.7 %collective-permute-start.2 = (bf16[64,512]{1,0:T(8,128)(2,1)S(1)}, bf16[64,512]{1,0:T(8,128)(2,1)S(1)}, u32[]{:S(2)}, u32[]{:S(2)}) collective-permute-start(bf16[64,512]{1,0:T(8,128)(2,1)S(1)} %get-tuple-element.42), channel_id=1, source_target_pairs={{0,4},{4,8},{8,12},{1,5},{5,9},{9,13},{2,6},{6,10},{10,14},{3,7},{... | collective-permute-start | bytes 196616 | tf_op jit(solution)/shard_map/ppermute | solution.py:487
  264.6 1.9 copy-start.3
  267.7 1.5 copy-start.2
Sparse Core Ops, SparseCore 0:
  10.1 115.0 all-gather.1
  149.7 85.2 reduce-scatter.1

commit v12 on v11

--- a/solution.py
+++ b/solution.py
@@ -341,13 +341,16 @@
                 weights, grad, (((0,), (0,)), ((), ())), preferred_element_type=jnp.float32
             )
         )
-    terms = jnp.concatenate(key_parts + value_parts, axis=1)
     for slot in range(SLOTS):
-        piece = terms[slot * BLOCK : (slot + 1) * BLOCK]
-        if slot >= 3:
-            piece = piece.astype(jnp.bfloat16).astype(jnp.float32)
         target = write_ref[step * SLOTS + slot]
-        acc_ref[target] = acc_ref[target] + piece
+        rows = slice(slot * BLOCK, (slot + 1) * BLOCK)
+        for head in range(width // DH):
+            for parts, base in ((key_parts, 0), (value_parts, width)):
+                piece = parts[head][rows]
+                if slot >= 3:
+                    piece = piece.astype(jnp.bfloat16).astype(jnp.float32)
+                cols = pl.ds(base + head * DH, DH)
+                acc_ref[target, :, cols] = acc_ref[target, :, cols] + piece
 
     @pl.when(step == steps - 1)
     def _():

time: 285 us -> 285 us (level)
  no operation moved by 1% of the time
where the time goes in v12:
time: 285 us; the launch traced here: 280 us
  waiting for transfers between devices  162 us (57%)
  Pallas kernels  48.8 us (17%)
  starting transfers between devices  23.2 us (8%)
  local copies, waits for them, and re-layouts  16.7 us (6%)
  between operations  15.7 us (6%)
  other arithmetic  10.3 us (4%)
  matrix products  2.86 us (1%)
    all_to_all x1, waiting for transfers between devices, gathered_shards(): lax.all_to_all(outgoing, 'seq', split_axis=0, concat_axis=0, tiled=True)  100 us
    all_to_all x1, waiting for transfers between devices, gathered_shards(): lax.all_to_all(spread[:slots], 'seq', split_axis=0, concat_axis=0, tiled=...  57.2 us
    pallas_call x2, Pallas kernels, block_attention(): pl.pallas_call(block_kernel, grid_spec=grid_spec, out_shape=[jax.ShapeDty...  48.8 us
  transfers between devices with their start and end apart: 8, of which 4 were waited for; matrix products, arithmetic and copies ran while one was open for 8% of the time, Pallas kernels for 9%

profile of v12, /device:TPU:22, one launch (start us, length us, event | category | flops | bytes accessed | tf_op | source)
XLA Modules:
  0.0 279.6 jit_solution(46072613443243832)
XLA Ops:
  7.2 1.5 fusion.21
  8.8 1.0 pad_maximum_fusion.2
  12.1 1.0 copy.51
  13.1 1.6 slice.132
  14.7 5.2 %all-to-all-start = ((bf16[36,64,512]{2,1,0:T(8,128)(2,1)}), bf16[36,64,512]{2,1,0:T(8,128)(2,1)S(1)}, u32[]{:S(2)}, u32[]{:S(2)}) async-start(bf16[36,64,512]{2,1,0:T(8,128)(2,1)} %slice.132), calls=%async_computation | async-start | bytes 4718592 | tf_op jit(solution)/shard_map/all_to_all | solution.py:450
  22.8 100.3 %all-to-all-done = bf16[36,64,512]{2,1,0:T(8,128)(2,1)S(1)} async-done(((bf16[36,64,512]{2,1,0:T(8,128)(2,1)}), bf16[36,64,512]{2,1,0:T(8,128)(2,1)S(1)}, u32[]{:S(2)}, u32[]{:S(2)}) %all-to-all-start) | async-done | bytes 2359328 | tf_op jit(solution)/shard_map/all_to_all | solution.py:450
  125.2 24.4 %shard_map.85 = (f32[13,64,512]{2,1,0:T(8,128)}, bf16[52,64,512]{2,1,0:T(8,128)(2,1)}, bf16[832,256]{1,0:T(8,128)(2,1)}) custom-call(s32[65]{0:T(128)} %reshape.199.ids_ref.write_ref, s32[65]{0:T(128)} %reshape.199.ids_ref.write_ref, s32[65]{0:T(128)} %reshape.212.valid_ref, s32[1]{0:T(128)S(6)} %add.138.first_ref, bf16[832,512]{1,0:T(8,128)(2,1)} %q_ref.3, ...), custom_call_target="tpu_custom_call" | custom-call | tf_op jit(solution)/shard_map/pallas_call | solution.py:388
  150.4 4.6 %collective-permute-start = (bf16[1,64,512]{2,1,0:T(8,128)(2,1)S(1)}, bf16[1,64,512]{2,1,0:T(8,128)(2,1)S(1)}, u32[]{:S(2)}, u32[]{:S(2)}) collective-permute-start(bf16[1,64,512]{2,1,0:T(8,128)(2,1)S(1)} %get-tuple-element.47), channel_id=1, source_target_pairs={{0,4},{4,8},{8,12},{1,5},{5,9},{9,13},{2,6},{6,10},{10,14},{3,7},{... | collective-permute-start | bytes 196616 | tf_op jit(solution)/shard_map/ppermute | solution.py:20
  155.1 1.9 collective-permute-start.1
  158.6 3.6 %collective-permute-done.1 = bf16[1,64,512]{2,1,0:T(8,128)(2,1)S(1)} collective-permute-done((bf16[1,64,512]{2,1,0:T(8,128)(2,1)S(1)}, bf16[1,64,512]{2,1,0:T(8,128)(2,1)S(1)}, u32[]{:S(2)}, u32[]{:S(2)}) %collective-permute-start.1) | collective-permute-done | bytes 65568 | tf_op jit(solution)/shard_map/ppermute | solution.py:23
  162.2 1.9 pad_maximum_fusion.rest_0_.rest_1_.rest_2_.rest_3_.rest_4_
  164.2 1.2 slice.107
  166.0 24.4 %shard_map.86 = (f32[13,64,512]{2,1,0:T(8,128)}, bf16[51,64,512]{2,1,0:T(8,128)(2,1)}, bf16[832,256]{1,0:T(8,128)(2,1)}) custom-call(s32[65]{0:T(128)} %reshape.203.ids_ref, s32[65]{0:T(128)} %reshape.204.write_ref, s32[65]{0:T(128)} %reshape.212.valid_ref, s32[1]{0:T(128)} %bitcast.3.first_ref, bf16[832,512]{1,0:T(8,128)(2,1)} %q_ref.3, ...), custom_call_target="tpu_custom_call" | custom-call | tf_op jit(solution)/shard_map/pallas_call | solution.py:388
  190.4 3.4 %slice.113 = bf16[36,64,512]{2,1,0:T(8,128)(2,1)} slice(bf16[51,64,512]{2,1,0:T(8,128)(2,1)} %get-tuple-element.38), slice={[0:36], [0:64], [0:512]} | slice | bytes 4718592 | tf_op jit(solution)/shard_map/slice | solution.py:479
  193.8 5.4 %all-to-all-start.1 = ((bf16[36,64,512]{2,1,0:T(8,128)(2,1)}), bf16[36,64,512]{2,1,0:T(8,128)(2,1)S(1)}, u32[]{:S(2)}, u32[]{:S(2)}) async-start(bf16[36,64,512]{2,1,0:T(8,128)(2,1)} %slice.113), calls=%async_computation.2 | async-start | bytes 4718592 | tf_op jit(solution)/shard_map/all_to_all | solution.py:478
  200.1 2.8 %collective-permute-start.3 = (bf16[64,512]{1,0:T(8,128)(2,1)S(1)}, bf16[64,512]{1,0:T(8,128)(2,1)S(1)}, u32[]{:S(2)}, u32[]{:S(2)}) collective-permute-start(bf16[64,512]{1,0:T(8,128)(2,1)S(1)} %get-tuple-element.41), channel_id=1, source_target_pairs={{4,0},{8,4},{12,8},{5,1},{9,5},{13,9},{6,2},{10,6},{14,10},{7,3},{... | collective-permute-start | bytes 196616 | tf_op jit(solution)/shard_map/ppermute | solution.py:489
  202.9 3.2 %collective-permute-start.2 = (bf16[64,512]{1,0:T(8,128)(2,1)S(1)}, bf16[64,512]{1,0:T(8,128)(2,1)S(1)}, u32[]{:S(2)}, u32[]{:S(2)}) collective-permute-start(bf16[64,512]{1,0:T(8,128)(2,1)S(1)} %get-tuple-element.42), channel_id=1, source_target_pairs={{0,4},{4,8},{8,12},{1,5},{5,9},{9,13},{2,6},{6,10},{10,14},{3,7},{... | collective-permute-start | bytes 196616 | tf_op jit(solution)/shard_map/ppermute | solution.py:490
  206.2 1.0 pad_maximum_fusion.3
  207.1 57.2 %all-to-all-done.1 = bf16[36,64,512]{2,1,0:T(8,128)(2,1)S(1)} async-done(((bf16[36,64,512]{2,1,0:T(8,128)(2,1)}), bf16[36,64,512]{2,1,0:T(8,128)(2,1)S(1)}, u32[]{:S(2)}, u32[]{:S(2)}) %all-to-all-start.1) | async-done | bytes 2359328 | tf_op jit(solution)/shard_map/all_to_all | solution.py:478
  264.6 1.9 fusion
  266.5 1.1 copy_add_fusion
  267.9 1.2 copy-done.2
  269.2 1.5 fusion.2
  270.8 1.0 pad_maximum_fusion.5
  (80 shorter events, 11.5 us)
Async XLA Ops:
  7.2 118.0 %all-gather.2.cloned.1.call-start = ((), (), s32[]{:S(2)}) async-start(), calls=%async_computation.3 | async-start | bytes 4259840 | tf_op jit(solution)/shard_map/all_gather | solution.py:437
  8.7 1.8 copy-start
  8.8 1.8 copy-start.1
  8.8 1.0 copy-start.6
  8.8 1.4 copy-start.7
  14.7 108.4 %all-to-all-start = ((bf16[36,64,512]{2,1,0:T(8,128)(2,1)}), bf16[36,64,512]{2,1,0:T(8,128)(2,1)S(1)}, u32[]{:S(2)}, u32[]{:S(2)}) async-start(bf16[36,64,512]{2,1,0:T(8,128)(2,1)} %slice.132), calls=%async_computation | async-start | bytes 4718592 | tf_op jit(solution)/shard_map/all_to_all | solution.py:450
  19.9 248.1 %reduce-scatter.2.cloned.1.call-start = ((), (), s32[]{:S(2)}) async-start(), calls=%async_computation.4 | async-start | bytes 4259840 | tf_op jit(solution)/shard_map/reduce_scatter | solution.py:465
  150.4 8.2 %collective-permute-start = (bf16[1,64,512]{2,1,0:T(8,128)(2,1)S(1)}, bf16[1,64,512]{2,1,0:T(8,128)(2,1)S(1)}, u32[]{:S(2)}, u32[]{:S(2)}) collective-permute-start(bf16[1,64,512]{2,1,0:T(8,128)(2,1)S(1)} %get-tuple-element.47), channel_id=1, source_target_pairs={{0,4},{4,8},{8,12},{1,5},{5,9},{9,13},{2,6},{6,10},{10,14},{3,7},{... | collective-permute-start | bytes 196616 | tf_op jit(solution)/shard_map/ppermute | solution.py:20
  155.1 7.1 %collective-permute-start.1 = (bf16[1,64,512]{2,1,0:T(8,128)(2,1)S(1)}, bf16[1,64,512]{2,1,0:T(8,128)(2,1)S(1)}, u32[]{:S(2)}, u32[]{:S(2)}) collective-permute-start(bf16[1,64,512]{2,1,0:T(8,128)(2,1)S(1)} %get-tuple-element.48), channel_id=1, source_target_pairs={{4,0},{8,4},{12,8},{5,1},{9,5},{13,9},{6,2},{10,6},{14,10},{7,3},{... | collective-permute-start | bytes 196616 | tf_op jit(solution)/shard_map/ppermute | solution.py:23
  193.8 12.3 %copy-start.4 = (bf16[832,256]{1,0:T(8,128)(2,1)S(1)}, bf16[832,256]{1,0:T(8,128)(2,1)}, u32[]{:S(2)}) copy-start(bf16[832,256]{1,0:T(8,128)(2,1)} %get-tuple-element.33) | copy-start | bytes 1277956
  193.8 12.3 %copy-start.5 = (bf16[832,256]{1,0:T(8,128)(2,1)S(1)}, bf16[832,256]{1,0:T(8,128)(2,1)}, u32[]{:S(2)}) copy-start(bf16[832,256]{1,0:T(8,128)(2,1)} %get-tuple-element.35) | copy-start | bytes 1277956
  193.8 70.5 %all-to-all-start.1 = ((bf16[36,64,512]{2,1,0:T(8,128)(2,1)}), bf16[36,64,512]{2,1,0:T(8,128)(2,1)S(1)}, u32[]{:S(2)}, u32[]{:S(2)}) async-start(bf16[36,64,512]{2,1,0:T(8,128)(2,1)} %slice.113), calls=%async_computation.2 | async-start | bytes 4718592 | tf_op jit(solution)/shard_map/all_to_all | solution.py:478
  200.1 67.6 %collective-permute-start.3 = (bf16[64,512]{1,0:T(8,128)(2,1)S(1)}, bf16[64,512]{1,0:T(8,128)(2,1)S(1)}, u32[]{:S(2)}, u32[]{:S(2)}) collective-permute-start(bf16[64,512]{1,0:T(8,128)(2,1)S(1)} %get-tuple-element.41), channel_id=1, source_target_pairs={{4,0},{8,4},{12,8},{5,1},{9,5},{13,9},{6,2},{10,6},{14,10},{7,3},{... | collective-permute-start | bytes 196616 | tf_op jit(solution)/shard_map/ppermute | solution.py:489
  202.9 64.7 %collective-permute-start.2 = (bf16[64,512]{1,0:T(8,128)(2,1)S(1)}, bf16[64,512]{1,0:T(8,128)(2,1)S(1)}, u32[]{:S(2)}, u32[]{:S(2)}) collective-permute-start(bf16[64,512]{1,0:T(8,128)(2,1)S(1)} %get-tuple-element.42), channel_id=1, source_target_pairs={{0,4},{4,8},{8,12},{1,5},{5,9},{9,13},{2,6},{6,10},{10,14},{3,7},{... | collective-permute-start | bytes 196616 | tf_op jit(solution)/shard_map/ppermute | solution.py:490
  264.6 1.9 copy-start.3
  267.7 1.5 copy-start.2
Sparse Core Ops, SparseCore 0:
  10.1 115.0 all-gather.1
  149.7 85.2 reduce-scatter.1

commit v13 on v11

--- a/solution.py
+++ b/solution.py
@@ -392,6 +392,48 @@
         ],
         compiler_params=pltpu.CompilerParams(vmem_limit_bytes=60 * 1024 * 1024),
     )(ids, write_ids, valid, first, queries, out_grad, *([source] * SLOTS))
+
+
+def finish_kernel(target_ref, returned_ref, own_b_ref, left_ref, right_ref, own_a_ref,
+                  rs_a_ref, key_ref, value_ref, sum_ref):
+    blocks_dev = own_b_ref.shape[0]
+    half = own_b_ref.shape[2] // 2
+    sum_ref[...] = own_b_ref[...]
+    sum_ref[0] = sum_ref[0] + left_ref[...].astype(jnp.float32)
+    sum_ref[blocks_dev - 1] = sum_ref[blocks_dev - 1] + right_ref[...].astype(jnp.float32)
+    for slot in range(returned_ref.shape[0]):
+        target = target_ref[slot]
+
+        @pl.when(target >= 0)
+        def _():
+            sum_ref[target] = sum_ref[target] + returned_ref[slot].astype(jnp.float32)
+
+    for block in range(blocks_dev):
+        rows = pl.ds(block * BLOCK, BLOCK)
+        first = own_a_ref[block] + rs_a_ref[rows, :].astype(jnp.float32)
+        second = sum_ref[block]
+        key_ref[rows, pl.ds(0, half)] = first[:, :half].astype(jnp.bfloat16)
+        key_ref[rows, pl.ds(half, half)] = second[:, :half].astype(jnp.bfloat16)
+        value_ref[rows, pl.ds(0, half)] = first[:, half:].astype(jnp.bfloat16)
+        value_ref[rows, pl.ds(half, half)] = second[:, half:].astype(jnp.bfloat16)
+
+
+def finish(target, returned, own_b, left, right, own_a, rs_a):
+    blocks_dev, _, width = own_b.shape
+    tokens = blocks_dev * BLOCK
+    vmem = pltpu.MemorySpace.VMEM if hasattr(pltpu, "MemorySpace") else pltpu.VMEM
+    smem_spec = pl.BlockSpec(memory_space=pltpu.SMEM)
+    vmem_spec = pl.BlockSpec(memory_space=vmem)
+    return pl.pallas_call(
+        finish_kernel,
+        in_specs=[smem_spec] + [vmem_spec] * 6,
+        out_specs=[vmem_spec, vmem_spec],
+        out_shape=[
+            jax.ShapeDtypeStruct((tokens, width), jnp.bfloat16),
+            jax.ShapeDtypeStruct((tokens, width), jnp.bfloat16),
+        ],
+        scratch_shapes=[pltpu.VMEM(own_b.shape, jnp.float32)],
+    )(target, returned, own_b, left, right, own_a, rs_a)
 
 
 def gathered_shards(queries, key_rows, value_rows, out_grad, random_device, random_block):
@@ -462,7 +504,7 @@
             returned = lax.psum_scatter(
                 spread.reshape(total * BLOCK, 2 * part), "seq", scatter_dimension=0, tiled=True
             )
-            summed = own_sum.reshape(tokens, 2 * part) + returned.astype(jnp.float32)
+            first_half = (own_sum, returned)
         else:
             slots = seq_size * capacity
             far_rows = slot_index.reshape(blocks_dev, RAND).astype(jnp.int32)
@@ -476,34 +518,24 @@
                 spread[:slots], "seq", split_axis=0, concat_axis=0, tiled=True
             )
             spread = spread[slots:]
-            gathered = jnp.dot(
-                selector.T,
-                returned.reshape(seq_size * capacity, BLOCK * 2 * part),
-                preferred_element_type=jnp.float32,
-            ).reshape(blocks_dev, BLOCK, 2 * part)
+
             left_edge = spread[0]
             right_edge = spread[blocks_dev + 1]
             from_right = lax.ppermute(left_edge, "seq", [(i, i - 1) for i in range(1, seq_size)])
             from_left = lax.ppermute(right_edge, "seq", [(i, i + 1) for i in range(seq_size - 1)])
-            combined = (
-                (own_sum + gathered)
-                .at[0].add(from_left.astype(jnp.float32))
-                .at[blocks_dev - 1].add(from_right.astype(jnp.float32))
-            )
-            summed = combined.reshape(tokens, 2 * part)
+            hits = selector > 0
+            target = jnp.where(
+                jnp.any(hits, axis=1), jnp.argmax(hits, axis=1).astype(jnp.int32), -1
+            )
+            finished = (target, returned, own_sum, from_left, from_right)
         after = own_sum
         query_parts.append(query_out)
-        key_parts.append(summed[:, :part].astype(jnp.bfloat16))
-        value_parts.append(summed[:, part:].astype(jnp.bfloat16))
-    return (
-        jnp.concatenate(query_parts, axis=1),
-        jnp.concatenate(key_parts, axis=1),
-        jnp.concatenate(value_parts, axis=1),
-    )
+    key_out, value_out = finish(*finished, *first_half)
+    return (jnp.concatenate(query_parts, axis=1), key_out, value_out)
 
 
 def shards(queries, key_rows, value_rows, out_grad, random_device, random_block):
-    if lax.axis_size("seq") <= 8:
+    if lax.axis_size("seq") <= 8 and (queries.shape[1] // DH) % 2 == 0:
         return gathered_shards(queries, key_rows, value_rows, out_grad, random_device, random_block)
     return exchanged_shards(queries, key_rows, value_rows, out_grad, random_device, random_block)
 

time: 285 us -> 283 us (level)
  Pallas kernels: 48.8 us -> 53.7 us
  other arithmetic: 10.3 us -> 6.88 us
    all_to_all x1, waiting for transfers between devices: 57.2 us -> 0.01 us  [gathered_shards(): lax.all_to_all(spread[:slots], 'seq', split_axis=0, concat_axis=0, tiled=...]
    ppermute x1, waiting for transfers between devices: 0.01 us -> 57 us  [gathered_shards(): lax.ppermute(left_edge, 'seq', [(i, i - 1) for i in range(1, seq_size)])]
    pallas_call x0 -> x1, Pallas kernels: none -> 4.95 us  [finish(): pl.pallas_call(finish_kernel, in_specs=[smem_spec] + [vmem_spec] * 6, out...]
  transfers between devices with their start and end apart: 8 -> 8, of which waited for: 4 -> 5; matrix products, arithmetic and copies ran while one was open for 8% -> 7% of each run, Pallas kernels for 9% -> 9%
where the time goes in v13:
time: 283 us; the launch traced here: 279 us
  waiting for transfers between devices  162 us (57%)
  Pallas kernels  53.7 us (19%)
  starting transfers between devices  23 us (8%)
  local copies, waits for them, and re-layouts  16.7 us (6%)
  between operations  15.5 us (5%)
  other arithmetic  6.88 us (2%)
    all_to_all x1, waiting for transfers between devices, gathered_shards(): lax.all_to_all(outgoing, 'seq', split_axis=0, concat_axis=0, tiled=True)  100 us
    ppermute x1, waiting for transfers between devices, gathered_shards(): lax.ppermute(left_edge, 'seq', [(i, i - 1) for i in range(1, seq_size)])  57 us
    pallas_call x2, Pallas kernels, block_attention(): pl.pallas_call(block_kernel, grid_spec=grid_spec, out_shape=[jax.ShapeDty...  48.8 us
  transfers between devices with their start and end apart: 8, of which 5 were waited for; matrix products, arithmetic and copies ran while one was open for 7% of the time, Pallas kernels for 9%

profile of v13, /device:TPU:22, one launch (start us, length us, event | category | flops | bytes accessed | tf_op | source)
XLA Modules:
  0.0 279.1 jit_solution(9578889868307147294)
XLA Ops:
  7.2 1.5 fusion.15
  8.8 1.0 pad_maximum_fusion.2
  12.2 1.0 copy.47
  13.2 1.6 slice.60
  14.8 5.2 %all-to-all-start = ((bf16[36,64,512]{2,1,0:T(8,128)(2,1)}), bf16[36,64,512]{2,1,0:T(8,128)(2,1)S(1)}, u32[]{:S(2)}, u32[]{:S(2)}) async-start(bf16[36,64,512]{2,1,0:T(8,128)(2,1)} %slice.60), calls=%async_computation | async-start | bytes 4718592 | tf_op jit(solution)/shard_map/all_to_all | solution.py:489
  22.8 100.4 %all-to-all-done = bf16[36,64,512]{2,1,0:T(8,128)(2,1)S(1)} async-done(((bf16[36,64,512]{2,1,0:T(8,128)(2,1)}), bf16[36,64,512]{2,1,0:T(8,128)(2,1)S(1)}, u32[]{:S(2)}, u32[]{:S(2)}) %all-to-all-start) | async-done | bytes 2359328 | tf_op jit(solution)/shard_map/all_to_all | solution.py:489
  124.3 1.0 all-gather.2.cloned.1.call-done
  125.3 24.4 %shard_map.85 = (f32[13,64,512]{2,1,0:T(8,128)}, bf16[52,64,512]{2,1,0:T(8,128)(2,1)}, bf16[832,256]{1,0:T(8,128)(2,1)}) custom-call(s32[65]{0:T(128)} %reshape.127.ids_ref.write_ref, s32[65]{0:T(128)} %reshape.127.ids_ref.write_ref, s32[65]{0:T(128)} %reshape.135.valid_ref, s32[1]{0:T(128)S(6)} %add.118.first_ref, bf16[832,512]{1,0:T(8,128)(2,1)} %q_ref.3, ...), custom_call_target="tpu_custom_call" | custom-call | tf_op jit(solution)/shard_map/pallas_call | solution.py:385
  149.7 0.8 fusion.3
  150.5 4.6 %collective-permute-start = (bf16[1,64,512]{2,1,0:T(8,128)(2,1)S(1)}, bf16[1,64,512]{2,1,0:T(8,128)(2,1)S(1)}, u32[]{:S(2)}, u32[]{:S(2)}) collective-permute-start(bf16[1,64,512]{2,1,0:T(8,128)(2,1)S(1)} %get-tuple-element.25), channel_id=1, source_target_pairs={{0,4},{4,8},{8,12},{1,5},{5,9},{9,13},{2,6},{6,10},{10,14},{3,7},{... | collective-permute-start | bytes 196616 | tf_op jit(solution)/shard_map/ppermute | solution.py:20
  155.2 1.9 collective-permute-start.1
  158.8 3.6 %collective-permute-done.1 = bf16[1,64,512]{2,1,0:T(8,128)(2,1)S(1)} collective-permute-done((bf16[1,64,512]{2,1,0:T(8,128)(2,1)S(1)}, bf16[1,64,512]{2,1,0:T(8,128)(2,1)S(1)}, u32[]{:S(2)}, u32[]{:S(2)}) %collective-permute-start.1) | collective-permute-done | bytes 65568 | tf_op jit(solution)/shard_map/ppermute | solution.py:23
  162.3 1.9 pad_maximum_fusion.rest_0_.rest_1_.rest_2_.rest_3_.rest_4_
  164.2 1.2 slice.47
  166.1 24.4 %shard_map.86 = (f32[13,64,512]{2,1,0:T(8,128)}, bf16[51,64,512]{2,1,0:T(8,128)(2,1)}, bf16[832,256]{1,0:T(8,128)(2,1)}) custom-call(s32[65]{0:T(128)} %reshape.131.ids_ref, s32[65]{0:T(128)} %reshape.132.write_ref, s32[65]{0:T(128)} %reshape.135.valid_ref, s32[1]{0:T(128)} %bitcast.3.first_ref, bf16[832,512]{1,0:T(8,128)(2,1)} %q_ref.3, ...), custom_call_target="tpu_custom_call" | custom-call | tf_op jit(solution)/shard_map/pallas_call | solution.py:385
  190.5 3.4 %slice.52 = bf16[36,64,512]{2,1,0:T(8,128)(2,1)} slice(bf16[51,64,512]{2,1,0:T(8,128)(2,1)} %get-tuple-element.16), slice={[0:36], [0:64], [0:512]} | slice | bytes 4718592 | tf_op jit(solution)/shard_map/slice | solution.py:518
  193.9 5.4 %all-to-all-start.1 = ((bf16[36,64,512]{2,1,0:T(8,128)(2,1)}), bf16[36,64,512]{2,1,0:T(8,128)(2,1)S(1)}, u32[]{:S(2)}, u32[]{:S(2)}) async-start(bf16[36,64,512]{2,1,0:T(8,128)(2,1)} %slice.52), calls=%async_computation.1 | async-start | bytes 4718592 | tf_op jit(solution)/shard_map/all_to_all | solution.py:517
  200.7 0.9 slice_bitcast_fusion
  201.6 2.8 %collective-permute-start.3 = (bf16[64,512]{1,0:T(8,128)(2,1)S(1)}, bf16[64,512]{1,0:T(8,128)(2,1)S(1)}, u32[]{:S(2)}, u32[]{:S(2)}) collective-permute-start(bf16[64,512]{1,0:T(8,128)(2,1)S(1)} %get-tuple-element.23), channel_id=1, source_target_pairs={{4,0},{8,4},{12,8},{5,1},{9,5},{13,9},{6,2},{10,6},{14,10},{7,3},{... | collective-permute-start | bytes 196616 | tf_op jit(solution)/shard_map/ppermute | solution.py:524
  204.4 3.0 %collective-permute-start.2 = (bf16[64,512]{1,0:T(8,128)(2,1)S(1)}, bf16[64,512]{1,0:T(8,128)(2,1)S(1)}, u32[]{:S(2)}, u32[]{:S(2)}) collective-permute-start(bf16[64,512]{1,0:T(8,128)(2,1)S(1)} %get-tuple-element.24), channel_id=1, source_target_pairs={{0,4},{4,8},{8,12},{1,5},{5,9},{9,13},{2,6},{6,10},{10,14},{3,7},{... | collective-permute-start | bytes 196616 | tf_op jit(solution)/shard_map/ppermute | solution.py:525
  207.5 1.0 pad_maximum_fusion.3
  208.5 57.0 %collective-permute-done.3.right_ref = bf16[64,512]{1,0:T(8,128)(2,1)S(1)} collective-permute-done((bf16[64,512]{1,0:T(8,128)(2,1)S(1)}, bf16[64,512]{1,0:T(8,128)(2,1)S(1)}, u32[]{:S(2)}, u32[]{:S(2)}) %collective-permute-start.3) | collective-permute-done | bytes 65568 | tf_op jit(solution)/shard_map/ppermute | solution.py:524
  266.4 0.9 copy-done
  267.3 5.0 %shard_map.87 = (bf16[832,512]{1,0:T(8,128)(2,1)}, bf16[832,512]{1,0:T(8,128)(2,1)}) custom-call(s32[36]{0:T(128)} %broadcast_select_fusion.target_ref, bf16[36,64,512]{2,1,0:T(8,128)(2,1)} %copy-done, f32[13,64,512]{2,1,0:T(8,128)} %get-tuple-element.17.own_b_ref, bf16[64,512]{1,0:T(8,128)(2,1)} %copy-done.6, bf16[64,512]{1,0:T(8,128)(2,1)} %copy-done.5, ...), custom_call_target="tpu_custom_call" | custom-call | tf_op jit(solution)/shard_map/pallas_call | solution.py:427
  (79 shorter events, 9.7 us)
Async XLA Ops:
  7.2 2.7 copy-start.7
  7.2 3.1 %copy-start.8 = (s32[52,2]{0,1:T(2,128)S(1)}, s32[52,2]{0,1:T(2,128)}, u32[]{:S(2)}) copy-start(s32[52,2]{0,1:T(2,128)} %param.11) | copy-start | bytes 1252
  7.2 118.1 %all-gather.2.cloned.1.call-start = ((), (), s32[]{:S(2)}) async-start(), calls=%async_computation.3 | async-start | bytes 4259840 | tf_op jit(solution)/shard_map/all_gather | solution.py:476
  8.8 1.9 copy-start.1
  8.8 1.9 copy-start.2
  14.8 108.4 %all-to-all-start = ((bf16[36,64,512]{2,1,0:T(8,128)(2,1)}), bf16[36,64,512]{2,1,0:T(8,128)(2,1)S(1)}, u32[]{:S(2)}, u32[]{:S(2)}) async-start(bf16[36,64,512]{2,1,0:T(8,128)(2,1)} %slice.60), calls=%async_computation | async-start | bytes 4718592 | tf_op jit(solution)/shard_map/all_to_all | solution.py:489
  20.0 245.9 %reduce-scatter.2.cloned.1.call-start = ((), (), s32[]{:S(2)}) async-start(), calls=%async_computation.4 | async-start | bytes 4259840 | tf_op jit(solution)/shard_map/reduce_scatter | solution.py:504
  150.5 8.2 %collective-permute-start = (bf16[1,64,512]{2,1,0:T(8,128)(2,1)S(1)}, bf16[1,64,512]{2,1,0:T(8,128)(2,1)S(1)}, u32[]{:S(2)}, u32[]{:S(2)}) collective-permute-start(bf16[1,64,512]{2,1,0:T(8,128)(2,1)S(1)} %get-tuple-element.25), channel_id=1, source_target_pairs={{0,4},{4,8},{8,12},{1,5},{5,9},{9,13},{2,6},{6,10},{10,14},{3,7},{... | collective-permute-start | bytes 196616 | tf_op jit(solution)/shard_map/ppermute | solution.py:20
  155.2 7.1 %collective-permute-start.1 = (bf16[1,64,512]{2,1,0:T(8,128)(2,1)S(1)}, bf16[1,64,512]{2,1,0:T(8,128)(2,1)S(1)}, u32[]{:S(2)}, u32[]{:S(2)}) collective-permute-start(bf16[1,64,512]{2,1,0:T(8,128)(2,1)S(1)} %get-tuple-element.26), channel_id=1, source_target_pairs={{4,0},{8,4},{12,8},{5,1},{9,5},{13,9},{6,2},{10,6},{14,10},{7,3},{... | collective-permute-start | bytes 196616 | tf_op jit(solution)/shard_map/ppermute | solution.py:23
  193.9 13.6 %copy-start.3 = (bf16[832,256]{1,0:T(8,128)(2,1)S(1)}, bf16[832,256]{1,0:T(8,128)(2,1)}, u32[]{:S(2)}) copy-start(bf16[832,256]{1,0:T(8,128)(2,1)} %get-tuple-element.12) | copy-start | bytes 1277956
  193.9 13.6 %copy-start.4 = (bf16[832,256]{1,0:T(8,128)(2,1)S(1)}, bf16[832,256]{1,0:T(8,128)(2,1)}, u32[]{:S(2)}) copy-start(bf16[832,256]{1,0:T(8,128)(2,1)} %get-tuple-element.14) | copy-start | bytes 1277956
  193.9 71.9 %all-to-all-start.1 = ((bf16[36,64,512]{2,1,0:T(8,128)(2,1)}), bf16[36,64,512]{2,1,0:T(8,128)(2,1)S(1)}, u32[]{:S(2)}, u32[]{:S(2)}) async-start(bf16[36,64,512]{2,1,0:T(8,128)(2,1)} %slice.52), calls=%async_computation.1 | async-start | bytes 4718592 | tf_op jit(solution)/shard_map/all_to_all | solution.py:517
  201.6 63.9 %collective-permute-start.3 = (bf16[64,512]{1,0:T(8,128)(2,1)S(1)}, bf16[64,512]{1,0:T(8,128)(2,1)S(1)}, u32[]{:S(2)}, u32[]{:S(2)}) collective-permute-start(bf16[64,512]{1,0:T(8,128)(2,1)S(1)} %get-tuple-element.23), channel_id=1, source_target_pairs={{4,0},{8,4},{12,8},{5,1},{9,5},{13,9},{6,2},{10,6},{14,10},{7,3},{... | collective-permute-start | bytes 196616 | tf_op jit(solution)/shard_map/ppermute | solution.py:524
  204.4 61.4 %collective-permute-start.2 = (bf16[64,512]{1,0:T(8,128)(2,1)S(1)}, bf16[64,512]{1,0:T(8,128)(2,1)S(1)}, u32[]{:S(2)}, u32[]{:S(2)}) collective-permute-start(bf16[64,512]{1,0:T(8,128)(2,1)S(1)} %get-tuple-element.24), channel_id=1, source_target_pairs={{0,4},{4,8},{8,12},{1,5},{5,9},{9,13},{2,6},{6,10},{10,14},{3,7},{... | collective-permute-start | bytes 196616 | tf_op jit(solution)/shard_map/ppermute | solution.py:525
  265.5 0.6 copy-start.5
  265.8 0.6 copy-start.6
  265.8 1.5 copy-start
Sparse Core Ops, SparseCore 0:
  10.2 115.0 all-gather.1
  149.8 85.2 reduce-scatter.1

commit v14 on v13

--- a/solution.py
+++ b/solution.py
@@ -396,43 +396,54 @@
 
 def finish_kernel(target_ref, returned_ref, own_b_ref, left_ref, right_ref, own_a_ref,
                   rs_a_ref, key_ref, value_ref, sum_ref):
-    blocks_dev = own_b_ref.shape[0]
+    block = pl.program_id(0)
+    last = pl.num_programs(0) - 1
     half = own_b_ref.shape[2] // 2
-    sum_ref[...] = own_b_ref[...]
-    sum_ref[0] = sum_ref[0] + left_ref[...].astype(jnp.float32)
-    sum_ref[blocks_dev - 1] = sum_ref[blocks_dev - 1] + right_ref[...].astype(jnp.float32)
+    sum_ref[...] = own_b_ref[0]
+
+    @pl.when(block == 0)
+    def _():
+        sum_ref[...] = sum_ref[...] + left_ref[...].astype(jnp.float32)
+
+    @pl.when(block == last)
+    def _():
+        sum_ref[...] = sum_ref[...] + right_ref[...].astype(jnp.float32)
+
     for slot in range(returned_ref.shape[0]):
-        target = target_ref[slot]
-
-        @pl.when(target >= 0)
+
+        @pl.when(target_ref[slot] == block)
         def _():
-            sum_ref[target] = sum_ref[target] + returned_ref[slot].astype(jnp.float32)
-
-    for block in range(blocks_dev):
-        rows = pl.ds(block * BLOCK, BLOCK)
-        first = own_a_ref[block] + rs_a_ref[rows, :].astype(jnp.float32)
-        second = sum_ref[block]
-        key_ref[rows, pl.ds(0, half)] = first[:, :half].astype(jnp.bfloat16)
-        key_ref[rows, pl.ds(half, half)] = second[:, :half].astype(jnp.bfloat16)
-        value_ref[rows, pl.ds(0, half)] = first[:, half:].astype(jnp.bfloat16)
-        value_ref[rows, pl.ds(half, half)] = second[:, half:].astype(jnp.bfloat16)
+            sum_ref[...] = sum_ref[...] + returned_ref[slot].astype(jnp.float32)
+
+    first = own_a_ref[0] + rs_a_ref[...].astype(jnp.float32)
+    second = sum_ref[...]
+    key_ref[:, pl.ds(0, half)] = first[:, :half].astype(jnp.bfloat16)
+    key_ref[:, pl.ds(half, half)] = second[:, :half].astype(jnp.bfloat16)
+    value_ref[:, pl.ds(0, half)] = first[:, half:].astype(jnp.bfloat16)
+    value_ref[:, pl.ds(half, half)] = second[:, half:].astype(jnp.bfloat16)
 
 
 def finish(target, returned, own_b, left, right, own_a, rs_a):
     blocks_dev, _, width = own_b.shape
     tokens = blocks_dev * BLOCK
-    vmem = pltpu.MemorySpace.VMEM if hasattr(pltpu, "MemorySpace") else pltpu.VMEM
-    smem_spec = pl.BlockSpec(memory_space=pltpu.SMEM)
-    vmem_spec = pl.BlockSpec(memory_space=vmem)
+    whole = pl.BlockSpec(returned.shape, lambda j, target: (0, 0, 0))
+    edge = pl.BlockSpec(left.shape, lambda j, target: (0, 0))
+    stacked = pl.BlockSpec((1, BLOCK, width), lambda j, target: (j, 0, 0))
+    rows = pl.BlockSpec((BLOCK, width), lambda j, target: (j, 0))
+    grid_spec = pltpu.PrefetchScalarGridSpec(
+        num_scalar_prefetch=1,
+        grid=(blocks_dev,),
+        in_specs=[whole, stacked, edge, edge, stacked, rows],
+        out_specs=[rows, rows],
+        scratch_shapes=[pltpu.VMEM((BLOCK, width), jnp.float32)],
+    )
     return pl.pallas_call(
         finish_kernel,
-        in_specs=[smem_spec] + [vmem_spec] * 6,
-        out_specs=[vmem_spec, vmem_spec],
+        grid_spec=grid_spec,
         out_shape=[
             jax.ShapeDtypeStruct((tokens, width), jnp.bfloat16),
             jax.ShapeDtypeStruct((tokens, width), jnp.bfloat16),
         ],
-        scratch_shapes=[pltpu.VMEM(own_b.shape, jnp.float32)],
     )(target, returned, own_b, left, right, own_a, rs_a)
 
 

time: 283 us -> 290 us (1.025)
  Pallas kernels: 53.7 us -> 60.7 us
    pallas_call x1, Pallas kernels: 4.95 us -> 12 us  [finish(): pl.pallas_call(finish_kernel, grid_spec=grid_spec, out_shape=[jax.ShapeDt...]
where the time goes in v14:
time: 290 us; the launch traced here: 286 us
  waiting for transfers between devices  162 us (56%)
  Pallas kernels  60.7 us (21%)
  starting transfers between devices  23 us (8%)
  local copies, waits for them, and re-layouts  16.7 us (6%)
  between operations  15.5 us (5%)
  other arithmetic  6.88 us (2%)
    all_to_all x1, waiting for transfers between devices, gathered_shards(): lax.all_to_all(outgoing, 'seq', split_axis=0, concat_axis=0, tiled=True)  100 us
    ppermute x1, waiting for transfers between devices, gathered_shards(): lax.ppermute(left_edge, 'seq', [(i, i - 1) for i in range(1, seq_size)])  57 us
    pallas_call x2, Pallas kernels, block_attention(): pl.pallas_call(block_kernel, grid_spec=grid_spec, out_shape=[jax.ShapeDty...  48.8 us
    pallas_call x1, Pallas kernels, finish(): pl.pallas_call(finish_kernel, grid_spec=grid_spec, out_shape=[jax.ShapeDt...  12 us
  transfers between devices with their start and end apart: 8, of which 5 were waited for; matrix products, arithmetic and copies ran while one was open for 7% of the time, Pallas kernels for 9%

profile of v14, /device:TPU:22, one launch (start us, length us, event | category | flops | bytes accessed | tf_op | source)
XLA Modules:
  0.0 286.1 jit_solution(8286236274916901588)
XLA Ops:
  7.2 1.5 fusion.15
  8.8 1.0 pad_maximum_fusion.2
  12.2 1.0 copy.47
  13.2 1.6 slice.60
  14.8 5.2 %all-to-all-start = ((bf16[36,64,512]{2,1,0:T(8,128)(2,1)}), bf16[36,64,512]{2,1,0:T(8,128)(2,1)S(1)}, u32[]{:S(2)}, u32[]{:S(2)}) async-start(bf16[36,64,512]{2,1,0:T(8,128)(2,1)} %slice.60), calls=%async_computation | async-start | bytes 4718592 | tf_op jit(solution)/shard_map/all_to_all | solution.py:500
  22.8 100.4 %all-to-all-done = bf16[36,64,512]{2,1,0:T(8,128)(2,1)S(1)} async-done(((bf16[36,64,512]{2,1,0:T(8,128)(2,1)}), bf16[36,64,512]{2,1,0:T(8,128)(2,1)S(1)}, u32[]{:S(2)}, u32[]{:S(2)}) %all-to-all-start) | async-done | bytes 2359328 | tf_op jit(solution)/shard_map/all_to_all | solution.py:500
  124.3 1.0 all-gather.2.cloned.1.call-done
  125.3 24.4 %shard_map.85 = (f32[13,64,512]{2,1,0:T(8,128)}, bf16[52,64,512]{2,1,0:T(8,128)(2,1)}, bf16[832,256]{1,0:T(8,128)(2,1)}) custom-call(s32[65]{0:T(128)} %reshape.127.ids_ref.write_ref, s32[65]{0:T(128)} %reshape.127.ids_ref.write_ref, s32[65]{0:T(128)} %reshape.135.valid_ref, s32[1]{0:T(128)S(6)} %add.118.first_ref, bf16[832,512]{1,0:T(8,128)(2,1)} %q_ref.3, ...), custom_call_target="tpu_custom_call" | custom-call | tf_op jit(solution)/shard_map/pallas_call | solution.py:385
  149.7 0.8 fusion.3
  150.5 4.6 %collective-permute-start = (bf16[1,64,512]{2,1,0:T(8,128)(2,1)S(1)}, bf16[1,64,512]{2,1,0:T(8,128)(2,1)S(1)}, u32[]{:S(2)}, u32[]{:S(2)}) collective-permute-start(bf16[1,64,512]{2,1,0:T(8,128)(2,1)S(1)} %get-tuple-element.25), channel_id=1, source_target_pairs={{0,4},{4,8},{8,12},{1,5},{5,9},{9,13},{2,6},{6,10},{10,14},{3,7},{... | collective-permute-start | bytes 196616 | tf_op jit(solution)/shard_map/ppermute | solution.py:20
  155.2 1.9 collective-permute-start.1
  158.8 3.6 %collective-permute-done.1 = bf16[1,64,512]{2,1,0:T(8,128)(2,1)S(1)} collective-permute-done((bf16[1,64,512]{2,1,0:T(8,128)(2,1)S(1)}, bf16[1,64,512]{2,1,0:T(8,128)(2,1)S(1)}, u32[]{:S(2)}, u32[]{:S(2)}) %collective-permute-start.1) | collective-permute-done | bytes 65568 | tf_op jit(solution)/shard_map/ppermute | solution.py:23
  162.3 1.9 pad_maximum_fusion.rest_0_.rest_1_.rest_2_.rest_3_.rest_4_
  164.2 1.2 slice.47
  166.1 24.4 %shard_map.86 = (f32[13,64,512]{2,1,0:T(8,128)}, bf16[51,64,512]{2,1,0:T(8,128)(2,1)}, bf16[832,256]{1,0:T(8,128)(2,1)}) custom-call(s32[65]{0:T(128)} %reshape.131.ids_ref, s32[65]{0:T(128)} %reshape.132.write_ref, s32[65]{0:T(128)} %reshape.135.valid_ref, s32[1]{0:T(128)} %bitcast.3.first_ref, bf16[832,512]{1,0:T(8,128)(2,1)} %q_ref.3, ...), custom_call_target="tpu_custom_call" | custom-call | tf_op jit(solution)/shard_map/pallas_call | solution.py:385
  190.5 3.4 %slice.52 = bf16[36,64,512]{2,1,0:T(8,128)(2,1)} slice(bf16[51,64,512]{2,1,0:T(8,128)(2,1)} %get-tuple-element.16), slice={[0:36], [0:64], [0:512]} | slice | bytes 4718592 | tf_op jit(solution)/shard_map/slice | solution.py:529
  193.9 5.4 %all-to-all-start.1 = ((bf16[36,64,512]{2,1,0:T(8,128)(2,1)}), bf16[36,64,512]{2,1,0:T(8,128)(2,1)S(1)}, u32[]{:S(2)}, u32[]{:S(2)}) async-start(bf16[36,64,512]{2,1,0:T(8,128)(2,1)} %slice.52), calls=%async_computation.1 | async-start | bytes 4718592 | tf_op jit(solution)/shard_map/all_to_all | solution.py:528
  200.7 0.9 slice_bitcast_fusion
  201.6 2.8 collective-permute-start.3
  204.4 3.0 %collective-permute-start.2 = (bf16[64,512]{1,0:T(8,128)(2,1)S(1)}, bf16[64,512]{1,0:T(8,128)(2,1)S(1)}, u32[]{:S(2)}, u32[]{:S(2)}) collective-permute-start(bf16[64,512]{1,0:T(8,128)(2,1)S(1)} %get-tuple-element.24), channel_id=1, source_target_pairs={{0,4},{4,8},{8,12},{1,5},{5,9},{9,13},{2,6},{6,10},{10,14},{3,7},{... | collective-permute-start | bytes 196616 | tf_op jit(solution)/shard_map/ppermute | solution.py:536
  207.5 1.0 pad_maximum_fusion.3
  208.5 57.0 %collective-permute-done.3.right_ref = bf16[64,512]{1,0:T(8,128)(2,1)S(1)} collective-permute-done((bf16[64,512]{1,0:T(8,128)(2,1)S(1)}, bf16[64,512]{1,0:T(8,128)(2,1)S(1)}, u32[]{:S(2)}, u32[]{:S(2)}) %collective-permute-start.3) | collective-permute-done | bytes 65568 | tf_op jit(solution)/shard_map/ppermute | solution.py:535
  266.4 0.9 copy-done
  267.3 12.0 %shard_map.87 = (bf16[832,512]{1,0:T(8,128)(2,1)}, bf16[832,512]{1,0:T(8,128)(2,1)}) custom-call(s32[36]{0:T(128)} %broadcast_select_fusion.target_ref, bf16[36,64,512]{2,1,0:T(8,128)(2,1)} %copy-done, f32[13,64,512]{2,1,0:T(8,128)} %get-tuple-element.17.own_b_ref, bf16[64,512]{1,0:T(8,128)(2,1)} %copy-done.6, bf16[64,512]{1,0:T(8,128)(2,1)} %copy-done.5, ...), custom_call_target="tpu_custom_call" | custom-call | tf_op jit(solution)/shard_map/pallas_call | solution.py:440
  (79 shorter events, 9.7 us)
Async XLA Ops:
  7.2 2.7 copy-start.7
  7.2 3.1 %copy-start.8 = (s32[52,2]{0,1:T(2,128)S(1)}, s32[52,2]{0,1:T(2,128)}, u32[]{:S(2)}) copy-start(s32[52,2]{0,1:T(2,128)} %param.11) | copy-start | bytes 1252
  7.2 118.1 %all-gather.2.cloned.1.call-start = ((), (), s32[]{:S(2)}) async-start(), calls=%async_computation.3 | async-start | bytes 4259840 | tf_op jit(solution)/shard_map/all_gather | solution.py:487
  8.8 1.9 copy-start.1
  8.8 1.9 copy-start.2
  14.8 108.4 %all-to-all-start = ((bf16[36,64,512]{2,1,0:T(8,128)(2,1)}), bf16[36,64,512]{2,1,0:T(8,128)(2,1)S(1)}, u32[]{:S(2)}, u32[]{:S(2)}) async-start(bf16[36,64,512]{2,1,0:T(8,128)(2,1)} %slice.60), calls=%async_computation | async-start | bytes 4718592 | tf_op jit(solution)/shard_map/all_to_all | solution.py:500
  20.0 245.9 %reduce-scatter.2.cloned.1.call-start = ((), (), s32[]{:S(2)}) async-start(), calls=%async_computation.4 | async-start | bytes 4259840 | tf_op jit(solution)/shard_map/reduce_scatter | solution.py:515
  150.5 8.2 %collective-permute-start = (bf16[1,64,512]{2,1,0:T(8,128)(2,1)S(1)}, bf16[1,64,512]{2,1,0:T(8,128)(2,1)S(1)}, u32[]{:S(2)}, u32[]{:S(2)}) collective-permute-start(bf16[1,64,512]{2,1,0:T(8,128)(2,1)S(1)} %get-tuple-element.25), channel_id=1, source_target_pairs={{0,4},{4,8},{8,12},{1,5},{5,9},{9,13},{2,6},{6,10},{10,14},{3,7},{... | collective-permute-start | bytes 196616 | tf_op jit(solution)/shard_map/ppermute | solution.py:20
  155.2 7.1 %collective-permute-start.1 = (bf16[1,64,512]{2,1,0:T(8,128)(2,1)S(1)}, bf16[1,64,512]{2,1,0:T(8,128)(2,1)S(1)}, u32[]{:S(2)}, u32[]{:S(2)}) collective-permute-start(bf16[1,64,512]{2,1,0:T(8,128)(2,1)S(1)} %get-tuple-element.26), channel_id=1, source_target_pairs={{4,0},{8,4},{12,8},{5,1},{9,5},{13,9},{6,2},{10,6},{14,10},{7,3},{... | collective-permute-start | bytes 196616 | tf_op jit(solution)/shard_map/ppermute | solution.py:23
  193.9 13.6 %copy-start.3 = (bf16[832,256]{1,0:T(8,128)(2,1)S(1)}, bf16[832,256]{1,0:T(8,128)(2,1)}, u32[]{:S(2)}) copy-start(bf16[832,256]{1,0:T(8,128)(2,1)} %get-tuple-element.12) | copy-start | bytes 1277956
  193.9 13.6 %copy-start.4 = (bf16[832,256]{1,0:T(8,128)(2,1)S(1)}, bf16[832,256]{1,0:T(8,128)(2,1)}, u32[]{:S(2)}) copy-start(bf16[832,256]{1,0:T(8,128)(2,1)} %get-tuple-element.14) | copy-start | bytes 1277956
  193.9 71.9 %all-to-all-start.1 = ((bf16[36,64,512]{2,1,0:T(8,128)(2,1)}), bf16[36,64,512]{2,1,0:T(8,128)(2,1)S(1)}, u32[]{:S(2)}, u32[]{:S(2)}) async-start(bf16[36,64,512]{2,1,0:T(8,128)(2,1)} %slice.52), calls=%async_computation.1 | async-start | bytes 4718592 | tf_op jit(solution)/shard_map/all_to_all | solution.py:528
  201.6 63.9 %collective-permute-start.3 = (bf16[64,512]{1,0:T(8,128)(2,1)S(1)}, bf16[64,512]{1,0:T(8,128)(2,1)S(1)}, u32[]{:S(2)}, u32[]{:S(2)}) collective-permute-start(bf16[64,512]{1,0:T(8,128)(2,1)S(1)} %get-tuple-element.23), channel_id=1, source_target_pairs={{4,0},{8,4},{12,8},{5,1},{9,5},{13,9},{6,2},{10,6},{14,10},{7,3},{... | collective-permute-start | bytes 196616 | tf_op jit(solution)/shard_map/ppermute | solution.py:535
  204.4 61.4 %collective-permute-start.2 = (bf16[64,512]{1,0:T(8,128)(2,1)S(1)}, bf16[64,512]{1,0:T(8,128)(2,1)S(1)}, u32[]{:S(2)}, u32[]{:S(2)}) collective-permute-start(bf16[64,512]{1,0:T(8,128)(2,1)S(1)} %get-tuple-element.24), channel_id=1, source_target_pairs={{0,4},{4,8},{8,12},{1,5},{5,9},{9,13},{2,6},{6,10},{10,14},{3,7},{... | collective-permute-start | bytes 196616 | tf_op jit(solution)/shard_map/ppermute | solution.py:536
  265.5 0.6 copy-start.5
  265.8 0.6 copy-start.6
  265.8 1.5 copy-start
Sparse Core Ops, SparseCore 0:
  10.2 115.0 all-gather.1
  149.8 85.2 reduce-scatter.1

commit v15 on v13

--- a/solution.py
+++ b/solution.py
@@ -292,15 +292,11 @@
     blocks_dev = own_ref.shape[0]
     logit_scale = 1.0 / math.sqrt(DH)
 
-    @pl.when(step == 0)
-    def _():
-        acc_ref[...] = jnp.zeros(acc_ref.shape, jnp.float32)
-
     context = jnp.concatenate([ref[0] for ref in kv_refs], axis=0)
     slot_of = lax.broadcasted_iota(jnp.int32, (1, SLOTS * BLOCK), 1) // BLOCK
     usable = slot_of < 0
     for slot in range(SLOTS):
-        usable = usable | ((slot_of == slot) & (valid_ref[step * SLOTS + slot] > 0))
+        usable = usable | ((slot_of == slot) & (valid_ref[step * SLOTS + slot] % 2 > 0))
     key_parts, value_parts = [], []
     for head in range(width // DH):
         cols = slice(head * DH, (head + 1) * DH)
@@ -347,12 +343,20 @@
         if slot >= 3:
             piece = piece.astype(jnp.bfloat16).astype(jnp.float32)
         target = write_ref[step * SLOTS + slot]
-        acc_ref[target] = acc_ref[target] + piece
+        fresh = valid_ref[step * SLOTS + slot] >= 2
+        acc_ref[target] = jnp.where(fresh, piece, acc_ref[target] + piece)
 
     @pl.when(step == steps - 1)
     def _():
         first = first_ref[0]
-        spread_ref[...] = acc_ref[...].astype(jnp.bfloat16)
+        spread_ref[...] = jnp.zeros(spread_ref.shape, jnp.bfloat16)
+        for entry in range(blocks_dev * SLOTS):
+            row = write_ref[entry]
+
+            @pl.when(valid_ref[entry] >= 2)
+            def _():
+                spread_ref[row] = acc_ref[row].astype(jnp.bfloat16)
+
         for block in range(blocks_dev):
             own_ref[block] = acc_ref[first + block]
             spread_ref[first + block] = jnp.zeros(spread_ref.shape[1:], jnp.bfloat16)
@@ -361,6 +365,11 @@
 def block_attention(ids, write_ids, valid, first, queries, out_grad, source, chunk, width, total):
     tokens = queries.shape[0]
     blocks_dev = tokens // BLOCK
+    entries = write_ids.shape[0]
+    same = write_ids[:, None] == write_ids[None, :]
+    before = jnp.arange(entries)[None, :] < jnp.arange(entries)[:, None]
+    fresh = jnp.logical_not(jnp.any(same & before, axis=1))
+    valid = valid + 2 * fresh.astype(jnp.int32)
 
     def context_spec(slot):
         return pl.BlockSpec(

time: 283 us -> 283 us (level)
  no operation moved by 1% of the time
where the time goes in v15:
time: 283 us; the launch traced here: 279 us
  waiting for transfers between devices  163 us (58%)
  Pallas kernels  54.4 us (19%)
  starting transfers between devices  23 us (8%)
  between operations  15.5 us (5%)
  local copies, waits for them, and re-layouts  15 us (5%)
  other arithmetic  7.68 us (3%)
    all_to_all x1, waiting for transfers between devices, gathered_shards(): lax.all_to_all(outgoing, 'seq', split_axis=0, concat_axis=0, tiled=True)  100 us
    ppermute x1, waiting for transfers between devices, gathered_shards(): lax.ppermute(left_edge, 'seq', [(i, i - 1) for i in range(1, seq_size)])  56.7 us
    pallas_call x2, Pallas kernels, block_attention(): pl.pallas_call(block_kernel, grid_spec=grid_spec, out_shape=[jax.ShapeDty...  49.4 us
  transfers between devices with their start and end apart: 8, of which 5 were waited for; matrix products, arithmetic and copies ran while one was open for 7% of the time, Pallas kernels for 9%

profile of v15, /device:TPU:22, one launch (start us, length us, event | category | flops | bytes accessed | tf_op | source)
XLA Modules:
  0.0 279.4 jit_solution(16058581680136492723)
XLA Ops:
  7.2 1.5 fusion.19
  8.8 1.0 pad_maximum_fusion.2
  12.2 1.0 copy.58
  13.2 1.6 slice.60
  14.8 5.2 %all-to-all-start = ((bf16[36,64,512]{2,1,0:T(8,128)(2,1)}), bf16[36,64,512]{2,1,0:T(8,128)(2,1)S(1)}, u32[]{:S(2)}, u32[]{:S(2)}) async-start(bf16[36,64,512]{2,1,0:T(8,128)(2,1)} %slice.60), calls=%async_computation | async-start | bytes 4718592 | tf_op jit(solution)/shard_map/all_to_all | solution.py:498
  22.9 100.3 %all-to-all-done = bf16[36,64,512]{2,1,0:T(8,128)(2,1)S(1)} async-done(((bf16[36,64,512]{2,1,0:T(8,128)(2,1)}), bf16[36,64,512]{2,1,0:T(8,128)(2,1)S(1)}, u32[]{:S(2)}, u32[]{:S(2)}) %all-to-all-start) | async-done | bytes 2359328 | tf_op jit(solution)/shard_map/all_to_all | solution.py:498
  124.3 1.0 all-gather.2.cloned.1.call-done
  125.3 24.7 %shard_map.85 = (f32[13,64,512]{2,1,0:T(8,128)}, bf16[52,64,512]{2,1,0:T(8,128)(2,1)}, bf16[832,256]{1,0:T(8,128)(2,1)}) custom-call(s32[65]{0:T(128)} %copy-done.7, s32[65]{0:T(128)} %copy-done.7, s32[65]{0:T(128)} %get-tuple-element.32.valid_ref, s32[1]{0:T(128)S(6)} %add.125.first_ref, bf16[832,512]{1,0:T(8,128)(2,1)} %q_ref.3, bf16[832,512]{1,0:T(8,128)(2,1)} %g_ref.3, ...), custom_call_target="tpu_custom_call" | custom-call | tf_op jit(solution)/shard_map/pallas_call | solution.py:394
  150.0 0.8 fusion.3
  150.8 4.6 %collective-permute-start = (bf16[1,64,512]{2,1,0:T(8,128)(2,1)S(1)}, bf16[1,64,512]{2,1,0:T(8,128)(2,1)S(1)}, u32[]{:S(2)}, u32[]{:S(2)}) collective-permute-start(bf16[1,64,512]{2,1,0:T(8,128)(2,1)S(1)} %get-tuple-element.25), channel_id=1, source_target_pairs={{0,4},{4,8},{8,12},{1,5},{5,9},{9,13},{2,6},{6,10},{10,14},{3,7},{... | collective-permute-start | bytes 196616 | tf_op jit(solution)/shard_map/ppermute | solution.py:20
  155.5 1.9 collective-permute-start.1
  158.2 4.4 %collective-permute-done.1 = bf16[1,64,512]{2,1,0:T(8,128)(2,1)S(1)} collective-permute-done((bf16[1,64,512]{2,1,0:T(8,128)(2,1)S(1)}, bf16[1,64,512]{2,1,0:T(8,128)(2,1)S(1)}, u32[]{:S(2)}, u32[]{:S(2)}) %collective-permute-start.1) | collective-permute-done | bytes 65568 | tf_op jit(solution)/shard_map/ppermute | solution.py:23
  162.6 1.9 pad_maximum_fusion.rest_0_.rest_1_.rest_2_.rest_3_.rest_4_
  164.5 1.2 slice.47
  166.4 24.7 %shard_map.86 = (f32[13,64,512]{2,1,0:T(8,128)}, bf16[51,64,512]{2,1,0:T(8,128)(2,1)}, bf16[832,256]{1,0:T(8,128)(2,1)}) custom-call(s32[65]{0:T(128)} %reshape.135.ids_ref, s32[65]{0:T(128)} %copy-done.9, s32[65]{0:T(128)} %get-tuple-element.33.valid_ref, s32[1]{0:T(128)} %bitcast.3.first_ref, bf16[832,512]{1,0:T(8,128)(2,1)} %q_ref.3, ...), custom_call_target="tpu_custom_call" | custom-call | tf_op jit(solution)/shard_map/pallas_call | solution.py:394
  191.1 3.5 %slice.52 = bf16[36,64,512]{2,1,0:T(8,128)(2,1)} slice(bf16[51,64,512]{2,1,0:T(8,128)(2,1)} %get-tuple-element.16), slice={[0:36], [0:64], [0:512]} | slice | bytes 4718592 | tf_op jit(solution)/shard_map/slice | solution.py:527
  194.6 5.4 %all-to-all-start.1 = ((bf16[36,64,512]{2,1,0:T(8,128)(2,1)}), bf16[36,64,512]{2,1,0:T(8,128)(2,1)S(1)}, u32[]{:S(2)}, u32[]{:S(2)}) async-start(bf16[36,64,512]{2,1,0:T(8,128)(2,1)} %slice.52), calls=%async_computation.1 | async-start | bytes 4718592 | tf_op jit(solution)/shard_map/all_to_all | solution.py:526
  201.4 0.9 slice_bitcast_fusion
  202.3 2.8 %collective-permute-start.3 = (bf16[64,512]{1,0:T(8,128)(2,1)S(1)}, bf16[64,512]{1,0:T(8,128)(2,1)S(1)}, u32[]{:S(2)}, u32[]{:S(2)}) collective-permute-start(bf16[64,512]{1,0:T(8,128)(2,1)S(1)} %get-tuple-element.23), channel_id=1, source_target_pairs={{4,0},{8,4},{12,8},{5,1},{9,5},{13,9},{6,2},{10,6},{14,10},{7,3},{... | collective-permute-start | bytes 196616 | tf_op jit(solution)/shard_map/ppermute | solution.py:533
  205.1 3.0 %collective-permute-start.2 = (bf16[64,512]{1,0:T(8,128)(2,1)S(1)}, bf16[64,512]{1,0:T(8,128)(2,1)S(1)}, u32[]{:S(2)}, u32[]{:S(2)}) collective-permute-start(bf16[64,512]{1,0:T(8,128)(2,1)S(1)} %get-tuple-element.24), channel_id=1, source_target_pairs={{0,4},{4,8},{8,12},{1,5},{5,9},{9,13},{2,6},{6,10},{10,14},{3,7},{... | collective-permute-start | bytes 196616 | tf_op jit(solution)/shard_map/ppermute | solution.py:534
  208.1 1.0 pad_maximum_fusion.3
  209.1 56.7 %collective-permute-done.3.right_ref = bf16[64,512]{1,0:T(8,128)(2,1)S(1)} collective-permute-done((bf16[64,512]{1,0:T(8,128)(2,1)S(1)}, bf16[64,512]{1,0:T(8,128)(2,1)S(1)}, u32[]{:S(2)}, u32[]{:S(2)}) %collective-permute-start.3) | collective-permute-done | bytes 65568 | tf_op jit(solution)/shard_map/ppermute | solution.py:533
  266.7 0.9 copy-done
  267.6 5.0 %shard_map.87 = (bf16[832,512]{1,0:T(8,128)(2,1)}, bf16[832,512]{1,0:T(8,128)(2,1)}) custom-call(s32[36]{0:T(128)} %broadcast_select_fusion.target_ref, bf16[36,64,512]{2,1,0:T(8,128)(2,1)} %copy-done, f32[13,64,512]{2,1,0:T(8,128)} %get-tuple-element.17.own_b_ref, bf16[64,512]{1,0:T(8,128)(2,1)} %copy-done.6, bf16[64,512]{1,0:T(8,128)(2,1)} %copy-done.5, ...), custom_call_target="tpu_custom_call" | custom-call | tf_op jit(solution)/shard_map/pallas_call | solution.py:436
  (86 shorter events, 8.8 us)
Async XLA Ops:
  7.2 2.7 copy-start.8
  7.2 3.1 %copy-start.10 = (s32[52,2]{0,1:T(2,128)S(1)}, s32[52,2]{0,1:T(2,128)}, u32[]{:S(2)}) copy-start(s32[52,2]{0,1:T(2,128)} %param.11) | copy-start | bytes 1252
  7.2 118.1 %all-gather.2.cloned.1.call-start = ((), (), s32[]{:S(2)}) async-start(), calls=%async_computation.3 | async-start | bytes 4259840 | tf_op jit(solution)/shard_map/all_gather | solution.py:485
  8.8 1.9 copy-start.1
  8.8 1.9 copy-start.2
  14.8 108.4 %all-to-all-start = ((bf16[36,64,512]{2,1,0:T(8,128)(2,1)}), bf16[36,64,512]{2,1,0:T(8,128)(2,1)S(1)}, u32[]{:S(2)}, u32[]{:S(2)}) async-start(bf16[36,64,512]{2,1,0:T(8,128)(2,1)} %slice.60), calls=%async_computation | async-start | bytes 4718592 | tf_op jit(solution)/shard_map/all_to_all | solution.py:498
  20.0 246.2 %reduce-scatter.2.cloned.1.call-start = ((), (), s32[]{:S(2)}) async-start(), calls=%async_computation.4 | async-start | bytes 4259840 | tf_op jit(solution)/shard_map/reduce_scatter | solution.py:513
  21.7 103.6 %copy-start.7 = (s32[65]{0:T(128)}, s32[65]{0:T(128)S(1)}, u32[]{:S(2)}) copy-start(s32[65]{0:T(128)S(1)} %reshape.131.ids_ref.write_ref) | copy-start | bytes 784
  22.0 128.0 %copy-start.9 = (s32[65]{0:T(128)}, s32[65]{0:T(128)S(1)}, u32[]{:S(2)}) copy-start(s32[65]{0:T(128)S(1)} %reshape.136.write_ref) | copy-start | bytes 784
  150.8 7.4 %collective-permute-start = (bf16[1,64,512]{2,1,0:T(8,128)(2,1)S(1)}, bf16[1,64,512]{2,1,0:T(8,128)(2,1)S(1)}, u32[]{:S(2)}, u32[]{:S(2)}) collective-permute-start(bf16[1,64,512]{2,1,0:T(8,128)(2,1)S(1)} %get-tuple-element.25), channel_id=1, source_target_pairs={{0,4},{4,8},{8,12},{1,5},{5,9},{9,13},{2,6},{6,10},{10,14},{3,7},{... | collective-permute-start | bytes 196616 | tf_op jit(solution)/shard_map/ppermute | solution.py:20
  155.5 7.1 %collective-permute-start.1 = (bf16[1,64,512]{2,1,0:T(8,128)(2,1)S(1)}, bf16[1,64,512]{2,1,0:T(8,128)(2,1)S(1)}, u32[]{:S(2)}, u32[]{:S(2)}) collective-permute-start(bf16[1,64,512]{2,1,0:T(8,128)(2,1)S(1)} %get-tuple-element.26), channel_id=1, source_target_pairs={{4,0},{8,4},{12,8},{5,1},{9,5},{13,9},{6,2},{10,6},{14,10},{7,3},{... | collective-permute-start | bytes 196616 | tf_op jit(solution)/shard_map/ppermute | solution.py:23
  194.6 13.5 %copy-start.3 = (bf16[832,256]{1,0:T(8,128)(2,1)S(1)}, bf16[832,256]{1,0:T(8,128)(2,1)}, u32[]{:S(2)}) copy-start(bf16[832,256]{1,0:T(8,128)(2,1)} %get-tuple-element.12) | copy-start | bytes 1277956
  194.6 13.5 %copy-start.4 = (bf16[832,256]{1,0:T(8,128)(2,1)S(1)}, bf16[832,256]{1,0:T(8,128)(2,1)}, u32[]{:S(2)}) copy-start(bf16[832,256]{1,0:T(8,128)(2,1)} %get-tuple-element.14) | copy-start | bytes 1277956
  194.6 71.5 %all-to-all-start.1 = ((bf16[36,64,512]{2,1,0:T(8,128)(2,1)}), bf16[36,64,512]{2,1,0:T(8,128)(2,1)S(1)}, u32[]{:S(2)}, u32[]{:S(2)}) async-start(bf16[36,64,512]{2,1,0:T(8,128)(2,1)} %slice.52), calls=%async_computation.1 | async-start | bytes 4718592 | tf_op jit(solution)/shard_map/all_to_all | solution.py:526
  202.3 63.5 %collective-permute-start.3 = (bf16[64,512]{1,0:T(8,128)(2,1)S(1)}, bf16[64,512]{1,0:T(8,128)(2,1)S(1)}, u32[]{:S(2)}, u32[]{:S(2)}) collective-permute-start(bf16[64,512]{1,0:T(8,128)(2,1)S(1)} %get-tuple-element.23), channel_id=1, source_target_pairs={{4,0},{8,4},{12,8},{5,1},{9,5},{13,9},{6,2},{10,6},{14,10},{7,3},{... | collective-permute-start | bytes 196616 | tf_op jit(solution)/shard_map/ppermute | solution.py:533
  205.1 61.0 %collective-permute-start.2 = (bf16[64,512]{1,0:T(8,128)(2,1)S(1)}, bf16[64,512]{1,0:T(8,128)(2,1)S(1)}, u32[]{:S(2)}, u32[]{:S(2)}) collective-permute-start(bf16[64,512]{1,0:T(8,128)(2,1)S(1)} %get-tuple-element.24), channel_id=1, source_target_pairs={{0,4},{4,8},{8,12},{1,5},{5,9},{9,13},{2,6},{6,10},{10,14},{3,7},{... | collective-permute-start | bytes 196616 | tf_op jit(solution)/shard_map/ppermute | solution.py:534
  265.8 0.6 copy-start.5
  266.1 0.6 copy-start.6
  266.1 1.5 copy-start
Sparse Core Ops, SparseCore 0:
  10.2 115.0 all-gather.1
  150.1 84.9 reduce-scatter.1

commit v16 on v13

--- a/solution.py
+++ b/solution.py
@@ -354,7 +354,7 @@
         first = first_ref[0]
         spread_ref[...] = acc_ref[...].astype(jnp.bfloat16)
         for block in range(blocks_dev):
-            own_ref[block] = acc_ref[first + block]
+            own_ref[block] = acc_ref[first + block].astype(jnp.bfloat16)
             spread_ref[first + block] = jnp.zeros(spread_ref.shape[1:], jnp.bfloat16)
 
 
@@ -386,7 +386,7 @@
         block_kernel,
         grid_spec=grid_spec,
         out_shape=[
-            jax.ShapeDtypeStruct((blocks_dev, BLOCK, 2 * width), jnp.float32),
+            jax.ShapeDtypeStruct((blocks_dev, BLOCK, 2 * width), jnp.bfloat16),
             jax.ShapeDtypeStruct((total, BLOCK, 2 * width), jnp.bfloat16),
             jax.ShapeDtypeStruct((tokens, width), jnp.bfloat16),
         ],
@@ -398,7 +398,7 @@
                   rs_a_ref, key_ref, value_ref, sum_ref):
     blocks_dev = own_b_ref.shape[0]
     half = own_b_ref.shape[2] // 2
-    sum_ref[...] = own_b_ref[...]
+    sum_ref[...] = own_b_ref[...].astype(jnp.float32)
     sum_ref[0] = sum_ref[0] + left_ref[...].astype(jnp.float32)
     sum_ref[blocks_dev - 1] = sum_ref[blocks_dev - 1] + right_ref[...].astype(jnp.float32)
     for slot in range(returned_ref.shape[0]):
@@ -410,7 +410,7 @@
 
     for block in range(blocks_dev):
         rows = pl.ds(block * BLOCK, BLOCK)
-        first = own_a_ref[block] + rs_a_ref[rows, :].astype(jnp.float32)
+        first = own_a_ref[block].astype(jnp.float32) + rs_a_ref[rows, :].astype(jnp.float32)
         second = sum_ref[block]
         key_ref[rows, pl.ds(0, half)] = first[:, :half].astype(jnp.bfloat16)
         key_ref[rows, pl.ds(half, half)] = second[:, :half].astype(jnp.bfloat16)

time: 283 us -> 282 us (level)
  no operation moved by 1% of the time
where the time goes in v16:
time: 282 us; the launch traced here: 278 us
  waiting for transfers between devices  163 us (58%)
  Pallas kernels  52.6 us (19%)
  starting transfers between devices  23.1 us (8%)
  local copies, waits for them, and re-layouts  16.5 us (6%)
  between operations  15.5 us (5%)
  other arithmetic  6.9 us (2%)
    all_to_all x1, waiting for transfers between devices, gathered_shards(): lax.all_to_all(outgoing, 'seq', split_axis=0, concat_axis=0, tiled=True)  100 us
    ppermute x1, waiting for transfers between devices, gathered_shards(): lax.ppermute(left_edge, 'seq', [(i, i - 1) for i in range(1, seq_size)])  57.3 us
    pallas_call x2, Pallas kernels, block_attention(): pl.pallas_call(block_kernel, grid_spec=grid_spec, out_shape=[jax.ShapeDty...  48.1 us
  transfers between devices with their start and end apart: 8, of which 5 were waited for; matrix products, arithmetic and copies ran while one was open for 7% of the time, Pallas kernels for 9%

profile of v16, /device:TPU:22, one launch (start us, length us, event | category | flops | bytes accessed | tf_op | source)
XLA Modules:
  0.0 278.3 jit_solution(173290616031006389)
XLA Ops:
  7.2 1.5 fusion.15
  8.8 1.1 pad_maximum_fusion.2
  12.2 1.0 copy.47
  13.2 1.6 slice.60
  14.7 5.2 %all-to-all-start = ((bf16[36,64,512]{2,1,0:T(8,128)(2,1)}), bf16[36,64,512]{2,1,0:T(8,128)(2,1)S(1)}, u32[]{:S(2)}, u32[]{:S(2)}) async-start(bf16[36,64,512]{2,1,0:T(8,128)(2,1)} %slice.60), calls=%async_computation | async-start | bytes 4718592 | tf_op jit(solution)/shard_map/all_to_all | solution.py:489
  22.7 100.5 %all-to-all-done = bf16[36,64,512]{2,1,0:T(8,128)(2,1)S(1)} async-done(((bf16[36,64,512]{2,1,0:T(8,128)(2,1)}), bf16[36,64,512]{2,1,0:T(8,128)(2,1)S(1)}, u32[]{:S(2)}, u32[]{:S(2)}) %all-to-all-start) | async-done | bytes 2359328 | tf_op jit(solution)/shard_map/all_to_all | solution.py:489
  124.2 1.0 all-gather.2.cloned.1.call-done
  125.3 24.1 %shard_map.85 = (bf16[13,64,512]{2,1,0:T(8,128)(2,1)}, bf16[52,64,512]{2,1,0:T(8,128)(2,1)}, bf16[832,256]{1,0:T(8,128)(2,1)}) custom-call(s32[65]{0:T(128)} %reshape.127.ids_ref.write_ref, s32[65]{0:T(128)} %reshape.127.ids_ref.write_ref, s32[65]{0:T(128)} %reshape.135.valid_ref, s32[1]{0:T(128)S(6)} %add.118.first_ref, bf16[832,512]{1,0:T(8,128)(2,1)} %q_ref.3, ...), custom_call_target="tpu_custom_call" | custom-call | tf_op jit(solution)/shard_map/pallas_call | solution.py:385
  149.4 0.8 fusion.3
  150.2 4.6 %collective-permute-start = (bf16[1,64,512]{2,1,0:T(8,128)(2,1)S(1)}, bf16[1,64,512]{2,1,0:T(8,128)(2,1)S(1)}, u32[]{:S(2)}, u32[]{:S(2)}) collective-permute-start(bf16[1,64,512]{2,1,0:T(8,128)(2,1)S(1)} %get-tuple-element.25), channel_id=1, source_target_pairs={{0,4},{4,8},{8,12},{1,5},{5,9},{9,13},{2,6},{6,10},{10,14},{3,7},{... | collective-permute-start | bytes 196616 | tf_op jit(solution)/shard_map/ppermute | solution.py:20
  154.8 1.9 collective-permute-start.1
  158.4 3.6 %collective-permute-done.1 = bf16[1,64,512]{2,1,0:T(8,128)(2,1)S(1)} collective-permute-done((bf16[1,64,512]{2,1,0:T(8,128)(2,1)S(1)}, bf16[1,64,512]{2,1,0:T(8,128)(2,1)S(1)}, u32[]{:S(2)}, u32[]{:S(2)}) %collective-permute-start.1) | collective-permute-done | bytes 65568 | tf_op jit(solution)/shard_map/ppermute | solution.py:23
  162.0 1.9 pad_maximum_fusion.rest_0_.rest_1_.rest_2_.rest_3_.rest_4_
  163.9 1.2 slice.47
  165.8 24.1 %shard_map.86 = (bf16[13,64,512]{2,1,0:T(8,128)(2,1)}, bf16[51,64,512]{2,1,0:T(8,128)(2,1)}, bf16[832,256]{1,0:T(8,128)(2,1)}) custom-call(s32[65]{0:T(128)} %reshape.131.ids_ref, s32[65]{0:T(128)} %reshape.132.write_ref, s32[65]{0:T(128)} %reshape.135.valid_ref, s32[1]{0:T(128)} %bitcast.3.first_ref, bf16[832,512]{1,0:T(8,128)(2,1)} %q_ref.3, ...), custom_call_target="tpu_custom_call" | custom-call | tf_op jit(solution)/shard_map/pallas_call | solution.py:385
  189.8 3.4 %slice.52 = bf16[36,64,512]{2,1,0:T(8,128)(2,1)} slice(bf16[51,64,512]{2,1,0:T(8,128)(2,1)} %get-tuple-element.16), slice={[0:36], [0:64], [0:512]} | slice | bytes 4718592 | tf_op jit(solution)/shard_map/slice | solution.py:518
  193.2 5.4 %all-to-all-start.1 = ((bf16[36,64,512]{2,1,0:T(8,128)(2,1)}), bf16[36,64,512]{2,1,0:T(8,128)(2,1)S(1)}, u32[]{:S(2)}, u32[]{:S(2)}) async-start(bf16[36,64,512]{2,1,0:T(8,128)(2,1)} %slice.52), calls=%async_computation.1 | async-start | bytes 4718592 | tf_op jit(solution)/shard_map/all_to_all | solution.py:517
  200.1 0.9 slice_bitcast_fusion
  201.0 2.8 %collective-permute-start.3 = (bf16[64,512]{1,0:T(8,128)(2,1)S(1)}, bf16[64,512]{1,0:T(8,128)(2,1)S(1)}, u32[]{:S(2)}, u32[]{:S(2)}) collective-permute-start(bf16[64,512]{1,0:T(8,128)(2,1)S(1)} %get-tuple-element.23), channel_id=1, source_target_pairs={{4,0},{8,4},{12,8},{5,1},{9,5},{13,9},{6,2},{10,6},{14,10},{7,3},{... | collective-permute-start | bytes 196616 | tf_op jit(solution)/shard_map/ppermute | solution.py:524
  203.8 3.0 %collective-permute-start.2 = (bf16[64,512]{1,0:T(8,128)(2,1)S(1)}, bf16[64,512]{1,0:T(8,128)(2,1)S(1)}, u32[]{:S(2)}, u32[]{:S(2)}) collective-permute-start(bf16[64,512]{1,0:T(8,128)(2,1)S(1)} %get-tuple-element.24), channel_id=1, source_target_pairs={{0,4},{4,8},{8,12},{1,5},{5,9},{9,13},{2,6},{6,10},{10,14},{3,7},{... | collective-permute-start | bytes 196616 | tf_op jit(solution)/shard_map/ppermute | solution.py:525
  206.9 1.0 pad_maximum_fusion.3
  207.8 57.3 %collective-permute-done.3.right_ref = bf16[64,512]{1,0:T(8,128)(2,1)S(1)} collective-permute-done((bf16[64,512]{1,0:T(8,128)(2,1)S(1)}, bf16[64,512]{1,0:T(8,128)(2,1)S(1)}, u32[]{:S(2)}, u32[]{:S(2)}) %collective-permute-start.3) | collective-permute-done | bytes 65568 | tf_op jit(solution)/shard_map/ppermute | solution.py:524
  266.1 0.9 copy-done
  267.0 4.5 %shard_map.87 = (bf16[832,512]{1,0:T(8,128)(2,1)}, bf16[832,512]{1,0:T(8,128)(2,1)}) custom-call(s32[36]{0:T(128)} %broadcast_select_fusion.target_ref, bf16[36,64,512]{2,1,0:T(8,128)(2,1)} %copy-done, bf16[13,64,512]{2,1,0:T(8,128)(2,1)} %get-tuple-element.17.own_b_ref, bf16[64,512]{1,0:T(8,128)(2,1)} %copy-done.6, bf16[64,512]{1,0:T(8,128)(2,1)} %copy-done.5, ...), custom_call_target="tpu_custom_call" | custom-call | tf_op jit(solution)/shard_map/pallas_call | solution.py:427
  (79 shorter events, 9.6 us)
Async XLA Ops:
  7.2 2.7 copy-start.7
  7.2 3.1 %copy-start.8 = (s32[52,2]{0,1:T(2,128)S(1)}, s32[52,2]{0,1:T(2,128)}, u32[]{:S(2)}) copy-start(s32[52,2]{0,1:T(2,128)} %param.11) | copy-start | bytes 1252
  7.2 118.1 %all-gather.2.cloned.1.call-start = ((), (), s32[]{:S(2)}) async-start(), calls=%async_computation.3 | async-start | bytes 4259840 | tf_op jit(solution)/shard_map/all_gather | solution.py:476
  8.7 1.9 copy-start.1
  8.8 1.9 copy-start.2
  14.7 108.4 %all-to-all-start = ((bf16[36,64,512]{2,1,0:T(8,128)(2,1)}), bf16[36,64,512]{2,1,0:T(8,128)(2,1)S(1)}, u32[]{:S(2)}, u32[]{:S(2)}) async-start(bf16[36,64,512]{2,1,0:T(8,128)(2,1)} %slice.60), calls=%async_computation | async-start | bytes 4718592 | tf_op jit(solution)/shard_map/all_to_all | solution.py:489
  20.0 245.5 %reduce-scatter.2.cloned.1.call-start = ((), (), s32[]{:S(2)}) async-start(), calls=%async_computation.4 | async-start | bytes 4259840 | tf_op jit(solution)/shard_map/reduce_scatter | solution.py:504
  150.2 8.2 %collective-permute-start = (bf16[1,64,512]{2,1,0:T(8,128)(2,1)S(1)}, bf16[1,64,512]{2,1,0:T(8,128)(2,1)S(1)}, u32[]{:S(2)}, u32[]{:S(2)}) collective-permute-start(bf16[1,64,512]{2,1,0:T(8,128)(2,1)S(1)} %get-tuple-element.25), channel_id=1, source_target_pairs={{0,4},{4,8},{8,12},{1,5},{5,9},{9,13},{2,6},{6,10},{10,14},{3,7},{... | collective-permute-start | bytes 196616 | tf_op jit(solution)/shard_map/ppermute | solution.py:20
  154.8 7.1 %collective-permute-start.1 = (bf16[1,64,512]{2,1,0:T(8,128)(2,1)S(1)}, bf16[1,64,512]{2,1,0:T(8,128)(2,1)S(1)}, u32[]{:S(2)}, u32[]{:S(2)}) collective-permute-start(bf16[1,64,512]{2,1,0:T(8,128)(2,1)S(1)} %get-tuple-element.26), channel_id=1, source_target_pairs={{4,0},{8,4},{12,8},{5,1},{9,5},{13,9},{6,2},{10,6},{14,10},{7,3},{... | collective-permute-start | bytes 196616 | tf_op jit(solution)/shard_map/ppermute | solution.py:23
  193.2 13.6 %copy-start.3 = (bf16[832,256]{1,0:T(8,128)(2,1)S(1)}, bf16[832,256]{1,0:T(8,128)(2,1)}, u32[]{:S(2)}) copy-start(bf16[832,256]{1,0:T(8,128)(2,1)} %get-tuple-element.12) | copy-start | bytes 1277956
  193.2 13.6 %copy-start.4 = (bf16[832,256]{1,0:T(8,128)(2,1)S(1)}, bf16[832,256]{1,0:T(8,128)(2,1)}, u32[]{:S(2)}) copy-start(bf16[832,256]{1,0:T(8,128)(2,1)} %get-tuple-element.14) | copy-start | bytes 1277956
  193.2 72.3 %all-to-all-start.1 = ((bf16[36,64,512]{2,1,0:T(8,128)(2,1)}), bf16[36,64,512]{2,1,0:T(8,128)(2,1)S(1)}, u32[]{:S(2)}, u32[]{:S(2)}) async-start(bf16[36,64,512]{2,1,0:T(8,128)(2,1)} %slice.52), calls=%async_computation.1 | async-start | bytes 4718592 | tf_op jit(solution)/shard_map/all_to_all | solution.py:517
  201.0 64.2 %collective-permute-start.3 = (bf16[64,512]{1,0:T(8,128)(2,1)S(1)}, bf16[64,512]{1,0:T(8,128)(2,1)S(1)}, u32[]{:S(2)}, u32[]{:S(2)}) collective-permute-start(bf16[64,512]{1,0:T(8,128)(2,1)S(1)} %get-tuple-element.23), channel_id=1, source_target_pairs={{4,0},{8,4},{12,8},{5,1},{9,5},{13,9},{6,2},{10,6},{14,10},{7,3},{... | collective-permute-start | bytes 196616 | tf_op jit(solution)/shard_map/ppermute | solution.py:524
  203.8 61.7 %collective-permute-start.2 = (bf16[64,512]{1,0:T(8,128)(2,1)S(1)}, bf16[64,512]{1,0:T(8,128)(2,1)S(1)}, u32[]{:S(2)}, u32[]{:S(2)}) collective-permute-start(bf16[64,512]{1,0:T(8,128)(2,1)S(1)} %get-tuple-element.24), channel_id=1, source_target_pairs={{0,4},{4,8},{8,12},{1,5},{5,9},{9,13},{2,6},{6,10},{10,14},{3,7},{... | collective-permute-start | bytes 196616 | tf_op jit(solution)/shard_map/ppermute | solution.py:525
  265.2 0.6 copy-start.5
  265.5 0.6 copy-start.6
  265.5 1.5 copy-start
Sparse Core Ops, SparseCore 0:
  10.2 115.0 all-gather.1
  149.5 85.5 reduce-scatter.1

commit v17 on v16

--- a/solution.py
+++ b/solution.py
@@ -479,12 +479,8 @@
             link = source[0, 0, :1]
         else:
             packed = packed.reshape(blocks_dev, BLOCK, 2 * part)
-            route = selector
-            outgoing = jnp.dot(
-                route, packed.reshape(blocks_dev, BLOCK * 2 * part),
-                preferred_element_type=jnp.float32,
-            ).astype(jnp.bfloat16)
-            outgoing = outgoing.reshape(seq_size * capacity, BLOCK, 2 * part)
+            picked = jnp.argmax(selector > 0, axis=1).astype(jnp.int32)
+            outgoing = jnp.take(packed, picked, axis=0, mode="clip")
             haloed = extended(packed, (("seq", 0),), 1)
             arrived = lax.all_to_all(outgoing, "seq", split_axis=0, concat_axis=0, tiled=True)
             source = jnp.concatenate([haloed, arrived], axis=0)

time: 282 us -> 281 us (level)
  no operation moved by 1% of the time
where the time goes in v17:
time: 281 us; the launch traced here: 277 us
  waiting for transfers between devices  163 us (58%)
  Pallas kernels  52.5 us (19%)
  starting transfers between devices  23.1 us (8%)
  local copies, waits for them, and re-layouts  15.6 us (6%)
  between operations  15.6 us (6%)
  other arithmetic  6.88 us (2%)
    all_to_all x1, waiting for transfers between devices, gathered_shards(): lax.all_to_all(outgoing, 'seq', split_axis=0, concat_axis=0, tiled=True)  100 us
    ppermute x1, waiting for transfers between devices, gathered_shards(): lax.ppermute(left_edge, 'seq', [(i, i - 1) for i in range(1, seq_size)])  58 us
    pallas_call x2, Pallas kernels, block_attention(): pl.pallas_call(block_kernel, grid_spec=grid_spec, out_shape=[jax.ShapeDty...  48.1 us
  transfers between devices with their start and end apart: 8, of which 5 were waited for; matrix products, arithmetic and copies ran while one was open for 7% of the time, Pallas kernels for 9%

profile of v17, /device:TPU:22, one launch (start us, length us, event | category | flops | bytes accessed | tf_op | source)
XLA Modules:
  0.0 277.2 jit_solution(9927833013741782052)
XLA Ops:
  7.2 1.5 fusion.19
  8.8 1.1 pad_maximum_fusion.2
  11.4 2.3 gather_fusion
  13.7 5.2 %all-to-all-start = ((bf16[36,64,512]{2,1,0:T(8,128)(2,1)}), bf16[36,64,512]{2,1,0:T(8,128)(2,1)S(1)}, u32[]{:S(2)}, u32[]{:S(2)}) async-start(bf16[36,64,512]{2,1,0:T(8,128)(2,1)} %gather_fusion), calls=%async_computation | async-start | bytes 4718592 | tf_op jit(solution)/shard_map/all_to_all | solution.py:485
  19.4 0.6 reshape.130.valid_ref
  21.7 100.4 %all-to-all-done = bf16[36,64,512]{2,1,0:T(8,128)(2,1)S(1)} async-done(((bf16[36,64,512]{2,1,0:T(8,128)(2,1)}), bf16[36,64,512]{2,1,0:T(8,128)(2,1)S(1)}, u32[]{:S(2)}, u32[]{:S(2)}) %all-to-all-start) | async-done | bytes 2359328 | tf_op jit(solution)/shard_map/all_to_all | solution.py:485
  123.3 0.9 all-gather.2.cloned.1.call-done
  124.3 24.1 %shard_map.85 = (bf16[13,64,512]{2,1,0:T(8,128)(2,1)}, bf16[52,64,512]{2,1,0:T(8,128)(2,1)}, bf16[832,256]{1,0:T(8,128)(2,1)}) custom-call(s32[65]{0:T(128)} %reshape.123.ids_ref.write_ref, s32[65]{0:T(128)} %reshape.123.ids_ref.write_ref, s32[65]{0:T(128)} %reshape.130.valid_ref, s32[1]{0:T(128)S(6)} %add.118.first_ref, bf16[832,512]{1,0:T(8,128)(2,1)} %q_ref.3, ...), custom_call_target="tpu_custom_call" | custom-call | tf_op jit(solution)/shard_map/pallas_call | solution.py:385
  148.3 0.8 fusion.8
  149.2 4.7 %collective-permute-start = (bf16[1,64,512]{2,1,0:T(8,128)(2,1)S(1)}, bf16[1,64,512]{2,1,0:T(8,128)(2,1)S(1)}, u32[]{:S(2)}, u32[]{:S(2)}) collective-permute-start(bf16[1,64,512]{2,1,0:T(8,128)(2,1)S(1)} %get-tuple-element.25), channel_id=1, source_target_pairs={{0,4},{4,8},{8,12},{1,5},{5,9},{9,13},{2,6},{6,10},{10,14},{3,7},{... | collective-permute-start | bytes 196616 | tf_op jit(solution)/shard_map/ppermute | solution.py:20
  153.8 1.9 collective-permute-start.1
  157.3 3.6 %collective-permute-done.1 = bf16[1,64,512]{2,1,0:T(8,128)(2,1)S(1)} collective-permute-done((bf16[1,64,512]{2,1,0:T(8,128)(2,1)S(1)}, bf16[1,64,512]{2,1,0:T(8,128)(2,1)S(1)}, u32[]{:S(2)}, u32[]{:S(2)}) %collective-permute-start.1) | collective-permute-done | bytes 65568 | tf_op jit(solution)/shard_map/ppermute | solution.py:23
  161.0 1.9 pad_maximum_fusion.rest_0_.rest_1_.rest_2_.rest_3_.rest_4_
  162.8 1.2 slice.47
  164.7 24.1 %shard_map.86 = (bf16[13,64,512]{2,1,0:T(8,128)(2,1)}, bf16[51,64,512]{2,1,0:T(8,128)(2,1)}, bf16[832,256]{1,0:T(8,128)(2,1)}) custom-call(s32[65]{0:T(128)} %reshape.127.ids_ref, s32[65]{0:T(128)} %reshape.128.write_ref, s32[65]{0:T(128)} %reshape.130.valid_ref, s32[1]{0:T(128)} %bitcast.4.first_ref, bf16[832,512]{1,0:T(8,128)(2,1)} %q_ref.3, ...), custom_call_target="tpu_custom_call" | custom-call | tf_op jit(solution)/shard_map/pallas_call | solution.py:385
  188.8 3.4 %slice.52 = bf16[36,64,512]{2,1,0:T(8,128)(2,1)} slice(bf16[51,64,512]{2,1,0:T(8,128)(2,1)} %get-tuple-element.16), slice={[0:36], [0:64], [0:512]} | slice | bytes 4718592 | tf_op jit(solution)/shard_map/slice | solution.py:514
  192.2 5.4 %all-to-all-start.1 = ((bf16[36,64,512]{2,1,0:T(8,128)(2,1)}), bf16[36,64,512]{2,1,0:T(8,128)(2,1)S(1)}, u32[]{:S(2)}, u32[]{:S(2)}) async-start(bf16[36,64,512]{2,1,0:T(8,128)(2,1)} %slice.52), calls=%async_computation.1 | async-start | bytes 4718592 | tf_op jit(solution)/shard_map/all_to_all | solution.py:513
  198.4 0.9 slice_bitcast_fusion
  199.2 2.8 %collective-permute-start.3 = (bf16[64,512]{1,0:T(8,128)(2,1)S(1)}, bf16[64,512]{1,0:T(8,128)(2,1)S(1)}, u32[]{:S(2)}, u32[]{:S(2)}) collective-permute-start(bf16[64,512]{1,0:T(8,128)(2,1)S(1)} %get-tuple-element.23), channel_id=1, source_target_pairs={{4,0},{8,4},{12,8},{5,1},{9,5},{13,9},{6,2},{10,6},{14,10},{7,3},{... | collective-permute-start | bytes 196616 | tf_op jit(solution)/shard_map/ppermute | solution.py:520
  202.1 3.0 %collective-permute-start.2 = (bf16[64,512]{1,0:T(8,128)(2,1)S(1)}, bf16[64,512]{1,0:T(8,128)(2,1)S(1)}, u32[]{:S(2)}, u32[]{:S(2)}) collective-permute-start(bf16[64,512]{1,0:T(8,128)(2,1)S(1)} %get-tuple-element.24), channel_id=1, source_target_pairs={{0,4},{4,8},{8,12},{1,5},{5,9},{9,13},{2,6},{6,10},{10,14},{3,7},{... | collective-permute-start | bytes 196616 | tf_op jit(solution)/shard_map/ppermute | solution.py:521
  205.1 1.0 pad_maximum_fusion.3
  206.1 58.0 %collective-permute-done.3.right_ref = bf16[64,512]{1,0:T(8,128)(2,1)S(1)} collective-permute-done((bf16[64,512]{1,0:T(8,128)(2,1)S(1)}, bf16[64,512]{1,0:T(8,128)(2,1)S(1)}, u32[]{:S(2)}, u32[]{:S(2)}) %collective-permute-start.3) | collective-permute-done | bytes 65568 | tf_op jit(solution)/shard_map/ppermute | solution.py:520
  265.1 0.9 copy-done
  265.9 4.4 %shard_map.87 = (bf16[832,512]{1,0:T(8,128)(2,1)}, bf16[832,512]{1,0:T(8,128)(2,1)}) custom-call(s32[36]{0:T(128)} %broadcast_select_fusion.target_ref, bf16[36,64,512]{2,1,0:T(8,128)(2,1)} %copy-done, bf16[13,64,512]{2,1,0:T(8,128)(2,1)} %get-tuple-element.17.own_b_ref, bf16[64,512]{1,0:T(8,128)(2,1)} %copy-done.6, bf16[64,512]{1,0:T(8,128)(2,1)} %copy-done.5, ...), custom_call_target="tpu_custom_call" | custom-call | tf_op jit(solution)/shard_map/pallas_call | solution.py:427
  (76 shorter events, 7.5 us)
Async XLA Ops:
  7.2 2.7 copy-start.7
  7.2 3.1 %copy-start.8 = (s32[52,2]{0,1:T(2,128)S(1)}, s32[52,2]{0,1:T(2,128)}, u32[]{:S(2)}) copy-start(s32[52,2]{0,1:T(2,128)} %param.11) | copy-start | bytes 1252
  7.2 117.1 %all-gather.2.cloned.1.call-start = ((), (), s32[]{:S(2)}) async-start(), calls=%async_computation.3 | async-start | bytes 4259840 | tf_op jit(solution)/shard_map/all_gather | solution.py:476
  8.7 5.0 %copy-start.1 = (bf16[832,256]{1,0:T(8,128)(2,1)}, bf16[832,256]{1,0:T(8,128)(2,1)S(1)}, u32[]{:S(2)}) copy-start(bf16[832,256]{1,0:T(8,128)(2,1)S(1)} %get-tuple-element.28) | copy-start | bytes 1277956
  8.8 5.0 %copy-start.2 = (bf16[832,256]{1,0:T(8,128)(2,1)}, bf16[832,256]{1,0:T(8,128)(2,1)S(1)}, u32[]{:S(2)}) copy-start(bf16[832,256]{1,0:T(8,128)(2,1)S(1)} %get-tuple-element.36) | copy-start | bytes 1277956
  13.7 108.4 %all-to-all-start = ((bf16[36,64,512]{2,1,0:T(8,128)(2,1)}), bf16[36,64,512]{2,1,0:T(8,128)(2,1)S(1)}, u32[]{:S(2)}, u32[]{:S(2)}) async-start(bf16[36,64,512]{2,1,0:T(8,128)(2,1)} %gather_fusion), calls=%async_computation | async-start | bytes 4718592 | tf_op jit(solution)/shard_map/all_to_all | solution.py:485
  18.9 245.6 %reduce-scatter.2.cloned.1.call-start = ((), (), s32[]{:S(2)}) async-start(), calls=%async_computation.4 | async-start | bytes 4259840 | tf_op jit(solution)/shard_map/reduce_scatter | solution.py:500
  149.2 8.2 %collective-permute-start = (bf16[1,64,512]{2,1,0:T(8,128)(2,1)S(1)}, bf16[1,64,512]{2,1,0:T(8,128)(2,1)S(1)}, u32[]{:S(2)}, u32[]{:S(2)}) collective-permute-start(bf16[1,64,512]{2,1,0:T(8,128)(2,1)S(1)} %get-tuple-element.25), channel_id=1, source_target_pairs={{0,4},{4,8},{8,12},{1,5},{5,9},{9,13},{2,6},{6,10},{10,14},{3,7},{... | collective-permute-start | bytes 196616 | tf_op jit(solution)/shard_map/ppermute | solution.py:20
  153.8 7.1 %collective-permute-start.1 = (bf16[1,64,512]{2,1,0:T(8,128)(2,1)S(1)}, bf16[1,64,512]{2,1,0:T(8,128)(2,1)S(1)}, u32[]{:S(2)}, u32[]{:S(2)}) collective-permute-start(bf16[1,64,512]{2,1,0:T(8,128)(2,1)S(1)} %get-tuple-element.26), channel_id=1, source_target_pairs={{4,0},{8,4},{12,8},{5,1},{9,5},{13,9},{6,2},{10,6},{14,10},{7,3},{... | collective-permute-start | bytes 196616 | tf_op jit(solution)/shard_map/ppermute | solution.py:23
  192.2 12.9 %copy-start.3 = (bf16[832,256]{1,0:T(8,128)(2,1)S(1)}, bf16[832,256]{1,0:T(8,128)(2,1)}, u32[]{:S(2)}) copy-start(bf16[832,256]{1,0:T(8,128)(2,1)} %get-tuple-element.13) | copy-start | bytes 1277956
  192.2 12.9 %copy-start.4 = (bf16[832,256]{1,0:T(8,128)(2,1)S(1)}, bf16[832,256]{1,0:T(8,128)(2,1)}, u32[]{:S(2)}) copy-start(bf16[832,256]{1,0:T(8,128)(2,1)} %get-tuple-element.15) | copy-start | bytes 1277956
  192.2 72.3 %all-to-all-start.1 = ((bf16[36,64,512]{2,1,0:T(8,128)(2,1)}), bf16[36,64,512]{2,1,0:T(8,128)(2,1)S(1)}, u32[]{:S(2)}, u32[]{:S(2)}) async-start(bf16[36,64,512]{2,1,0:T(8,128)(2,1)} %slice.52), calls=%async_computation.1 | async-start | bytes 4718592 | tf_op jit(solution)/shard_map/all_to_all | solution.py:513
  199.2 64.9 %collective-permute-start.3 = (bf16[64,512]{1,0:T(8,128)(2,1)S(1)}, bf16[64,512]{1,0:T(8,128)(2,1)S(1)}, u32[]{:S(2)}, u32[]{:S(2)}) collective-permute-start(bf16[64,512]{1,0:T(8,128)(2,1)S(1)} %get-tuple-element.23), channel_id=1, source_target_pairs={{4,0},{8,4},{12,8},{5,1},{9,5},{13,9},{6,2},{10,6},{14,10},{7,3},{... | collective-permute-start | bytes 196616 | tf_op jit(solution)/shard_map/ppermute | solution.py:520
  202.1 62.4 %collective-permute-start.2 = (bf16[64,512]{1,0:T(8,128)(2,1)S(1)}, bf16[64,512]{1,0:T(8,128)(2,1)S(1)}, u32[]{:S(2)}, u32[]{:S(2)}) collective-permute-start(bf16[64,512]{1,0:T(8,128)(2,1)S(1)} %get-tuple-element.24), channel_id=1, source_target_pairs={{0,4},{4,8},{8,12},{1,5},{5,9},{9,13},{2,6},{6,10},{10,14},{3,7},{... | collective-permute-start | bytes 196616 | tf_op jit(solution)/shard_map/ppermute | solution.py:521
  264.1 0.6 copy-start.5
  264.5 0.6 copy-start.6
  264.5 1.5 copy-start
Sparse Core Ops, SparseCore 0:
  10.2 114.0 all-gather.1
  148.5 85.5 reduce-scatter.1

commit v18 on v17

--- a/solution.py
+++ b/solution.py
@@ -479,7 +479,15 @@
             link = source[0, 0, :1]
         else:
             packed = packed.reshape(blocks_dev, BLOCK, 2 * part)
-            picked = jnp.argmax(selector > 0, axis=1).astype(jnp.int32)
+            wanted_from = random_device.reshape(seq_size, blocks_dev * RAND)
+            wanted_block = random_block.reshape(seq_size, blocks_dev * RAND)
+            from_me = (wanted_from == own_index).astype(jnp.int32)
+            rank = jnp.cumsum(from_me, axis=1) - from_me
+            hit = (from_me[:, None, :] > 0) & (
+                rank[:, None, :] == jnp.arange(capacity, dtype=jnp.int32)[None, :, None]
+            )
+            picked = jnp.sum(jnp.where(hit, wanted_block[:, None, :], 0), axis=2)
+            picked = picked.reshape(-1).astype(jnp.int32)
             outgoing = jnp.take(packed, picked, axis=0, mode="clip")
             haloed = extended(packed, (("seq", 0),), 1)
             arrived = lax.all_to_all(outgoing, "seq", split_axis=0, concat_axis=0, tiled=True)

time: 281 us -> 280 us (level)
  no operation moved by 1% of the time
where the time goes in v18:
time: 280 us; the launch traced here: 277 us
  waiting for transfers between devices  163 us (58%)
  Pallas kernels  52.6 us (19%)
  starting transfers between devices  23.1 us (8%)
  local copies, waits for them, and re-layouts  15.7 us (6%)
  between operations  15.5 us (6%)
  other arithmetic  7.08 us (3%)
    all_to_all x1, waiting for transfers between devices, gathered_shards(): lax.all_to_all(outgoing, 'seq', split_axis=0, concat_axis=0, tiled=True)  100 us
    ppermute x1, waiting for transfers between devices, gathered_shards(): lax.ppermute(left_edge, 'seq', [(i, i - 1) for i in range(1, seq_size)])  57.2 us
    pallas_call x2, Pallas kernels, block_attention(): pl.pallas_call(block_kernel, grid_spec=grid_spec, out_shape=[jax.ShapeDty...  48.1 us
  transfers between devices with their start and end apart: 8, of which 5 were waited for; matrix products, arithmetic and copies ran while one was open for 7% of the time, Pallas kernels for 9%

profile of v18, /device:TPU:22, one launch (start us, length us, event | category | flops | bytes accessed | tf_op | source)
XLA Modules:
  0.0 276.7 jit_solution(2129072312197665033)
XLA Ops:
  7.2 1.5 fusion.20
  8.8 1.1 pad_maximum_fusion.2
  10.8 2.3 gather_fusion
  13.1 5.2 %all-to-all-start = ((bf16[36,64,512]{2,1,0:T(8,128)(2,1)}), bf16[36,64,512]{2,1,0:T(8,128)(2,1)S(1)}, u32[]{:S(2)}, u32[]{:S(2)}) async-start(bf16[36,64,512]{2,1,0:T(8,128)(2,1)} %gather_fusion), calls=%async_computation | async-start | bytes 4718592 | tf_op jit(solution)/shard_map/all_to_all | solution.py:493
  20.5 0.6 reshape.132.ids_ref.write_ref
  21.1 100.4 %all-to-all-done = bf16[36,64,512]{2,1,0:T(8,128)(2,1)S(1)} async-done(((bf16[36,64,512]{2,1,0:T(8,128)(2,1)}), bf16[36,64,512]{2,1,0:T(8,128)(2,1)S(1)}, u32[]{:S(2)}, u32[]{:S(2)}) %all-to-all-start) | async-done | bytes 2359328 | tf_op jit(solution)/shard_map/all_to_all | solution.py:493
  122.6 1.0 all-gather.2.cloned.1.call-done
  123.6 24.1 %shard_map.85 = (bf16[13,64,512]{2,1,0:T(8,128)(2,1)}, bf16[52,64,512]{2,1,0:T(8,128)(2,1)}, bf16[832,256]{1,0:T(8,128)(2,1)}) custom-call(s32[65]{0:T(128)} %reshape.132.ids_ref.write_ref, s32[65]{0:T(128)} %reshape.132.ids_ref.write_ref, s32[65]{0:T(128)} %reshape.139.valid_ref, s32[1]{0:T(128)S(6)} %add.118.first_ref, bf16[832,512]{1,0:T(8,128)(2,1)} %q_ref.3, ...), custom_call_target="tpu_custom_call" | custom-call | tf_op jit(solution)/shard_map/pallas_call | solution.py:385
  147.7 0.8 fusion.8
  148.5 4.7 %collective-permute-start = (bf16[1,64,512]{2,1,0:T(8,128)(2,1)S(1)}, bf16[1,64,512]{2,1,0:T(8,128)(2,1)S(1)}, u32[]{:S(2)}, u32[]{:S(2)}) collective-permute-start(bf16[1,64,512]{2,1,0:T(8,128)(2,1)S(1)} %get-tuple-element.25), channel_id=1, source_target_pairs={{0,4},{4,8},{8,12},{1,5},{5,9},{9,13},{2,6},{6,10},{10,14},{3,7},{... | collective-permute-start | bytes 196616 | tf_op jit(solution)/shard_map/ppermute | solution.py:20
  153.2 1.9 collective-permute-start.1
  156.7 3.6 %collective-permute-done.1 = bf16[1,64,512]{2,1,0:T(8,128)(2,1)S(1)} collective-permute-done((bf16[1,64,512]{2,1,0:T(8,128)(2,1)S(1)}, bf16[1,64,512]{2,1,0:T(8,128)(2,1)S(1)}, u32[]{:S(2)}, u32[]{:S(2)}) %collective-permute-start.1) | collective-permute-done | bytes 65568 | tf_op jit(solution)/shard_map/ppermute | solution.py:23
  160.3 1.9 pad_maximum_fusion.rest_0_.rest_1_.rest_2_.rest_3_.rest_4_
  162.3 1.2 slice.47
  164.1 24.1 %shard_map.86 = (bf16[13,64,512]{2,1,0:T(8,128)(2,1)}, bf16[51,64,512]{2,1,0:T(8,128)(2,1)}, bf16[832,256]{1,0:T(8,128)(2,1)}) custom-call(s32[65]{0:T(128)} %reshape.136.ids_ref, s32[65]{0:T(128)} %reshape.137.write_ref, s32[65]{0:T(128)} %reshape.139.valid_ref, s32[1]{0:T(128)} %bitcast.4.first_ref, bf16[832,512]{1,0:T(8,128)(2,1)} %q_ref.3, ...), custom_call_target="tpu_custom_call" | custom-call | tf_op jit(solution)/shard_map/pallas_call | solution.py:385
  188.2 3.4 %slice.52 = bf16[36,64,512]{2,1,0:T(8,128)(2,1)} slice(bf16[51,64,512]{2,1,0:T(8,128)(2,1)} %get-tuple-element.16), slice={[0:36], [0:64], [0:512]} | slice | bytes 4718592 | tf_op jit(solution)/shard_map/slice | solution.py:522
  191.6 5.4 %all-to-all-start.1 = ((bf16[36,64,512]{2,1,0:T(8,128)(2,1)}), bf16[36,64,512]{2,1,0:T(8,128)(2,1)S(1)}, u32[]{:S(2)}, u32[]{:S(2)}) async-start(bf16[36,64,512]{2,1,0:T(8,128)(2,1)} %slice.52), calls=%async_computation.1 | async-start | bytes 4718592 | tf_op jit(solution)/shard_map/all_to_all | solution.py:521
  198.6 0.9 slice_bitcast_fusion
  199.5 2.8 %collective-permute-start.3 = (bf16[64,512]{1,0:T(8,128)(2,1)S(1)}, bf16[64,512]{1,0:T(8,128)(2,1)S(1)}, u32[]{:S(2)}, u32[]{:S(2)}) collective-permute-start(bf16[64,512]{1,0:T(8,128)(2,1)S(1)} %get-tuple-element.23), channel_id=1, source_target_pairs={{4,0},{8,4},{12,8},{5,1},{9,5},{13,9},{6,2},{10,6},{14,10},{7,3},{... | collective-permute-start | bytes 196616 | tf_op jit(solution)/shard_map/ppermute | solution.py:528
  202.3 3.0 %collective-permute-start.2 = (bf16[64,512]{1,0:T(8,128)(2,1)S(1)}, bf16[64,512]{1,0:T(8,128)(2,1)S(1)}, u32[]{:S(2)}, u32[]{:S(2)}) collective-permute-start(bf16[64,512]{1,0:T(8,128)(2,1)S(1)} %get-tuple-element.24), channel_id=1, source_target_pairs={{0,4},{4,8},{8,12},{1,5},{5,9},{9,13},{2,6},{6,10},{10,14},{3,7},{... | collective-permute-start | bytes 196616 | tf_op jit(solution)/shard_map/ppermute | solution.py:529
  205.4 1.0 pad_maximum_fusion.3
  206.3 57.2 %collective-permute-done.3.right_ref = bf16[64,512]{1,0:T(8,128)(2,1)S(1)} collective-permute-done((bf16[64,512]{1,0:T(8,128)(2,1)S(1)}, bf16[64,512]{1,0:T(8,128)(2,1)S(1)}, u32[]{:S(2)}, u32[]{:S(2)}) %collective-permute-start.3) | collective-permute-done | bytes 65568 | tf_op jit(solution)/shard_map/ppermute | solution.py:528
  264.5 0.9 copy-done
  265.3 4.5 %shard_map.87 = (bf16[832,512]{1,0:T(8,128)(2,1)}, bf16[832,512]{1,0:T(8,128)(2,1)}) custom-call(s32[36]{0:T(128)} %broadcast_select_fusion.target_ref, bf16[36,64,512]{2,1,0:T(8,128)(2,1)} %copy-done, bf16[13,64,512]{2,1,0:T(8,128)(2,1)} %get-tuple-element.17.own_b_ref, bf16[64,512]{1,0:T(8,128)(2,1)} %copy-done.6, bf16[64,512]{1,0:T(8,128)(2,1)} %copy-done.5, ...), custom_call_target="tpu_custom_call" | custom-call | tf_op jit(solution)/shard_map/pallas_call | solution.py:427
  (79 shorter events, 7.7 us)
Async XLA Ops:
  7.2 2.7 copy-start.7
  7.2 3.1 %copy-start.8 = (s32[52,2]{0,1:T(2,128)S(1)}, s32[52,2]{0,1:T(2,128)}, u32[]{:S(2)}) copy-start(s32[52,2]{0,1:T(2,128)} %param.11) | copy-start | bytes 1252
  7.2 116.5 %all-gather.2.cloned.1.call-start = ((), (), s32[]{:S(2)}) async-start(), calls=%async_computation.3 | async-start | bytes 4259840 | tf_op jit(solution)/shard_map/all_gather | solution.py:476
  8.7 4.4 %copy-start.1 = (bf16[832,256]{1,0:T(8,128)(2,1)}, bf16[832,256]{1,0:T(8,128)(2,1)S(1)}, u32[]{:S(2)}) copy-start(bf16[832,256]{1,0:T(8,128)(2,1)S(1)} %get-tuple-element.28) | copy-start | bytes 1277956
  8.8 4.4 %copy-start.2 = (bf16[832,256]{1,0:T(8,128)(2,1)}, bf16[832,256]{1,0:T(8,128)(2,1)S(1)}, u32[]{:S(2)}) copy-start(bf16[832,256]{1,0:T(8,128)(2,1)S(1)} %get-tuple-element.36) | copy-start | bytes 1277956
  13.1 108.4 %all-to-all-start = ((bf16[36,64,512]{2,1,0:T(8,128)(2,1)}), bf16[36,64,512]{2,1,0:T(8,128)(2,1)S(1)}, u32[]{:S(2)}, u32[]{:S(2)}) async-start(bf16[36,64,512]{2,1,0:T(8,128)(2,1)} %gather_fusion), calls=%async_computation | async-start | bytes 4718592 | tf_op jit(solution)/shard_map/all_to_all | solution.py:493
  18.3 245.6 %reduce-scatter.2.cloned.1.call-start = ((), (), s32[]{:S(2)}) async-start(), calls=%async_computation.4 | async-start | bytes 4259840 | tf_op jit(solution)/shard_map/reduce_scatter | solution.py:508
  148.5 8.2 %collective-permute-start = (bf16[1,64,512]{2,1,0:T(8,128)(2,1)S(1)}, bf16[1,64,512]{2,1,0:T(8,128)(2,1)S(1)}, u32[]{:S(2)}, u32[]{:S(2)}) collective-permute-start(bf16[1,64,512]{2,1,0:T(8,128)(2,1)S(1)} %get-tuple-element.25), channel_id=1, source_target_pairs={{0,4},{4,8},{8,12},{1,5},{5,9},{9,13},{2,6},{6,10},{10,14},{3,7},{... | collective-permute-start | bytes 196616 | tf_op jit(solution)/shard_map/ppermute | solution.py:20
  153.2 7.1 %collective-permute-start.1 = (bf16[1,64,512]{2,1,0:T(8,128)(2,1)S(1)}, bf16[1,64,512]{2,1,0:T(8,128)(2,1)S(1)}, u32[]{:S(2)}, u32[]{:S(2)}) collective-permute-start(bf16[1,64,512]{2,1,0:T(8,128)(2,1)S(1)} %get-tuple-element.26), channel_id=1, source_target_pairs={{4,0},{8,4},{12,8},{5,1},{9,5},{13,9},{6,2},{10,6},{14,10},{7,3},{... | collective-permute-start | bytes 196616 | tf_op jit(solution)/shard_map/ppermute | solution.py:23
  191.6 13.8 %copy-start.3 = (bf16[832,256]{1,0:T(8,128)(2,1)S(1)}, bf16[832,256]{1,0:T(8,128)(2,1)}, u32[]{:S(2)}) copy-start(bf16[832,256]{1,0:T(8,128)(2,1)} %get-tuple-element.12) | copy-start | bytes 1277956
  191.6 13.8 %copy-start.4 = (bf16[832,256]{1,0:T(8,128)(2,1)S(1)}, bf16[832,256]{1,0:T(8,128)(2,1)}, u32[]{:S(2)}) copy-start(bf16[832,256]{1,0:T(8,128)(2,1)} %get-tuple-element.14) | copy-start | bytes 1277956
  191.6 72.3 %all-to-all-start.1 = ((bf16[36,64,512]{2,1,0:T(8,128)(2,1)}), bf16[36,64,512]{2,1,0:T(8,128)(2,1)S(1)}, u32[]{:S(2)}, u32[]{:S(2)}) async-start(bf16[36,64,512]{2,1,0:T(8,128)(2,1)} %slice.52), calls=%async_computation.1 | async-start | bytes 4718592 | tf_op jit(solution)/shard_map/all_to_all | solution.py:521
  199.5 64.0 %collective-permute-start.3 = (bf16[64,512]{1,0:T(8,128)(2,1)S(1)}, bf16[64,512]{1,0:T(8,128)(2,1)S(1)}, u32[]{:S(2)}, u32[]{:S(2)}) collective-permute-start(bf16[64,512]{1,0:T(8,128)(2,1)S(1)} %get-tuple-element.23), channel_id=1, source_target_pairs={{4,0},{8,4},{12,8},{5,1},{9,5},{13,9},{6,2},{10,6},{14,10},{7,3},{... | collective-permute-start | bytes 196616 | tf_op jit(solution)/shard_map/ppermute | solution.py:528
  202.3 61.5 %collective-permute-start.2 = (bf16[64,512]{1,0:T(8,128)(2,1)S(1)}, bf16[64,512]{1,0:T(8,128)(2,1)S(1)}, u32[]{:S(2)}, u32[]{:S(2)}) collective-permute-start(bf16[64,512]{1,0:T(8,128)(2,1)S(1)} %get-tuple-element.24), channel_id=1, source_target_pairs={{0,4},{4,8},{8,12},{1,5},{5,9},{9,13},{2,6},{6,10},{10,14},{3,7},{... | collective-permute-start | bytes 196616 | tf_op jit(solution)/shard_map/ppermute | solution.py:529
  263.5 0.6 copy-start.5
  263.8 0.6 copy-start.6
  263.8 1.5 copy-start
Sparse Core Ops, SparseCore 0:
  10.2 113.4 all-gather.1
  147.8 85.5 reduce-scatter.1
